TPU v7x, 256 devices: a whole 4x4x8 slice. The times are simulated.
256 devices in a mesh: seq: 8 (over z_lo, core), blk: 32 (over y, z_hi, x).
Axes of the slice: x: 4, y: 4, z: 8 (z_hi: 2, z_lo: 4; z = z_hi * 4 + z_lo), core: 2. Of those that a mesh axis runs over, the one named last changes fastest.
Arguments:
- stream: float32 [4096, 3072], P(('seq', 'blk')), may hold values from -39 to 39
- key_keep: int32 [4096], replicated, may hold values 0 or 1
- positions: int32 [4096, 3], replicated, may hold values from 0 to 63
- lengths: int32 [4], replicated, may hold values from 1 to 2048, 4096 in all
- step_index: int32 [4], replicated, may hold values from 0 to 27
- mod_table: bfloat16 [4, 28, 3, 3072], replicated, may hold values from -4 to 4
- w_qkv: bfloat16 [3072, 9216], P(None, 'blk'), may hold values from -0.109375 to 0.109375
- w_mlp_in: bfloat16 [3072, 12288], P(None, 'blk'), may hold values from -0.109375 to 0.109375
- q_gain: float32 [128], replicated, may hold values from 0.5 to 10
- k_gain: float32 [128], replicated, may hold values from 0.5 to 10
- w_attn_out: bfloat16 [3072, 3072], P('blk'), may hold values from -0.109375 to 0.109375
- w_mlp_out: bfloat16 [12288, 3072], P('blk'), may hold values from -0.0546875 to 0.0546875
Outputs:
- stream_next: float32 [4096, 3072], P(('seq', 'blk'))
Inputs may be any that keep to these rules, and one draw needn't show every extreme that they name: The lengths sum to 4096; the longest request has exactly 2048 tokens.
All inputs are finite; a program needn't handle non-finite values.
Results may differ from a plain program's by a relative error of at most 0.0082.
The roundings to bfloat16 on the way count: a program that leaves them out, or rounds other values in their place, can miss the bound.
Values may be sent and summed in bfloat16 or wider, within the bound.
No kernel may reach another device: no remote copies, remote signals or barrier semaphores. Data moves between devices by JAX's collectives and lax.ppermute only.
A program may use at most 64 MiB of HBM per device.

v0:
```python
import math

import jax
import jax.numpy as jnp
from jax import lax
from jax.sharding import PartitionSpec as P


def rope_table(head_size):
    first_count = head_size // 16
    second = 7 * head_size // 32
    pair_ids = jnp.arange(head_size // 2, dtype=jnp.int32)
    pair_axis = jnp.where(
        pair_ids < first_count, 0, jnp.where(pair_ids < first_count + second, 1, 2)
    )
    pair_local = jnp.where(
        pair_ids < first_count,
        pair_ids,
        jnp.where(
            pair_ids < first_count + second, pair_ids - first_count, pair_ids - first_count - second
        ),
    )
    axis_dims = jnp.where(pair_axis == 0, 2 * first_count, 2 * second)
    frequency = jnp.power(
        jnp.float32(10000.0), -(2 * pair_local).astype(jnp.float32) / axis_dims.astype(jnp.float32)
    )
    return jnp.where(
        jnp.arange(3)[:, None] == pair_axis[None, :], frequency[None, :], jnp.float32(0.0)
    )


def angles_of(places, freq_table):
    return jnp.sum(places.astype(jnp.float32)[:, :, None] * freq_table[None, :, :], axis=1)


def rotate(values, angles):
    paired = values.reshape(values.shape[:-1] + (values.shape[-1] // 2, 2))
    even_part = paired[..., 0]
    odd_part = paired[..., 1]
    cos_part = jnp.cos(angles)[:, None, :]
    sin_part = jnp.sin(angles)[:, None, :]
    turned = jnp.stack(
        [cos_part * even_part - sin_part * odd_part, sin_part * even_part + cos_part * odd_part],
        axis=-1,
    )
    return turned.reshape(values.shape)


def rms_scale(values, gain_vec):
    return values * lax.rsqrt(jnp.mean(values * values, axis=-1, keepdims=True) + 1e-06) * gain_vec


def segment_of(row_ids, request_ends):
    return jnp.sum((row_ids[:, None] >= request_ends[None, :]).astype(jnp.int32), axis=1)


def spread_rows(row_ids, query_rows, block_rows, tok_seq):
    owner = row_ids // query_rows
    within = row_ids % query_rows
    return within // block_rows * tok_seq + owner * block_rows + within % block_rows


def body(
    stream,
    key_keep,
    positions,
    lengths,
    step_index,
    mod_table,
    w_qkv,
    w_mlp_in,
    q_gain,
    k_gain,
    w_attn_out,
    w_mlp_out,
):
    blk_count = lax.axis_size("blk")
    seq_count = lax.axis_size("seq")
    seq_at = lax.axis_index("seq")
    blk_at = lax.axis_index("blk")
    block_rows = stream.shape[0]
    width = stream.shape[1]
    tok_seq = block_rows * blk_count
    head_size = q_gain.shape[0]
    local_heads = width // head_size // seq_count
    requests = mod_table.shape[0]
    step_total = mod_table.shape[1]
    inv_root = 1.0 / math.sqrt(head_size)
    request_ends = jnp.cumsum(lengths)
    own_rows = seq_at * tok_seq + blk_at * block_rows + jnp.arange(block_rows, dtype=jnp.int32)
    own_request = segment_of(own_rows, request_ends)
    step_pick = (jnp.arange(step_total, dtype=jnp.int32)[None, :] == step_index[:, None]).astype(
        jnp.bfloat16
    )
    modulation = jnp.einsum(
        "rs,rsk->rk",
        step_pick,
        mod_table.reshape(requests, step_total, 3 * width),
        preferred_element_type=jnp.float32,
    )
    member = (own_request[:, None] == jnp.arange(requests, dtype=jnp.int32)[None, :]).astype(
        jnp.float32
    )
    token_mod = jnp.dot(member, modulation, precision=lax.Precision.HIGHEST)
    mod_shift = token_mod[:, :width]
    mod_scale = token_mod[:, width : 2 * width]
    mod_gate = token_mod[:, 2 * width :]
    row_mean = jnp.mean(stream, axis=1, keepdims=True)
    centered = stream - row_mean
    row_var = jnp.mean(centered * centered, axis=1, keepdims=True)
    normed = centered * lax.rsqrt(row_var + 1e-06)
    modin = ((1.0 + mod_scale) * normed + mod_shift).astype(jnp.bfloat16)
    qkv_width = w_qkv.shape[1]
    shard_rows = lax.all_gather(modin, "blk", axis=0, tiled=True)
    qkv_part = jnp.dot(shard_rows, w_qkv, preferred_element_type=jnp.float32).astype(jnp.bfloat16)
    mlp_part = jax.nn.gelu(
        jnp.dot(shard_rows, w_mlp_in, preferred_element_type=jnp.float32), approximate=True
    ).astype(jnp.bfloat16)
    joined = jnp.concatenate([qkv_part, mlp_part], axis=1)
    qkv_cols = joined[:, :qkv_width]
    mlp_act = joined[:, qkv_width:]
    heads_in = lax.all_to_all(
        lax.all_to_all(qkv_cols, "blk", split_axis=0, concat_axis=1, tiled=True),
        "seq",
        split_axis=1,
        concat_axis=0,
        tiled=True,
    )
    query_rows = heads_in.shape[0]
    heads4 = heads_in.reshape(query_rows, local_heads, 3, head_size)
    query_ids = spread_rows(
        blk_at * query_rows + jnp.arange(query_rows, dtype=jnp.int32),
        query_rows,
        block_rows,
        tok_seq,
    )
    query_request = segment_of(query_ids, request_ends)
    angles = angles_of(jnp.take(positions, query_ids, axis=0), rope_table(head_size))
    query_rot = rotate(rms_scale(heads4[:, :, 0].astype(jnp.float32), q_gain), angles).astype(
        jnp.bfloat16
    )
    key_rot = rotate(rms_scale(heads4[:, :, 1].astype(jnp.float32), k_gain), angles).astype(
        jnp.bfloat16
    )
    value_rows = heads4[:, :, 2]
    run_top = jnp.full((query_rows, local_heads), -1e30, jnp.float32)
    key_part = lax.all_gather(key_rot, "blk", axis=0, tiled=True)
    value_part = lax.all_gather(value_rows, "blk", axis=0, tiled=True)
    key_ids = spread_rows(
        jnp.arange(key_part.shape[0], dtype=jnp.int32), query_rows, block_rows, tok_seq
    )
    key_request = segment_of(key_ids, request_ends)
    kept = jnp.take(key_keep, key_ids) == 1
    visible = (
        (query_request[:, None] == key_request[None, :])
        & (kept[None, :] | (query_ids[:, None] == key_ids[None, :]))
    )[:, None, :]
    scores = (
        jnp.einsum("qhd,khd->qhk", query_rot, key_part, preferred_element_type=jnp.float32)
        * inv_root
    )
    row_high = jnp.max(jnp.where(visible, scores, -1e30), axis=2)
    new_top = jnp.maximum(run_top, row_high)
    weights = jnp.where(visible, jnp.exp(scores - new_top[:, :, None]), 0.0)
    run_norm = jnp.sum(weights, axis=2)
    run_sum = jnp.einsum(
        "qhk,khd->qhd", weights.astype(jnp.bfloat16), value_part, preferred_element_type=jnp.float32
    )
    run_top, run_norm, run_sum = (new_top, run_norm, run_sum)
    attended = (run_sum / run_norm[:, :, None]).astype(jnp.bfloat16)
    attended = attended.reshape(query_rows, local_heads * head_size)
    attn_local = lax.all_to_all(
        lax.all_to_all(attended, "seq", split_axis=0, concat_axis=1, tiled=True),
        "blk",
        split_axis=1,
        concat_axis=0,
        tiled=True,
    )
    mlp_part = mlp_act
    summed = lax.psum_scatter(
        (
            jnp.dot(attn_local, w_attn_out, preferred_element_type=jnp.float32)
            + jnp.dot(mlp_part, w_mlp_out, preferred_element_type=jnp.float32)
        ).astype(jnp.bfloat16),
        "blk",
        scatter_dimension=0,
        tiled=True,
    ).astype(jnp.float32)
    return stream + mod_gate * summed


def solution(mesh):
    in_specs = (
        P(("seq", "blk"), None),
        P(),
        P(),
        P(),
        P(),
        P(),
        P(None, "blk"),
        P(None, "blk"),
        P(),
        P(),
        P("blk", None),
        P("blk", None),
    )
    out_specs = P(("seq", "blk"), None)
    return jax.shard_map(body, mesh=mesh, in_specs=in_specs, out_specs=out_specs, check_vma=False)
```

profile of v0, /device:TPU:32, one launch (start us, length us, event | category | flops | bytes accessed | tf_op | source)
XLA Modules:
  0.0 693.1 jit_solution(4572374142016408520)
XLA Ops:
  6.5 0.9 fusion.70
  7.5 1.1 reduce_sum.82
  8.5 1.1 multiply_reduce_fusion.2
  9.7 0.8 reduce-window.8
  10.5 0.1 convert_reduce_fusion.2
  10.6 2.8 fusion.11
  13.4 0.4 fusion.44
  13.9 0.7 fusion.41
  14.7 102.6 %all-gather.5.cloned.1.call-done = bf16[512,3072]{1,0:T(8,128)(2,1)} async-done(((bf16[16,3072]{1,0:T(8,128)(2,1)}), bf16[512,3072]{1,0:T(8,128)(2,1)}) %all-gather.5.cloned.1.call-update) | async-done | bytes 3145744 | tf_op jit(solution)/shard_map/all_gather | solution.py:114
  117.3 3.5 convolution_convert_fusion
  120.9 0.9 copy.79
  121.8 5.1 all-to-all-start
  126.9 0.7 mul.314
  127.7 0.7 mul.325
  128.4 2.8 copy.83
  131.2 2.8 gather_fusion.1
  134.1 0.9 copy.84
  135.0 0.5 fusion.78
  135.5 7.3 %all-to-all-done = bf16[32,16,288]{2,1,0:T(8,128)(2,1)S(1)} async-done(((bf16[32,16,288]{2,1,0:T(8,128)(2,1)}), bf16[32,16,288]{2,1,0:T(8,128)(2,1)S(1)}, u32[]{:S(2)}, u32[]{:S(2)}) %all-to-all-start) | async-done | bytes 294944 | tf_op jit(solution)/shard_map/all_to_all | solution.py:123
  142.9 0.8 copy.80
  143.7 1.5 all_to_all.53
  145.1 0.7 copy.81
  145.9 4.0 all-to-all-start.1
  149.8 0.7 fusion.71
  150.5 0.1 multiply_reduce_fusion.3
  150.6 0.8 fusion.87
  151.3 6.8 all-to-all-done.1
  158.1 0.7 copy-done.5
  158.8 1.1 reshape.619
  159.9 1.1 fusion.86
  161.0 0.7 multiply_reduce_fusion
  161.7 0.7 copy_convert_fusion
  162.4 0.6 add_rsqrt_fusion.1
  163.0 1.7 copy.86
  164.7 1.3 add_rsqrt_fusion
  166.0 0.8 copy.91
  166.8 1.1 multiply_multiply_fusion.2
  167.9 1.1 multiply_multiply_fusion.1
  169.0 2.0 subtract_convert_fusion
  170.9 0.2 pad_maximum_fusion
  171.2 0.7 copy.89
  172.0 0.8 copy.106
  172.8 0.2 reduce-scatter.2.cloned.1.call-start
  173.0 0.1 compare_select_fusion
  173.2 23.0 %gather_fusion = s32[4096]{0:T(1024)S(1)} fusion(s32[4096]{0:T(1024)S(1)} %copy-done.1, s32[4096]{0:T(1024)S(1)} %broadcast_clamp_fusion), kind=kCustom, calls=%fused_computation | custom fusion | bytes 49152 | tf_op jit(solution)/shard_map/jit(_take)/gather | solution.py:153
  196.3 0.1 convert_reduce_fusion.1
  196.4 0.1 convert_reduce_fusion
  196.5 4.5 or_and_fusion
  201.1 0.2 pad_maximum_fusion.1
  201.3 67.5 %all-gather.7.cloned.1.call-done = bf16[4096,3,128]{2,0,1:T(8,128)(2,1)} async-done(((bf16[128,3,128]{2,0,1:T(8,128)(2,1)}), bf16[4096,3,128]{2,0,1:T(8,128)(2,1)}) %all-gather.7.cloned.1.call-update) | async-done | bytes 3145744 | tf_op jit(solution)/shard_map/all_gather | solution.py:147
  268.8 3.2 fusion
  272.0 2.6 copy-done.2
  274.7 1.2 fusion.3
  275.9 105.5 %all-gather.9.cloned.1.call-done = bf16[4096,3,1,128]{0,3,1,2:T(8,128)(2,1)} async-done(((bf16[128,3,1,128]{0,3,1,2:T(8,128)(2,1)}), bf16[4096,3,1,128]{0,3,1,2:T(8,128)(2,1)}) %all-gather.9.cloned.1.call-update) | async-done | bytes 3145744 | tf_op jit(solution)/shard_map/all_gather | solution.py:148
  381.3 5.3 fusion.23
  386.7 0.1 copy.96
  386.8 0.1 all_to_all.56
  386.9 8.7 %all_to_all.67 = bf16[8,16,384]{2,1,0:T(8,128)(2,1)S(1)} all-to-all(bf16[8,16,384]{2,1,0:T(8,128)(2,1)S(1)} %all_to_all.56), channel_id=1, replica_groups=mesh['seq'=8,'blk'=32] {'seq'}, dimensions={0} | all-to-all | bytes 196608 | tf_op jit(solution)/shard_map/all_to_all | solution.py:173
  395.6 0.1 all_to_all.59
  395.8 20.1 %all_to_all.68 = bf16[16,32,96]{2,0,1:T(8,128)(2,1)S(1)} all-to-all(bf16[16,32,96]{2,0,1:T(8,128)(2,1)S(1)} %copy.98), channel_id=1, replica_groups=mesh['seq'=8,'blk'=32] {'blk'}, dimensions={1} | all-to-all | bytes 196608 | tf_op jit(solution)/shard_map/all_to_all | solution.py:172
  415.9 4.7 fusion.90
  420.6 9.6 %add_convert_fusion = bf16[512,3072]{1,0:T(8,128)(2,1)} fusion(f32[512,3072]{1,0:T(8,128)} %fusion.90, bf16[384,3072]{1,0:T(8,128)(2,1)S(1)} %copy-done, bf16[512,3072]{1,0:T(8,128)(2,1)} %all-gather.5.cloned.1.call-done, bf16[3072,384]{1,0:T(8,128)(2,1)} %param.19), kind=kOutput, calls=%fused_computation.7 | convolution fusion | flops 2420834304 | bytes 17301504 | tf_op jit(solution)/shard_map/dot_general | solution.py:183
  430.2 254.8 %reduce-scatter.2.cloned.1.call-done = bf16[16,3072]{1,0:T(8,128)(2,1)} async-done(((bf16[512,3072]{1,0:T(8,128)(2,1)}), bf16[16,3072]{1,0:T(8,128)(2,1)}) %reduce-scatter.2.cloned.1.call-update) | async-done | bytes 98320 | tf_op jit(solution)/shard_map/reduce_scatter | solution.py:180
  685.0 1.6 fusion.43
  (46 shorter events, 0.4 us)
Async XLA Ops:
  6.5 414.1 %copy-start = (bf16[384,3072]{1,0:T(8,128)(2,1)S(1)}, bf16[384,3072]{1,0:T(8,128)(2,1)}, u32[]{:S(2)}) copy-start(bf16[384,3072]{1,0:T(8,128)(2,1)} %param.23) | copy-start | bytes 7077892
  6.5 7.3 %copy-start.3 = (f32[16,3072]{1,0:T(8,128)S(1)}, f32[16,3072]{1,0:T(8,128)}, u32[]{:S(2)}) copy-start(f32[16,3072]{1,0:T(8,128)} %param.12) | copy-start | bytes 589828
  6.5 110.8 %all-gather.5.cloned.1.call-start = ((), (), s32[]{:S(2)}) async-start(), calls=%async_computation.5 | async-start | bytes 3244032 | tf_op jit(solution)/shard_map/all_gather | solution.py:114
  10.5 4.2 copy-start.11
  14.7 112.2 %copy-start.9 = (f32[128]{0:T(128)S(1)}, f32[128]{0:T(128)}, u32[]{:S(2)}) copy-start(f32[128]{0:T(128)} %param.21) | copy-start | bytes 1540
  14.7 113.0 %copy-start.10 = (f32[128]{0:T(128)S(1)}, f32[128]{0:T(128)}, u32[]{:S(2)}) copy-start(f32[128]{0:T(128)} %param.20) | copy-start | bytes 1540
  121.8 21.0 %all-to-all-start = ((bf16[32,16,288]{2,1,0:T(8,128)(2,1)}), bf16[32,16,288]{2,1,0:T(8,128)(2,1)S(1)}, u32[]{:S(2)}, u32[]{:S(2)}) async-start(bf16[32,16,288]{2,1,0:T(8,128)(2,1)} %bitcast.68), calls=%async_computation | async-start | bytes 786432 | tf_op jit(solution)/shard_map/all_to_all | solution.py:123
  145.9 12.2 %all-to-all-start.1 = ((bf16[16,8,1152]{2,0,1:T(8,128)(2,1)}), bf16[16,8,1152]{2,0,1:T(8,128)(2,1)S(1)}, u32[]{:S(2)}, u32[]{:S(2)}) async-start(bf16[16,8,1152]{2,0,1:T(8,128)(2,1)} %copy.81), calls=%async_computation.1 | async-start | bytes 589824 | tf_op jit(solution)/shard_map/all_to_all | solution.py:122
  149.8 119.0 %all-gather.7.cloned.1.call-start = ((), (), s32[]{:S(2)}) async-start(), calls=%async_computation.6 | async-start | bytes 3244032 | tf_op jit(solution)/shard_map/all_gather | solution.py:147
  158.1 0.7 copy-start.5
  158.8 14.3 %copy-start.1 = (s32[4096]{0:T(1024)S(1)}, s32[4096]{0:T(1024)}, u32[]{:S(2)}) copy-start(s32[4096]{0:T(1024)} %param.13) | copy-start | bytes 49156
  161.0 11.0 %copy-start.6 = (bf16[128,3,1,128]{3,2,1,0:T(2,128)(2,1)S(1)}, bf16[128,3,1,128]{3,2,1,0:T(2,128)(2,1)}, u32[]{:S(2)}) copy-start(bf16[128,3,1,128]{3,2,1,0:T(2,128)(2,1)} %get-tuple-element.5) | copy-start | bytes 294916
  171.9 209.4 %all-gather.9.cloned.1.call-start = ((), (), s32[]{:S(2)}) async-start(), calls=%async_computation.8 | async-start | bytes 3244032 | tf_op jit(solution)/shard_map/all_gather | solution.py:148
  172.8 512.2 %reduce-scatter.2.cloned.1.call-start = ((), (), s32[]{:S(2)}) async-start(), calls=%async_computation.7 | async-start | bytes 3244032 | tf_op jit(solution)/shard_map/reduce_scatter | solution.py:180
  173.1 23.1 %copy-start.12 = (s32[4,1]{0,1:T(1,128)S(1)}, s32[4,1]{0,1:T(1,128)}, u32[]{:S(2)}) copy-start(s32[4,1]{0,1:T(1,128)} %copy-done.11) | copy-start | bytes 52
  173.2 27.9 %copy-start.7 = (bf16[128,3,64,1]{0,3,2,1:T(2,128)(2,1)S(1)}, bf16[128,3,64,1]{0,3,2,1:T(2,128)(2,1)}, u32[]{:S(2)}) copy-start(bf16[128,3,64,1]{0,3,2,1:T(2,128)(2,1)} %get-tuple-element.8) | copy-start | bytes 147460
  173.2 27.9 %copy-start.8 = (bf16[128,3,64,1]{0,3,2,1:T(2,128)(2,1)S(1)}, bf16[128,3,64,1]{0,3,2,1:T(2,128)(2,1)}, u32[]{:S(2)}) copy-start(bf16[128,3,64,1]{0,3,2,1:T(2,128)(2,1)} %get-tuple-element.9) | copy-start | bytes 147460
  268.8 5.9 copy-start.4
  272.0 2.7 copy-start.2
Sparse Core Ops, SparseCore 0:
  14.8 102.5 all-gather.4
  172.1 96.7 all-gather.6
  272.0 109.2 all-gather.8
  430.3 254.6 reduce-scatter.1
where the time goes:
time: 694 us; the launch traced here: 693 us
  waiting for transfers between devices  545 us (79%)
  local copies, waits for them, and re-layouts  45.8 us (7%)
  matrix products  29.6 us (4%)
  blocking collectives  28.8 us (4%)
  other arithmetic  21.7 us (3%)
  between operations  13.4 us (2%)
  starting transfers between devices  9.3 us (1%)
    reduce_scatter x1, waiting for transfers between devices, body(): lax.psum_scatter((jnp.dot(attn_local, w_attn_out, preferred_element_type=...  255 us
    all_gather x1, waiting for transfers between devices, body(): value_part = lax.all_gather(value_rows, 'blk', axis=0, tiled=True)  105 us
    all_gather x1, waiting for transfers between devices, body(): shard_rows = lax.all_gather(modin, 'blk', axis=0, tiled=True)  103 us
    all_gather x1, waiting for transfers between devices, body(): key_part = lax.all_gather(key_rot, 'blk', axis=0, tiled=True)  67.5 us
    gather x1, local copies, waits for them, and re-layouts, body(): kept = jnp.take(key_keep, key_ids) == 1  23 us
    all_to_all x1, blocking collectives, body(): lax.all_to_all(lax.all_to_all(attended, 'seq', split_axis=0, concat_axis=...  20.1 us
  transfers between devices with their start and end apart: 6, of which 6 were waited for; matrix products, arithmetic and copies ran while one was open for 6% of the time, Pallas kernels for 0%

commit v1 on v0

--- a/solution.py
+++ b/solution.py
@@ -111,7 +111,9 @@
     normed = centered * lax.rsqrt(row_var + 1e-06)
     modin = ((1.0 + mod_scale) * normed + mod_shift).astype(jnp.bfloat16)
     qkv_width = w_qkv.shape[1]
-    shard_rows = lax.all_gather(modin, "blk", axis=0, tiled=True)
+    shard_rows = lax.all_to_all(
+        jnp.broadcast_to(modin[None], (blk_count,) + modin.shape), "blk", 0, 0, tiled=True
+    ).reshape(blk_count * block_rows, width)
     qkv_part = jnp.dot(shard_rows, w_qkv, preferred_element_type=jnp.float32).astype(jnp.bfloat16)
     mlp_part = jax.nn.gelu(
         jnp.dot(shard_rows, w_mlp_in, preferred_element_type=jnp.float32), approximate=True
@@ -177,15 +179,14 @@
         tiled=True,
     )
     mlp_part = mlp_act
-    summed = lax.psum_scatter(
-        (
-            jnp.dot(attn_local, w_attn_out, preferred_element_type=jnp.float32)
-            + jnp.dot(mlp_part, w_mlp_out, preferred_element_type=jnp.float32)
-        ).astype(jnp.bfloat16),
-        "blk",
-        scatter_dimension=0,
-        tiled=True,
-    ).astype(jnp.float32)
+    partial = (
+        jnp.dot(attn_local, w_attn_out, preferred_element_type=jnp.float32)
+        + jnp.dot(mlp_part, w_mlp_out, preferred_element_type=jnp.float32)
+    ).astype(jnp.bfloat16)
+    pieces = lax.all_to_all(
+        partial.reshape(blk_count, block_rows, width), "blk", 0, 0, tiled=True
+    )
+    summed = jnp.sum(pieces.astype(jnp.float32), axis=0)
     return stream + mod_gate * summed
 
 

time: 694 us -> 508 us (0.73)
  waiting for transfers between devices: 545 us -> 265 us
  blocking collectives: 28.8 us -> 108 us
  starting transfers between devices: 9.3 us -> 22.5 us
    reduce_scatter x1 -> x0, waiting for transfers between devices: 255 us -> none  [body(): lax.psum_scatter((jnp.dot(attn_local, w_attn_out, preferred_element_type=...]
    all_gather x1 -> x0, waiting for transfers between devices: 103 us -> none  [body(): shard_rows = lax.all_gather(modin, 'blk', axis=0, tiled=True)]
    all_to_all x0 -> x1, blocking collectives: none -> 79 us  [body(): lax.all_to_all(partial.reshape(blk_count, block_rows, width), 'blk', 0, 0...]
    all_to_all x0 -> x1, waiting for transfers between devices: none -> 76.3 us  [body(): lax.all_to_all(jnp.broadcast_to(modin[None], (blk_count,) + modin.shape),...]
    all_to_all x0 -> x1, starting transfers between devices: none -> 13.2 us  [body(): lax.all_to_all(jnp.broadcast_to(modin[None], (blk_count,) + modin.shape),...]
  transfers between devices with their start and end apart: 6 -> 5, of which waited for: 6 -> 5; matrix products, arithmetic and copies ran while one was open for 6% -> 9% of each run, Pallas kernels for 0% -> 0%
where the time goes in v1:
time: 508 us; the launch traced here: 507 us
  waiting for transfers between devices  265 us (52%)
  blocking collectives  108 us (21%)
  local copies, waits for them, and re-layouts  47.8 us (9%)
  matrix products  29.6 us (6%)
  starting transfers between devices  22.5 us (4%)
  other arithmetic  20.6 us (4%)
  between operations  13.7 us (3%)
    all_gather x1, waiting for transfers between devices, body(): value_part = lax.all_gather(value_rows, 'blk', axis=0, tiled=True)  105 us
    all_to_all x1, blocking collectives, body(): lax.all_to_all(partial.reshape(blk_count, block_rows, width), 'blk', 0, 0...  79 us
    all_to_all x1, waiting for transfers between devices, body(): lax.all_to_all(jnp.broadcast_to(modin[None], (blk_count,) + modin.shape),...  76.3 us
    all_gather x1, waiting for transfers between devices, body(): key_part = lax.all_gather(key_rot, 'blk', axis=0, tiled=True)  69.1 us
    gather x1, local copies, waits for them, and re-layouts, body(): kept = jnp.take(key_keep, key_ids) == 1  23 us
    all_to_all x1, blocking collectives, body(): lax.all_to_all(lax.all_to_all(attended, 'seq', split_axis=0, concat_axis=...  20.1 us
    all_to_all x1, starting transfers between devices, body(): lax.all_to_all(jnp.broadcast_to(modin[None], (blk_count,) + modin.shape),...  13.2 us
  transfers between devices with their start and end apart: 5, of which 5 were waited for; matrix products, arithmetic and copies ran while one was open for 9% of the time, Pallas kernels for 0%

profile of v1, /device:TPU:32, one launch (start us, length us, event | category | flops | bytes accessed | tf_op | source)
XLA Modules:
  0.0 506.6 jit_solution(7781617142355008761)
XLA Ops:
  6.5 0.9 fusion.70
  7.4 1.1 reduce_sum.91
  8.5 1.1 multiply_reduce_fusion.2
  9.6 0.8 reduce-window.8
  10.6 2.8 fusion.11
  13.4 0.4 fusion.44
  13.8 0.1 fusion.41
  14.0 2.0 broadcast_in_dim.66
  16.0 13.2 %all-to-all-start = ((bf16[32,16,3072]{2,1,0:T(8,128)(2,1)}), bf16[32,16,3072]{2,1,0:T(8,128)(2,1)}, u32[]{:S(2)}, u32[]{:S(2)}) async-start(bf16[32,16,3072]{2,1,0:T(8,128)(2,1)} %broadcast_in_dim.66), calls=%async_computation | async-start | bytes 6291456 | tf_op jit(solution)/shard_map/all_to_all | solution.py:114
  29.2 76.3 %all-to-all-done = bf16[32,16,3072]{2,1,0:T(8,128)(2,1)} async-done(((bf16[32,16,3072]{2,1,0:T(8,128)(2,1)}), bf16[32,16,3072]{2,1,0:T(8,128)(2,1)}, u32[]{:S(2)}, u32[]{:S(2)}) %all-to-all-start) | async-done | bytes 3145760 | tf_op jit(solution)/shard_map/all_to_all | solution.py:114
  105.6 3.6 convolution_convert_fusion
  109.1 0.9 copy.79
  110.1 5.0 all-to-all-start.1
  115.1 0.7 mul.314
  115.9 0.7 mul.325
  116.6 2.8 copy.83
  119.4 2.8 gather_fusion.1
  122.3 0.9 copy.84
  123.2 0.5 fusion.78
  123.8 6.9 %all-to-all-done.1 = bf16[32,16,288]{2,1,0:T(8,128)(2,1)S(1)} async-done(((bf16[32,16,288]{2,1,0:T(8,128)(2,1)}), bf16[32,16,288]{2,1,0:T(8,128)(2,1)S(1)}, u32[]{:S(2)}, u32[]{:S(2)}) %all-to-all-start.1) | async-done | bytes 294944 | tf_op jit(solution)/shard_map/all_to_all | solution.py:125
  130.7 0.8 copy.80
  131.5 1.5 all_to_all.60
  133.0 0.7 copy.81
  133.7 4.1 all-to-all-start.2
  137.8 0.7 fusion.71
  138.4 0.1 multiply_reduce_fusion.3
  138.5 0.8 fusion.87
  139.3 6.8 %all-to-all-done.2 = bf16[16,8,1152]{2,0,1:T(8,128)(2,1)S(1)} async-done(((bf16[16,8,1152]{2,0,1:T(8,128)(2,1)}), bf16[16,8,1152]{2,0,1:T(8,128)(2,1)S(1)}, u32[]{:S(2)}, u32[]{:S(2)}) %all-to-all-start.2) | async-done | bytes 294944 | tf_op jit(solution)/shard_map/all_to_all | solution.py:124
  146.0 0.7 copy-done.5
  146.7 1.1 reshape.627
  147.8 1.1 fusion.86
  148.9 0.7 multiply_reduce_fusion
  149.6 0.7 copy_convert_fusion
  150.3 0.6 add_rsqrt_fusion.1
  150.9 1.7 copy.86
  152.6 1.3 add_rsqrt_fusion
  153.9 0.8 copy.91
  154.7 1.1 multiply_multiply_fusion.2
  155.8 1.1 multiply_multiply_fusion.1
  156.9 2.0 subtract_convert_fusion
  158.9 0.2 pad_maximum_fusion
  159.1 0.7 copy.89
  159.9 0.2 all-gather.6.cloned.1.call-start
  160.1 0.8 copy.106
  160.9 0.1 compare_select_fusion
  161.0 23.0 %gather_fusion = s32[4096]{0:T(1024)S(1)} fusion(s32[4096]{0:T(1024)S(1)} %copy-done.1, s32[4096]{0:T(1024)S(1)} %broadcast_clamp_fusion), kind=kCustom, calls=%fused_computation | custom fusion | bytes 49152 | tf_op jit(solution)/shard_map/jit(_take)/gather | solution.py:155
  184.2 0.1 convert_reduce_fusion.1
  184.4 4.5 or_and_fusion
  188.9 0.2 pad_maximum_fusion.1
  189.2 69.1 %all-gather.4.cloned.1.call-done = bf16[4096,3,128]{2,0,1:T(8,128)(2,1)} async-done(((bf16[128,3,128]{2,0,1:T(8,128)(2,1)}), bf16[4096,3,128]{2,0,1:T(8,128)(2,1)}) %all-gather.4.cloned.1.call-update) | async-done | bytes 3145744 | tf_op jit(solution)/shard_map/all_gather | solution.py:149
  258.2 3.2 fusion
  261.5 2.6 copy-done.2
  264.1 1.2 fusion.3
  265.3 105.5 %all-gather.6.cloned.1.call-done = bf16[4096,3,1,128]{0,3,1,2:T(8,128)(2,1)} async-done(((bf16[128,3,1,128]{0,3,1,2:T(8,128)(2,1)}), bf16[4096,3,1,128]{0,3,1,2:T(8,128)(2,1)}) %all-gather.6.cloned.1.call-update) | async-done | bytes 3145744 | tf_op jit(solution)/shard_map/all_gather | solution.py:150
  370.8 5.3 %fusion.23 = bf16[128,3,128]{0,2,1:T(8,128)(2,1)S(1)} fusion(f32[3,4096,128]{2,1,0:T(8,128)} %copy-done.2, f32[128,3]{0,1:T(4,128)S(1)} %broadcast_maximum_fusion, pred[128,4096]{0,1:T(8,128)(4,1)} %or_and_fusion, bf16[4096,3,1,128]{0,3,1,2:T(8,128)(2,1)} %all-gather.6.cloned.1.call-done, f32[128,3]{0,1:T(4,128)S(1)} %fusion.3), kind=kOutput, calls=%fused_computation.24 | convolution fusion | flops 407470080 | bytes 10062848 | tf_op jit(solution)/shard_map/qhk,khd->qhd/dot_general | solution.py:168
  376.1 0.1 copy.96
  376.3 8.7 %all_to_all.77 = bf16[8,16,384]{2,1,0:T(8,128)(2,1)S(1)} all-to-all(bf16[8,16,384]{2,1,0:T(8,128)(2,1)S(1)} %all_to_all.63), channel_id=1, replica_groups=mesh['seq'=8,'blk'=32] {'seq'}, dimensions={0} | all-to-all | bytes 196608 | tf_op jit(solution)/shard_map/all_to_all | solution.py:175
  385.0 0.1 all_to_all.66
  385.2 20.1 %all_to_all.78 = bf16[16,32,96]{2,0,1:T(8,128)(2,1)S(1)} all-to-all(bf16[16,32,96]{2,0,1:T(8,128)(2,1)S(1)} %copy.98), channel_id=1, replica_groups=mesh['seq'=8,'blk'=32] {'blk'}, dimensions={1} | all-to-all | bytes 196608 | tf_op jit(solution)/shard_map/all_to_all | solution.py:174
  405.3 4.7 fusion.90
  410.0 9.6 %add_convert_fusion = bf16[512,3072]{1,0:T(8,128)(2,1)} fusion(f32[512,3072]{1,0:T(8,128)} %fusion.90, bf16[384,3072]{1,0:T(8,128)(2,1)S(1)} %copy-done, bf16[512,3072]{1,0:T(8,128)(2,1)} %bitcast.5, bf16[3072,384]{1,0:T(8,128)(2,1)} %param.19), kind=kOutput, calls=%fused_computation.8 | convolution fusion | flops 2420834304 | bytes 17301504 | tf_op jit(solution)/shard_map/dot_general | solution.py:184
  419.6 79.0 %all_to_all.79 = bf16[32,16,3072]{2,1,0:T(8,128)(2,1)S(1)} all-to-all(bf16[32,16,3072]{2,1,0:T(8,128)(2,1)} %bitcast.68), channel_id=1, replica_groups=mesh['seq'=8,'blk'=32] {'blk'}, dimensions={0} | all-to-all | bytes 6291456 | tf_op jit(solution)/shard_map/all_to_all | solution.py:186
  498.6 0.5 convert_reduce_fusion
  499.0 0.7 fusion.43
  (45 shorter events, 0.6 us)
Async XLA Ops:
  6.5 403.5 %copy-start = (bf16[384,3072]{1,0:T(8,128)(2,1)S(1)}, bf16[384,3072]{1,0:T(8,128)(2,1)}, u32[]{:S(2)}) copy-start(bf16[384,3072]{1,0:T(8,128)(2,1)} %param.23) | copy-start | bytes 7077892
  6.5 7.3 %copy-start.3 = (f32[16,3072]{1,0:T(8,128)S(1)}, f32[16,3072]{1,0:T(8,128)}, u32[]{:S(2)}) copy-start(f32[16,3072]{1,0:T(8,128)} %param.12) | copy-start | bytes 589828
  10.5 5.5 %copy-start.11 = (s32[4,1]{0,1:T(1,128)}, s32[4,1]{0,1:T(1,128)S(1)}, u32[]{:S(2)}) copy-start(s32[4,1]{0,1:T(1,128)S(1)} %reduce-window.8) | copy-start | bytes 52
  16.0 89.5 %all-to-all-start = ((bf16[32,16,3072]{2,1,0:T(8,128)(2,1)}), bf16[32,16,3072]{2,1,0:T(8,128)(2,1)}, u32[]{:S(2)}, u32[]{:S(2)}) async-start(bf16[32,16,3072]{2,1,0:T(8,128)(2,1)} %broadcast_in_dim.66), calls=%async_computation | async-start | bytes 6291456 | tf_op jit(solution)/shard_map/all_to_all | solution.py:114
  105.5 9.6 %copy-start.9 = (f32[128]{0:T(128)S(1)}, f32[128]{0:T(128)}, u32[]{:S(2)}) copy-start(f32[128]{0:T(128)} %param.21) | copy-start | bytes 1540
  105.5 10.3 %copy-start.10 = (f32[128]{0:T(128)S(1)}, f32[128]{0:T(128)}, u32[]{:S(2)}) copy-start(f32[128]{0:T(128)} %param.20) | copy-start | bytes 1540
  110.1 20.6 %all-to-all-start.1 = ((bf16[32,16,288]{2,1,0:T(8,128)(2,1)}), bf16[32,16,288]{2,1,0:T(8,128)(2,1)S(1)}, u32[]{:S(2)}, u32[]{:S(2)}) async-start(bf16[32,16,288]{2,1,0:T(8,128)(2,1)} %bitcast.71), calls=%async_computation.1 | async-start | bytes 786432 | tf_op jit(solution)/shard_map/all_to_all | solution.py:125
  133.7 12.3 %all-to-all-start.2 = ((bf16[16,8,1152]{2,0,1:T(8,128)(2,1)}), bf16[16,8,1152]{2,0,1:T(8,128)(2,1)S(1)}, u32[]{:S(2)}, u32[]{:S(2)}) async-start(bf16[16,8,1152]{2,0,1:T(8,128)(2,1)} %copy.81), calls=%async_computation.2 | async-start | bytes 589824 | tf_op jit(solution)/shard_map/all_to_all | solution.py:124
  137.8 120.5 %all-gather.4.cloned.1.call-start = ((), (), s32[]{:S(2)}) async-start(), calls=%async_computation.6 | async-start | bytes 3244032 | tf_op jit(solution)/shard_map/all_gather | solution.py:149
  146.0 0.7 copy-start.5
  146.7 14.3 %copy-start.1 = (s32[4096]{0:T(1024)S(1)}, s32[4096]{0:T(1024)}, u32[]{:S(2)}) copy-start(s32[4096]{0:T(1024)} %param.13) | copy-start | bytes 49156
  148.9 11.2 %copy-start.6 = (bf16[128,3,1,128]{3,2,1,0:T(2,128)(2,1)S(1)}, bf16[128,3,1,128]{3,2,1,0:T(2,128)(2,1)}, u32[]{:S(2)}) copy-start(bf16[128,3,1,128]{3,2,1,0:T(2,128)(2,1)} %get-tuple-element.5) | copy-start | bytes 294916
  159.9 210.9 %all-gather.6.cloned.1.call-start = ((), (), s32[]{:S(2)}) async-start(), calls=%async_computation.7 | async-start | bytes 3244032 | tf_op jit(solution)/shard_map/all_gather | solution.py:150
  161.0 23.1 %copy-start.12 = (s32[4,1]{0,1:T(1,128)S(1)}, s32[4,1]{0,1:T(1,128)}, u32[]{:S(2)}) copy-start(s32[4,1]{0,1:T(1,128)} %copy-done.11) | copy-start | bytes 52
  161.0 27.9 %copy-start.7 = (bf16[128,3,64,1]{0,3,2,1:T(2,128)(2,1)S(1)}, bf16[128,3,64,1]{0,3,2,1:T(2,128)(2,1)}, u32[]{:S(2)}) copy-start(bf16[128,3,64,1]{0,3,2,1:T(2,128)(2,1)} %get-tuple-element.8) | copy-start | bytes 147460
  161.0 27.9 %copy-start.8 = (bf16[128,3,64,1]{0,3,2,1:T(2,128)(2,1)S(1)}, bf16[128,3,64,1]{0,3,2,1:T(2,128)(2,1)}, u32[]{:S(2)}) copy-start(bf16[128,3,64,1]{0,3,2,1:T(2,128)(2,1)} %get-tuple-element.9) | copy-start | bytes 147460
  258.2 5.9 %copy-start.4 = (pred[128,4096]{0,1:T(8,128)(4,1)S(1)}, pred[128,4096]{0,1:T(8,128)(4,1)}, u32[]{:S(2)}) copy-start(pred[128,4096]{0,1:T(8,128)(4,1)} %or_and_fusion) | copy-start | bytes 1572868
  261.4 2.7 copy-start.2
Sparse Core Ops, SparseCore 0:
  160.0 98.2 all-gather.3
  261.4 109.2 all-gather.5

commit v2 on v1

--- a/solution.py
+++ b/solution.py
@@ -58,6 +58,37 @@
     owner = row_ids // query_rows
     within = row_ids % query_rows
     return within // block_rows * tok_seq + owner * block_rows + within % block_rows
+
+
+SEQ = ("zl", "core")
+BLK = ("y", "zh", "x")
+PLANE = ("y", "x")
+SWAP = [(0, 1), (1, 0)]
+
+
+def by_half(mine, other):
+    first = lax.axis_index("zh") == 0
+    return jnp.where(first, mine, other), jnp.where(first, other, mine)
+
+
+def gather_blk(x):
+    low, high = by_half(x, lax.ppermute(x, "zh", SWAP))
+    pair = jnp.stack([low, high])
+    plane = lax.axis_size("y") * lax.axis_size("x")
+    got = lax.all_to_all(jnp.broadcast_to(pair[None], (plane,) + pair.shape), PLANE, 0, 0, tiled=True)
+    got = got.reshape((lax.axis_size("y"), lax.axis_size("x"), 2) + x.shape)
+    return jnp.swapaxes(got, 1, 2).reshape((-1,) + x.shape[1:])
+
+
+def reduce_blk(y):
+    ys, xs = lax.axis_size("y"), lax.axis_size("x")
+    rows = y.shape[0] // (ys * 2 * xs)
+    pieces = jnp.swapaxes(y.reshape((ys, 2, xs, rows) + y.shape[1:]), 1, 2)
+    pieces = pieces.reshape((ys * xs, 2, rows) + y.shape[1:])
+    got = lax.all_to_all(pieces, PLANE, 0, 0, tiled=True)
+    part = jnp.sum(got.astype(jnp.float32), axis=0)
+    mine, theirs = by_half(part[0], part[1])
+    return mine + lax.ppermute(theirs, "zh", SWAP)
 
 
 def body(
@@ -74,10 +105,10 @@
     w_attn_out,
     w_mlp_out,
 ):
-    blk_count = lax.axis_size("blk")
-    seq_count = lax.axis_size("seq")
-    seq_at = lax.axis_index("seq")
-    blk_at = lax.axis_index("blk")
+    blk_count = lax.axis_size(BLK)
+    seq_count = lax.axis_size(SEQ)
+    seq_at = lax.axis_index(SEQ)
+    blk_at = lax.axis_index(BLK)
     block_rows = stream.shape[0]
     width = stream.shape[1]
     tok_seq = block_rows * blk_count
@@ -111,9 +142,7 @@
     normed = centered * lax.rsqrt(row_var + 1e-06)
     modin = ((1.0 + mod_scale) * normed + mod_shift).astype(jnp.bfloat16)
     qkv_width = w_qkv.shape[1]
-    shard_rows = lax.all_to_all(
-        jnp.broadcast_to(modin[None], (blk_count,) + modin.shape), "blk", 0, 0, tiled=True
-    ).reshape(blk_count * block_rows, width)
+    shard_rows = gather_blk(modin)
     qkv_part = jnp.dot(shard_rows, w_qkv, preferred_element_type=jnp.float32).astype(jnp.bfloat16)
     mlp_part = jax.nn.gelu(
         jnp.dot(shard_rows, w_mlp_in, preferred_element_type=jnp.float32), approximate=True
@@ -122,8 +151,8 @@
     qkv_cols = joined[:, :qkv_width]
     mlp_act = joined[:, qkv_width:]
     heads_in = lax.all_to_all(
-        lax.all_to_all(qkv_cols, "blk", split_axis=0, concat_axis=1, tiled=True),
-        "seq",
+        lax.all_to_all(qkv_cols, BLK, split_axis=0, concat_axis=1, tiled=True),
+        SEQ,
         split_axis=1,
         concat_axis=0,
         tiled=True,
@@ -146,8 +175,13 @@
     )
     value_rows = heads4[:, :, 2]
     run_top = jnp.full((query_rows, local_heads), -1e30, jnp.float32)
-    key_part = lax.all_gather(key_rot, "blk", axis=0, tiled=True)
-    value_part = lax.all_gather(value_rows, "blk", axis=0, tiled=True)
+    kv_rows = jnp.concatenate(
+        [key_rot.reshape(query_rows, -1), value_rows.reshape(query_rows, -1)], axis=1
+    )
+    kv_all = gather_blk(kv_rows)
+    kv_half = kv_all.shape[1] // 2
+    key_part = kv_all[:, :kv_half].reshape(-1, local_heads, head_size)
+    value_part = kv_all[:, kv_half:].reshape(-1, local_heads, head_size)
     key_ids = spread_rows(
         jnp.arange(key_part.shape[0], dtype=jnp.int32), query_rows, block_rows, tok_seq
     )
@@ -172,8 +206,8 @@
     attended = (run_sum / run_norm[:, :, None]).astype(jnp.bfloat16)
     attended = attended.reshape(query_rows, local_heads * head_size)
     attn_local = lax.all_to_all(
-        lax.all_to_all(attended, "seq", split_axis=0, concat_axis=1, tiled=True),
-        "blk",
+        lax.all_to_all(attended, SEQ, split_axis=0, concat_axis=1, tiled=True),
+        BLK,
         split_axis=1,
         concat_axis=0,
         tiled=True,
@@ -183,27 +217,27 @@
         jnp.dot(attn_local, w_attn_out, preferred_element_type=jnp.float32)
         + jnp.dot(mlp_part, w_mlp_out, preferred_element_type=jnp.float32)
     ).astype(jnp.bfloat16)
-    pieces = lax.all_to_all(
-        partial.reshape(blk_count, block_rows, width), "blk", 0, 0, tiled=True
-    )
-    summed = jnp.sum(pieces.astype(jnp.float32), axis=0)
+    summed = reduce_blk(partial)
     return stream + mod_gate * summed
 
 
 def solution(mesh):
+    zl = mesh.shape["seq"] // 2
+    ys, xs = 4, mesh.shape["blk"] // 8
+    fine = jax.sharding.Mesh(mesh.devices.reshape(zl, 2, ys, 2, xs), SEQ + BLK)
     in_specs = (
-        P(("seq", "blk"), None),
-        P(),
-        P(),
-        P(),
-        P(),
-        P(),
-        P(None, "blk"),
-        P(None, "blk"),
-        P(),
-        P(),
-        P("blk", None),
-        P("blk", None),
-    )
-    out_specs = P(("seq", "blk"), None)
-    return jax.shard_map(body, mesh=mesh, in_specs=in_specs, out_specs=out_specs, check_vma=False)
+        P(SEQ + BLK, None),
+        P(),
+        P(),
+        P(),
+        P(),
+        P(),
+        P(None, BLK),
+        P(None, BLK),
+        P(),
+        P(),
+        P(BLK, None),
+        P(BLK, None),
+    )
+    out_specs = P(SEQ + BLK, None)
+    return jax.shard_map(body, mesh=fine, in_specs=in_specs, out_specs=out_specs, check_vma=False)

time: 508 us -> 365 us (0.72)
  waiting for transfers between devices: 265 us -> 145 us
  blocking collectives: 108 us -> 80.5 us
  starting transfers between devices: 22.5 us -> 39.5 us
  local copies, waits for them, and re-layouts: 47.8 us -> 61.3 us
  between operations: 13.7 us -> 0.44 us
  other arithmetic: 20.6 us -> 13.8 us
  matrix products: 29.6 us -> 24.2 us
    all_gather x2 -> x0, waiting for transfers between devices: 175 us -> none  [the longest x1 105 us: body(): value_part = lax.all_gather(value_rows, 'blk', axis=0, tiled=True)]
    all_to_all x3 -> x4, waiting for transfers between devices: 90 us -> 118 us  [the longest x2 101 us: gather_blk(): lax.all_to_all(jnp.broadcast_to(pair[None], (plane,) + pair.shape), PLANE...]
    all_to_all x3, blocking collectives: 108 us -> 80.5 us  [the longest x1 42.8 us: reduce_blk(): got = lax.all_to_all(pieces, PLANE, 0, 0, tiled=True)]
    ppermute x0 -> x3, waiting for transfers between devices: none -> 26.2 us  [the longest x2 14.5 us: gather_blk(): low, high = by_half(x, lax.ppermute(x, 'zh', SWAP))]
    slice x0 -> x4, local copies, waits for them, and re-layouts: none -> 13.3 us  [the longest x2 8.19 us: body(): key_part = kv_all[:, :kv_half].reshape(-1, local_heads, head_size)]
    ppermute x0 -> x3, starting transfers between devices: none -> 9 us  [the longest x2 8.26 us: gather_blk(): low, high = by_half(x, lax.ppermute(x, 'zh', SWAP))]
    all_to_all x3 -> x4, starting transfers between devices: 22.2 us -> 30.5 us  [the longest x2 11.9 us: gather_blk(): lax.all_to_all(jnp.broadcast_to(pair[None], (plane,) + pair.shape), PLANE...]
    transpose x0 -> x2, local copies, waits for them, and re-layouts: none -> 5.53 us  [gather_blk(): return jnp.swapaxes(got, 1, 2).reshape((-1,) + x.shape[1:])]
  transfers between devices with their start and end apart: 5 -> 7, of which waited for: 5 -> 7; matrix products, arithmetic and copies ran while one was open for 9% -> 9% of each run, Pallas kernels for 0% -> 0%
where the time goes in v2:
time: 365 us; the launch traced here: 364 us
  waiting for transfers between devices  145 us (40%)
  blocking collectives  80.5 us (22%)
  local copies, waits for them, and re-layouts  61.3 us (17%)
  starting transfers between devices  39.5 us (11%)
  matrix products  24.2 us (7%)
  other arithmetic  13.8 us (4%)
    all_to_all x2, waiting for transfers between devices, gather_blk(): lax.all_to_all(jnp.broadcast_to(pair[None], (plane,) + pair.shape), PLANE...  101 us
    all_to_all x1, blocking collectives, reduce_blk(): got = lax.all_to_all(pieces, PLANE, 0, 0, tiled=True)  42.8 us
    gather x1, local copies, waits for them, and re-layouts, body(): kept = jnp.take(key_keep, key_ids) == 1  23 us
    all_to_all x1, blocking collectives, body(): lax.all_to_all(attended, SEQ, split_axis=0, concat_axis=1, tiled=True)  19.4 us
    all_to_all x1, blocking collectives, body(): lax.all_to_all(lax.all_to_all(attended, SEQ, split_axis=0, concat_axis=1,...  18.4 us
    ppermute x2, waiting for transfers between devices, gather_blk(): low, high = by_half(x, lax.ppermute(x, 'zh', SWAP))  14.5 us
    all_to_all x2, starting transfers between devices, gather_blk(): lax.all_to_all(jnp.broadcast_to(pair[None], (plane,) + pair.shape), PLANE...  11.9 us
    ppermute x1, waiting for transfers between devices, reduce_blk(): return mine + lax.ppermute(theirs, 'zh', SWAP)  11.7 us
  transfers between devices with their start and end apart: 7, of which 7 were waited for; matrix products, arithmetic and copies ran while one was open for 9% of the time, Pallas kernels for 0%

profile of v2, /device:TPU:32, one launch (start us, length us, event | category | flops | bytes accessed | tf_op | source)
XLA Modules:
  0.0 364.2 jit_solution(7023942703265286765)
XLA Ops:
  0.0 0.9 fusion.63
  0.9 1.1 reduce_sum.92
  2.0 1.1 multiply_reduce_fusion.2
  3.1 2.8 fusion.10
  5.9 0.8 reduce-window.8
  6.8 0.4 fusion.37
  7.3 0.8 copy-done.5
  8.2 6.4 %collective-permute-start = (bf16[16,3072]{1,0:T(8,128)(2,1)S(1)}, bf16[16,3072]{1,0:T(8,128)(2,1)S(1)}, u32[]{:S(2)}, u32[]{:S(2)}) collective-permute-start(bf16[16,3072]{1,0:T(8,128)(2,1)S(1)} %fusion.34), channel_id=1, source_target_pairs={{0,4},{4,0},{1,5},{5,1},{2,6},{6,2},{3,7},{7,3},{8,12},{12,8},{9,1... | collective-permute-start | bytes 294920 | tf_op jit(solution)/shard_map/ppermute | solution.py:75
  14.6 4.3 %collective-permute-done = bf16[16,3072]{1,0:T(8,128)(2,1)S(1)} collective-permute-done((bf16[16,3072]{1,0:T(8,128)(2,1)S(1)}, bf16[16,3072]{1,0:T(8,128)(2,1)S(1)}, u32[]{:S(2)}, u32[]{:S(2)}) %collective-permute-start) | collective-permute-done | bytes 98336 | tf_op jit(solution)/shard_map/ppermute | solution.py:75
  18.9 2.1 broadcast_in_dim.123
  21.0 7.1 %all-to-all-start = ((bf16[16,2,16,3072]{3,2,1,0:T(8,128)(2,1)}), bf16[16,2,16,3072]{3,2,1,0:T(8,128)(2,1)}, u32[]{:S(2)}, u32[]{:S(2)}) async-start(bf16[16,2,16,3072]{3,2,1,0:T(8,128)(2,1)} %broadcast_in_dim.123), calls=%async_computation | async-start | bytes 6291456 | tf_op jit(solution)/shard_map/all_to_all | solution.py:78
  28.1 41.6 %all-to-all-done = bf16[16,2,16,3072]{3,2,1,0:T(8,128)(2,1)} async-done(((bf16[16,2,16,3072]{3,2,1,0:T(8,128)(2,1)}), bf16[16,2,16,3072]{3,2,1,0:T(8,128)(2,1)}, u32[]{:S(2)}, u32[]{:S(2)}) %all-to-all-start) | async-done | bytes 3145760 | tf_op jit(solution)/shard_map/all_to_all | solution.py:78
  69.8 2.3 copy.99
  72.1 1.7 copy-done.2
  73.8 1.1 convolution_convert_fusion
  74.9 0.9 copy.100
  75.8 7.3 %all-to-all-start.1 = ((bf16[32,16,288]{2,1,0:T(8,128)(2,1)}), bf16[32,16,288]{2,1,0:T(8,128)(2,1)S(1)}, u32[]{:S(2)}, u32[]{:S(2)}) async-start(bf16[32,16,288]{2,1,0:T(8,128)(2,1)} %bitcast.11), calls=%async_computation.1 | async-start | bytes 786432 | tf_op jit(solution)/shard_map/all_to_all | solution.py:154
  83.2 0.1 mul.337
  83.3 2.0 copy.97
  85.3 2.2 gather_fusion
  87.6 0.1 mul.320
  87.8 9.6 %all-to-all-done.1 = bf16[32,16,288]{2,1,0:T(8,128)(2,1)S(1)} async-done(((bf16[32,16,288]{2,1,0:T(8,128)(2,1)}), bf16[32,16,288]{2,1,0:T(8,128)(2,1)S(1)}, u32[]{:S(2)}, u32[]{:S(2)}) %all-to-all-start.1) | async-done | bytes 294944 | tf_op jit(solution)/shard_map/all_to_all | solution.py:154
  97.6 0.5 all_to_all.63
  98.0 0.7 copy.102
  98.8 11.3 %all-to-all-start.2 = ((bf16[16,8,1152]{2,0,1:T(8,128)(2,1)}), bf16[16,8,1152]{2,0,1:T(8,128)(2,1)S(1)}, u32[]{:S(2)}, u32[]{:S(2)}) async-start(bf16[16,8,1152]{2,0,1:T(8,128)(2,1)} %copy.102), calls=%async_computation.2 | async-start | bytes 589824 | tf_op jit(solution)/shard_map/all_to_all | solution.py:153
  110.3 8.0 %all-to-all-done.2 = bf16[16,8,1152]{2,0,1:T(8,128)(2,1)S(1)} async-done(((bf16[16,8,1152]{2,0,1:T(8,128)(2,1)}), bf16[16,8,1152]{2,0,1:T(8,128)(2,1)S(1)}, u32[]{:S(2)}, u32[]{:S(2)}) %all-to-all-start.2) | async-done | bytes 294944 | tf_op jit(solution)/shard_map/all_to_all | solution.py:153
  118.4 0.4 fusion.80
  118.9 0.2 multiply_reduce_fusion
  119.1 0.1 copy.107
  119.2 0.1 copy.113
  119.4 0.1 copy.104
  119.5 0.1 multiply_multiply_fusion.1
  119.6 0.1 multiply_multiply_fusion.2
  119.8 1.2 subtract_convert_fusion
  121.0 0.2 pad_maximum_fusion.3
  121.2 1.9 collective-permute-start.1
  123.1 10.2 %collective-permute-done.1 = bf16[128,768]{0,1:T(8,128)(2,1)S(1)} collective-permute-done((bf16[128,768]{0,1:T(8,128)(2,1)S(1)}, bf16[128,768]{0,1:T(8,128)(2,1)S(1)}, u32[]{:S(2)}, u32[]{:S(2)}) %collective-permute-start.1) | collective-permute-done | bytes 196640 | tf_op jit(solution)/shard_map/ppermute | solution.py:75
  133.5 0.2 copy.108
  133.7 3.4 broadcast_in_dim.124
  137.1 4.8 %all-to-all-start.3 = ((bf16[16,2,128,768]{3,2,1,0:T(8,128)(2,1)}), bf16[16,2,128,768]{3,2,1,0:T(8,128)(2,1)}, u32[]{:S(2)}, u32[]{:S(2)}) async-start(bf16[16,2,128,768]{3,2,1,0:T(8,128)(2,1)} %broadcast_in_dim.124), calls=%async_computation.3 | async-start | bytes 12582912 | tf_op jit(solution)/shard_map/all_to_all | solution.py:78
  142.0 0.6 copy-done.1
  142.6 23.0 %gather_fusion.1 = s32[4096]{0:T(1024)S(1)} fusion(s32[4096]{0:T(1024)S(1)} %copy-done.1, s32[4096]{0:T(1024)S(1)} %broadcast_clamp_fusion), kind=kCustom, calls=%fused_computation.1 | custom fusion | bytes 49152 | tf_op jit(solution)/shard_map/jit(_take)/gather | solution.py:189
  165.9 3.4 or_and_fusion
  169.3 0.2 pad_maximum_fusion.4
  169.6 59.1 %all-to-all-done.3 = bf16[16,2,128,768]{3,2,1,0:T(8,128)(2,1)} async-done(((bf16[16,2,128,768]{3,2,1,0:T(8,128)(2,1)}), bf16[16,2,128,768]{3,2,1,0:T(8,128)(2,1)}, u32[]{:S(2)}, u32[]{:S(2)}) %all-to-all-start.3) | async-done | bytes 6291488 | tf_op jit(solution)/shard_map/all_to_all | solution.py:78
  228.6 3.2 copy.109
  231.8 3.3 fusion.79
  235.1 4.7 %copy.110 = bf16[4096,384]{0,1:T(8,128)(2,1)} copy(bf16[4096,384]{1,0:T(8,128)(2,1)} %get-tuple-element.6) | data formatting | bytes 6291456 | tf_op jit(solution)/shard_map/slice | solution.py:184
  239.8 4.9 %copy.111 = bf16[4096,384]{0,1:T(8,128)(2,1)} copy(bf16[4096,384]{1,0:T(8,128)(2,1)} %get-tuple-element.5) | data formatting | bytes 6291456 | tf_op jit(solution)/shard_map/slice | solution.py:183
  244.7 3.6 fusion
  248.3 1.2 fusion.3
  249.5 0.7 copy-done.3
  250.2 1.8 fusion.18
  252.0 0.1 copy.119
  252.3 19.4 %all_to_all.82 = bf16[8,16,384]{2,1,0:T(8,128)(2,1)S(1)} all-to-all(bf16[8,16,384]{2,1,0:T(8,128)(2,1)S(1)} %all_to_all.67), channel_id=1, replica_groups=mesh['zl'=4,'core'=2,'y'=4,'zh'=2,'x'=4] {'zl','core'}, dimensions={0} | all-to-all | bytes 196608 | tf_op jit(solution)/shard_map/all_to_all | solution.py:209
  271.8 18.4 %all_to_all.83 = bf16[16,32,96]{2,0,1:T(8,128)(2,1)S(1)} all-to-all(bf16[16,32,96]{2,0,1:T(8,128)(2,1)S(1)} %copy.121), channel_id=1, replica_groups=mesh['zl'=4,'core'=2,'y'=4,'zh'=2,'x'=4] {'y','zh','x'}, dimensions={1} | all-to-all | bytes 196608 | tf_op jit(solution)/shard_map/all_to_all | solution.py:208
  290.2 4.7 %fusion.84 = f32[512,3072]{1,0:T(8,128)} fusion(bf16[512,96]{1,0:T(8,128)(2,1)S(1)} %bitcast.101, bf16[96,3072]{1,0:T(8,128)(2,1)} %param.22), kind=kOutput, calls=%fused_computation.178 | convolution fusion | flops 301989888 | bytes 6979584 | tf_op jit(solution)/shard_map/dot_general | solution.py:217
  294.9 9.7 %add_convert_fusion = bf16[512,3072]{1,0:T(8,128)(2,1)} fusion(f32[512,3072]{1,0:T(8,128)} %fusion.84, bf16[384,3072]{1,0:T(8,128)(2,1)S(1)} %copy-done, bf16[512,3072]{1,0:T(8,128)(2,1)} %bitcast.91, bf16[3072,384]{1,0:T(8,128)(2,1)} %param.19), kind=kOutput, calls=%fused_computation.8 | convolution fusion | flops 2420834304 | bytes 17301504 | tf_op jit(solution)/shard_map/dot_general | solution.py:218
  304.6 2.2 copy.122
  306.8 42.8 %all_to_all.84 = bf16[16,2,16,3072]{3,2,1,0:T(8,128)(2,1)S(1)} all-to-all(bf16[16,2,16,3072]{3,2,1,0:T(8,128)(2,1)S(1)} %bitcast.88), channel_id=1, replica_groups=mesh['zl'=4,'core'=2,'y'=4,'zh'=2,'x'=4] {'y','x'}, dimensions={0} | all-to-all | bytes 6291456 | tf_op jit(solution)/shard_map/all_to_all | solution.py:88
  349.5 0.6 convert_reduce_fusion
  350.1 0.7 collective-permute-start.2
  350.9 11.7 %collective-permute-done.2 = f32[16,3072]{1,0:T(8,128)S(1)} collective-permute-done((f32[16,3072]{1,0:T(8,128)S(1)}, f32[16,3072]{1,0:T(8,128)S(1)}, u32[]{:S(2)}, u32[]{:S(2)}) %collective-permute-start.2) | collective-permute-done | bytes 196640 | tf_op jit(solution)/shard_map/ppermute | solution.py:91
  362.5 1.7 fusion.36
  (58 shorter events, 1.7 us)
Async XLA Ops:
  0.0 294.9 %copy-start = (bf16[384,3072]{1,0:T(8,128)(2,1)S(1)}, bf16[384,3072]{1,0:T(8,128)(2,1)}, u32[]{:S(2)}) copy-start(bf16[384,3072]{1,0:T(8,128)(2,1)} %param.23) | copy-start | bytes 7077892
  0.0 8.1 %copy-start.4 = (f32[16,3072]{1,0:T(8,128)S(1)}, f32[16,3072]{1,0:T(8,128)}, u32[]{:S(2)}) copy-start(f32[16,3072]{1,0:T(8,128)} %param.12) | copy-start | bytes 589828
  7.3 0.8 copy-start.5
  8.2 10.6 %collective-permute-start = (bf16[16,3072]{1,0:T(8,128)(2,1)S(1)}, bf16[16,3072]{1,0:T(8,128)(2,1)S(1)}, u32[]{:S(2)}, u32[]{:S(2)}) collective-permute-start(bf16[16,3072]{1,0:T(8,128)(2,1)S(1)} %fusion.34), channel_id=1, source_target_pairs={{0,4},{4,0},{1,5},{5,1},{2,6},{6,2},{3,7},{7,3},{8,12},{12,8},{9,1... | collective-permute-start | bytes 294920 | tf_op jit(solution)/shard_map/ppermute | solution.py:75
  21.0 48.7 %all-to-all-start = ((bf16[16,2,16,3072]{3,2,1,0:T(8,128)(2,1)}), bf16[16,2,16,3072]{3,2,1,0:T(8,128)(2,1)}, u32[]{:S(2)}, u32[]{:S(2)}) async-start(bf16[16,2,16,3072]{3,2,1,0:T(8,128)(2,1)} %broadcast_in_dim.123), calls=%async_computation | async-start | bytes 6291456 | tf_op jit(solution)/shard_map/all_to_all | solution.py:78
  69.7 4.0 %copy-start.11 = (bf16[3072,288]{0,1:T(8,128)(2,1)S(1)}, bf16[3072,288]{0,1:T(8,128)(2,1)}, u32[]{:S(2)}) copy-start(bf16[3072,288]{0,1:T(8,128)(2,1)} %param.18) | copy-start | bytes 5308420
  72.1 1.7 copy-start.2
  73.8 9.4 %copy-start.9 = (f32[128]{0:T(128)S(1)}, f32[128]{0:T(128)}, u32[]{:S(2)}) copy-start(f32[128]{0:T(128)} %param.20) | copy-start | bytes 1540
  73.8 9.5 %copy-start.8 = (s32[4096,3]{0,1:T(4,128)S(1)}, s32[4096,3]{0,1:T(4,128)}, u32[]{:S(2)}) copy-start(s32[4096,3]{0,1:T(4,128)} %param.14) | copy-start | bytes 147460
  74.9 12.7 %copy-start.10 = (f32[128]{0:T(128)S(1)}, f32[128]{0:T(128)}, u32[]{:S(2)}) copy-start(f32[128]{0:T(128)} %param.21) | copy-start | bytes 1540
  75.8 21.6 %all-to-all-start.1 = ((bf16[32,16,288]{2,1,0:T(8,128)(2,1)}), bf16[32,16,288]{2,1,0:T(8,128)(2,1)S(1)}, u32[]{:S(2)}, u32[]{:S(2)}) async-start(bf16[32,16,288]{2,1,0:T(8,128)(2,1)} %bitcast.11), calls=%async_computation.1 | async-start | bytes 786432 | tf_op jit(solution)/shard_map/all_to_all | solution.py:154
  98.8 19.6 %all-to-all-start.2 = ((bf16[16,8,1152]{2,0,1:T(8,128)(2,1)}), bf16[16,8,1152]{2,0,1:T(8,128)(2,1)S(1)}, u32[]{:S(2)}, u32[]{:S(2)}) async-start(bf16[16,8,1152]{2,0,1:T(8,128)(2,1)} %copy.102), calls=%async_computation.2 | async-start | bytes 589824 | tf_op jit(solution)/shard_map/all_to_all | solution.py:153
  121.2 12.1 %collective-permute-start.1 = (bf16[128,768]{0,1:T(8,128)(2,1)S(1)}, bf16[128,768]{0,1:T(8,128)(2,1)S(1)}, u32[]{:S(2)}, u32[]{:S(2)}) collective-permute-start(bf16[128,768]{0,1:T(8,128)(2,1)S(1)} %pad_maximum_fusion.2), channel_id=1, source_target_pairs={{0,4},{4,0},{1,5},{5,1},{2,6},{6,2},{3,7},{7,3},{8,12},{12,8},{9,1... | collective-permute-start | bytes 589832 | tf_op jit(solution)/shard_map/ppermute | solution.py:75
  137.1 91.5 %all-to-all-start.3 = ((bf16[16,2,128,768]{3,2,1,0:T(8,128)(2,1)}), bf16[16,2,128,768]{3,2,1,0:T(8,128)(2,1)}, u32[]{:S(2)}, u32[]{:S(2)}) async-start(bf16[16,2,128,768]{3,2,1,0:T(8,128)(2,1)} %broadcast_in_dim.124), calls=%async_computation.3 | async-start | bytes 12582912 | tf_op jit(solution)/shard_map/all_to_all | solution.py:78
  141.9 0.7 copy-start.1
  142.6 26.7 %copy-start.6 = (bf16[128,3,64,1]{0,3,2,1:T(2,128)(2,1)S(1)}, bf16[128,3,64,1]{0,3,2,1:T(2,128)(2,1)}, u32[]{:S(2)}) copy-start(bf16[128,3,64,1]{0,3,2,1:T(2,128)(2,1)} %get-tuple-element.12) | copy-start | bytes 147460
  142.6 26.7 %copy-start.7 = (bf16[128,3,64,1]{0,3,2,1:T(2,128)(2,1)S(1)}, bf16[128,3,64,1]{0,3,2,1:T(2,128)(2,1)}, u32[]{:S(2)}) copy-start(bf16[128,3,64,1]{0,3,2,1:T(2,128)(2,1)} %get-tuple-element.13) | copy-start | bytes 147460
  248.3 1.9 copy-start.3
  350.1 12.4 %collective-permute-start.2 = (f32[16,3072]{1,0:T(8,128)S(1)}, f32[16,3072]{1,0:T(8,128)S(1)}, u32[]{:S(2)}, u32[]{:S(2)}) collective-permute-start(f32[16,3072]{1,0:T(8,128)S(1)} %select_bitcast_fusion), channel_id=1, source_target_pairs={{0,4},{4,0},{1,5},{5,1},{2,6},{6,2},{3,7},{7,3},{8,12},{12,8},{9,1... | collective-permute-start | bytes 589832 | tf_op jit(solution)/shard_map/ppermute | solution.py:91

commit v3 on v2

--- a/solution.py
+++ b/solution.py
@@ -71,20 +71,17 @@
     return jnp.where(first, mine, other), jnp.where(first, other, mine)
 
 
-def gather_blk(x):
+def gather_plane(x):
     low, high = by_half(x, lax.ppermute(x, "zh", SWAP))
     pair = jnp.stack([low, high])
     plane = lax.axis_size("y") * lax.axis_size("x")
     got = lax.all_to_all(jnp.broadcast_to(pair[None], (plane,) + pair.shape), PLANE, 0, 0, tiled=True)
-    got = got.reshape((lax.axis_size("y"), lax.axis_size("x"), 2) + x.shape)
-    return jnp.swapaxes(got, 1, 2).reshape((-1,) + x.shape[1:])
+    return got.reshape((lax.axis_size("y"), lax.axis_size("x"), 2) + x.shape)
 
 
 def reduce_blk(y):
-    ys, xs = lax.axis_size("y"), lax.axis_size("x")
-    rows = y.shape[0] // (ys * 2 * xs)
-    pieces = jnp.swapaxes(y.reshape((ys, 2, xs, rows) + y.shape[1:]), 1, 2)
-    pieces = pieces.reshape((ys * xs, 2, rows) + y.shape[1:])
+    plane = lax.axis_size("y") * lax.axis_size("x")
+    pieces = y.reshape((plane, 2, y.shape[0] // (plane * 2)) + y.shape[1:])
     got = lax.all_to_all(pieces, PLANE, 0, 0, tiled=True)
     part = jnp.sum(got.astype(jnp.float32), axis=0)
     mine, theirs = by_half(part[0], part[1])
@@ -142,7 +139,7 @@
     normed = centered * lax.rsqrt(row_var + 1e-06)
     modin = ((1.0 + mod_scale) * normed + mod_shift).astype(jnp.bfloat16)
     qkv_width = w_qkv.shape[1]
-    shard_rows = gather_blk(modin)
+    shard_rows = gather_plane(modin).reshape(blk_count * block_rows, width)
     qkv_part = jnp.dot(shard_rows, w_qkv, preferred_element_type=jnp.float32).astype(jnp.bfloat16)
     mlp_part = jax.nn.gelu(
         jnp.dot(shard_rows, w_mlp_in, preferred_element_type=jnp.float32), approximate=True
@@ -150,13 +147,10 @@
     joined = jnp.concatenate([qkv_part, mlp_part], axis=1)
     qkv_cols = joined[:, :qkv_width]
     mlp_act = joined[:, qkv_width:]
-    heads_in = lax.all_to_all(
-        lax.all_to_all(qkv_cols, BLK, split_axis=0, concat_axis=1, tiled=True),
-        SEQ,
-        split_axis=1,
-        concat_axis=0,
-        tiled=True,
-    )
+    ys, xs = lax.axis_size("y"), lax.axis_size("x")
+    by_token = lax.all_to_all(qkv_cols, ("y", "x", "zh"), split_axis=0, concat_axis=1, tiled=True)
+    by_token = by_token.reshape(block_rows, ys, xs, 2, -1).swapaxes(2, 3).reshape(block_rows, -1)
+    heads_in = lax.all_to_all(by_token, SEQ, split_axis=1, concat_axis=0, tiled=True)
     query_rows = heads_in.shape[0]
     heads4 = heads_in.reshape(query_rows, local_heads, 3, head_size)
     query_ids = spread_rows(
@@ -166,7 +160,10 @@
         tok_seq,
     )
     query_request = segment_of(query_ids, request_ends)
-    angles = angles_of(jnp.take(positions, query_ids, axis=0), rope_table(head_size))
+    query_places = lax.dynamic_index_in_dim(
+        positions.reshape(seq_count, blk_count, block_rows, -1), blk_at, axis=1, keepdims=False
+    ).reshape(query_rows, -1)
+    angles = angles_of(query_places, rope_table(head_size))
     query_rot = rotate(rms_scale(heads4[:, :, 0].astype(jnp.float32), q_gain), angles).astype(
         jnp.bfloat16
     )
@@ -178,21 +175,21 @@
     kv_rows = jnp.concatenate(
         [key_rot.reshape(query_rows, -1), value_rows.reshape(query_rows, -1)], axis=1
     )
-    kv_all = gather_blk(kv_rows)
-    kv_half = kv_all.shape[1] // 2
-    key_part = kv_all[:, :kv_half].reshape(-1, local_heads, head_size)
-    value_part = kv_all[:, kv_half:].reshape(-1, local_heads, head_size)
+    kv_all = gather_plane(kv_rows).reshape(ys, xs, 2, query_rows, 2 * local_heads, head_size)
+    kv_all = kv_all.transpose(4, 0, 2, 1, 3, 5).reshape(2 * local_heads, -1, head_size)
+    key_part = kv_all[:local_heads]
+    value_part = kv_all[local_heads:]
     key_ids = spread_rows(
-        jnp.arange(key_part.shape[0], dtype=jnp.int32), query_rows, block_rows, tok_seq
+        jnp.arange(key_part.shape[1], dtype=jnp.int32), query_rows, block_rows, tok_seq
     )
     key_request = segment_of(key_ids, request_ends)
-    kept = jnp.take(key_keep, key_ids) == 1
+    kept = key_keep.reshape(seq_count, blk_count, block_rows).swapaxes(0, 1).reshape(-1) == 1
     visible = (
         (query_request[:, None] == key_request[None, :])
         & (kept[None, :] | (query_ids[:, None] == key_ids[None, :]))
     )[:, None, :]
     scores = (
-        jnp.einsum("qhd,khd->qhk", query_rot, key_part, preferred_element_type=jnp.float32)
+        jnp.einsum("qhd,hkd->qhk", query_rot, key_part, preferred_element_type=jnp.float32)
         * inv_root
     )
     row_high = jnp.max(jnp.where(visible, scores, -1e30), axis=2)
@@ -200,23 +197,20 @@
     weights = jnp.where(visible, jnp.exp(scores - new_top[:, :, None]), 0.0)
     run_norm = jnp.sum(weights, axis=2)
     run_sum = jnp.einsum(
-        "qhk,khd->qhd", weights.astype(jnp.bfloat16), value_part, preferred_element_type=jnp.float32
+        "qhk,hkd->qhd", weights.astype(jnp.bfloat16), value_part, preferred_element_type=jnp.float32
     )
     run_top, run_norm, run_sum = (new_top, run_norm, run_sum)
     attended = (run_sum / run_norm[:, :, None]).astype(jnp.bfloat16)
     attended = attended.reshape(query_rows, local_heads * head_size)
-    attn_local = lax.all_to_all(
-        lax.all_to_all(attended, SEQ, split_axis=0, concat_axis=1, tiled=True),
-        BLK,
-        split_axis=1,
-        concat_axis=0,
-        tiled=True,
-    )
-    mlp_part = mlp_act
-    partial = (
-        jnp.dot(attn_local, w_attn_out, preferred_element_type=jnp.float32)
-        + jnp.dot(mlp_part, w_mlp_out, preferred_element_type=jnp.float32)
-    ).astype(jnp.bfloat16)
+    attn_feats = lax.all_to_all(attended, SEQ, split_axis=0, concat_axis=1, tiled=True)
+    attn_feats = attn_feats.reshape(block_rows, ys, 2, xs, -1).swapaxes(2, 3).reshape(block_rows, -1)
+    attn_local = lax.all_to_all(attn_feats, ("y", "x", "zh"), split_axis=1, concat_axis=0, tiled=True)
+    mlp_out = lax.optimization_barrier(
+        jnp.dot(mlp_act, w_mlp_out, preferred_element_type=jnp.float32)
+    )
+    partial = (jnp.dot(attn_local, w_attn_out, preferred_element_type=jnp.float32) + mlp_out).astype(
+        jnp.bfloat16
+    )
     summed = reduce_blk(partial)
     return stream + mod_gate * summed
 

time: 365 us -> 366 us (level)
  blocking collectives: 80.5 us -> 107 us
  waiting for transfers between devices: 145 us -> 128 us
  local copies, waits for them, and re-layouts: 61.3 us -> 46.3 us
  other arithmetic: 13.8 us -> 21 us
  starting transfers between devices: 39.5 us -> 35.1 us
    all_to_all x1, blocking collectives: 18.4 us -> 44.8 us  [gather_plane(): lax.all_to_all(jnp.broadcast_to(pair[None], (plane,) + pair.shape), PLANE...]
    gather x3 -> x0, local copies, waits for them, and re-layouts: 25.3 us -> none  [the longest x1 23 us: body(): kept = jnp.take(key_keep, key_ids) == 1]
    all_to_all x4, waiting for transfers between devices: 118 us -> 106 us  [the longest x1 80.9 us: gather_plane(): lax.all_to_all(jnp.broadcast_to(pair[None], (plane,) + pair.shape), PLANE...]
    slice x3 -> x4, local copies, waits for them, and re-layouts: 12.9 us -> 23.1 us  [the longest x2 12.8 us: body(): key_part = kv_all[:local_heads]]
    all_to_all x4, starting transfers between devices: 30.5 us -> 22.6 us  [the longest x1 7.77 us: body(): lax.all_to_all(qkv_cols, ('y', 'x', 'zh'), split_axis=0, concat_axis=1, t...]
    transpose x2 -> x0, local copies, waits for them, and re-layouts: 5.53 us -> none  [gather_blk(): return jnp.swapaxes(got, 1, 2).reshape((-1,) + x.shape[1:])]
    ppermute x1, waiting for transfers between devices: 11.7 us -> 7.83 us  [reduce_blk(): return mine + lax.ppermute(theirs, 'zh', SWAP)]
  transfers between devices with their start and end apart: 7 -> 7, of which waited for: 7 -> 7; matrix products, arithmetic and copies ran while one was open for 9% -> 5% of each run, Pallas kernels for 0% -> 0%
where the time goes in v3:
time: 366 us; the launch traced here: 365 us
  waiting for transfers between devices  128 us (35%)
  blocking collectives  107 us (29%)
  local copies, waits for them, and re-layouts  46.3 us (13%)
  starting transfers between devices  35.1 us (10%)
  matrix products  26.7 us (7%)
  other arithmetic  21 us (6%)
    all_to_all x1, waiting for transfers between devices, gather_plane(): lax.all_to_all(jnp.broadcast_to(pair[None], (plane,) + pair.shape), PLANE...  80.9 us
    all_to_all x1, blocking collectives, gather_plane(): lax.all_to_all(jnp.broadcast_to(pair[None], (plane,) + pair.shape), PLANE...  44.8 us
    all_to_all x1, blocking collectives, reduce_blk(): got = lax.all_to_all(pieces, PLANE, 0, 0, tiled=True)  42.6 us
    all_to_all x1, blocking collectives, body(): lax.all_to_all(attended, SEQ, split_axis=0, concat_axis=1, tiled=True)  19.6 us
    ppermute x2, waiting for transfers between devices, gather_plane(): low, high = by_half(x, lax.ppermute(x, 'zh', SWAP))  14.8 us
    all_to_all x1, waiting for transfers between devices, body(): lax.all_to_all(qkv_cols, ('y', 'x', 'zh'), split_axis=0, concat_axis=1, t...  13.3 us
    slice x2, local copies, waits for them, and re-layouts, body(): key_part = kv_all[:local_heads]  12.8 us
    slice x2, local copies, waits for them, and re-layouts, body(): value_part = kv_all[local_heads:]  10.3 us
  transfers between devices with their start and end apart: 7, of which 7 were waited for; matrix products, arithmetic and copies ran while one was open for 5% of the time, Pallas kernels for 0%

profile of v3, /device:TPU:32, one launch (start us, length us, event | category | flops | bytes accessed | tf_op | source)
XLA Modules:
  0.0 364.9 jit_solution(1382355680616182964)
XLA Ops:
  0.0 0.9 fusion.61
  0.9 1.1 reduce_sum.92
  2.0 1.1 multiply_reduce_fusion.2
  3.1 0.8 reduce-window.8
  4.0 0.5 copy-done.12
  4.5 2.8 fusion.10
  7.3 0.4 fusion.38
  7.9 6.4 %collective-permute-start = (bf16[16,3072]{1,0:T(8,128)(2,1)S(1)}, bf16[16,3072]{1,0:T(8,128)(2,1)S(1)}, u32[]{:S(2)}, u32[]{:S(2)}) collective-permute-start(bf16[16,3072]{1,0:T(8,128)(2,1)S(1)} %fusion.35), channel_id=1, source_target_pairs={{0,4},{4,0},{1,5},{5,1},{2,6},{6,2},{3,7},{7,3},{8,12},{12,8},{9,1... | collective-permute-start | bytes 294920 | tf_op jit(solution)/shard_map/ppermute | solution.py:75
  14.3 4.3 %collective-permute-done = bf16[16,3072]{1,0:T(8,128)(2,1)S(1)} collective-permute-done((bf16[16,3072]{1,0:T(8,128)(2,1)S(1)}, bf16[16,3072]{1,0:T(8,128)(2,1)S(1)}, u32[]{:S(2)}, u32[]{:S(2)}) %collective-permute-start) | collective-permute-done | bytes 98336 | tf_op jit(solution)/shard_map/ppermute | solution.py:75
  18.6 0.4 broadcast_in_dim.59
  19.0 44.8 %all_to_all.82 = bf16[16,2,16,3072]{3,2,1,0:T(8,128)(2,1)S(1)} all-to-all(bf16[16,2,16,3072]{3,2,1,0:T(8,128)(2,1)S(1)} %broadcast_in_dim.59), channel_id=1, replica_groups=mesh['zl'=4,'core'=2,'y'=4,'zh'=2,'x'=4] {'y','x'}, dimensions={0} | all-to-all | bytes 6291456 | tf_op jit(solution)/shard_map/all_to_all | solution.py:78
  63.8 1.7 copy-done.3
  65.5 1.1 convolution_convert_fusion
  66.6 0.9 copy.65
  67.5 7.8 %all-to-all-start.1 = ((bf16[32,16,288]{2,1,0:T(8,128)(2,1)}), bf16[32,16,288]{2,1,0:T(8,128)(2,1)S(1)}, u32[]{:S(2)}, u32[]{:S(2)}) async-start(bf16[32,16,288]{2,1,0:T(8,128)(2,1)} %bitcast.99), calls=%async_computation.1 | async-start | bytes 786432 | tf_op jit(solution)/shard_map/all_to_all | solution.py:151
  75.3 0.7 mul.259
  76.0 0.7 mul.277
  76.8 1.8 reshape.442
  78.5 0.9 convert_reduce_fusion.2
  79.6 13.3 %all-to-all-done.1 = bf16[32,16,288]{2,1,0:T(8,128)(2,1)S(1)} async-done(((bf16[32,16,288]{2,1,0:T(8,128)(2,1)}), bf16[32,16,288]{2,1,0:T(8,128)(2,1)S(1)}, u32[]{:S(2)}, u32[]{:S(2)}) %all-to-all-start.1) | async-done | bytes 294944 | tf_op jit(solution)/shard_map/all_to_all | solution.py:151
  92.9 0.9 copy.108
  93.8 1.3 all_to_all.63
  95.1 0.7 copy.67
  95.9 4.0 %all-to-all-start.2 = ((bf16[16,8,1152]{2,0,1:T(8,128)(2,1)}), bf16[16,8,1152]{2,0,1:T(8,128)(2,1)S(1)}, u32[]{:S(2)}, u32[]{:S(2)}) async-start(bf16[16,8,1152]{2,0,1:T(8,128)(2,1)} %copy.67), calls=%async_computation.2 | async-start | bytes 589824 | tf_op jit(solution)/shard_map/all_to_all | solution.py:153
  99.9 0.7 fusion.77
  100.7 7.4 %all-to-all-done.2 = bf16[16,8,1152]{2,0,1:T(8,128)(2,1)S(1)} async-done(((bf16[16,8,1152]{2,0,1:T(8,128)(2,1)}), bf16[16,8,1152]{2,0,1:T(8,128)(2,1)S(1)}, u32[]{:S(2)}, u32[]{:S(2)}) %all-to-all-start.2) | async-done | bytes 294944 | tf_op jit(solution)/shard_map/all_to_all | solution.py:153
  108.1 0.7 copy-done.6
  108.8 1.0 reshape.444
  109.9 1.1 fusion.76
  111.0 0.2 multiply_reduce_fusion
  111.2 0.8 copy_convert_fusion
  111.9 1.1 copy.69
  113.0 1.7 copy.77
  114.7 1.1 copy.72
  115.8 0.9 multiply_multiply_fusion.2
  116.7 1.1 multiply_multiply_fusion.1
  117.8 2.0 subtract_convert_fusion
  119.7 0.2 pad_maximum_fusion.3
  120.0 1.7 collective-permute-start.1
  121.7 10.5 %collective-permute-done.1 = bf16[128,768]{0,1:T(8,128)(2,1)S(1)} collective-permute-done((bf16[128,768]{0,1:T(8,128)(2,1)S(1)}, bf16[128,768]{0,1:T(8,128)(2,1)S(1)}, u32[]{:S(2)}, u32[]{:S(2)}) %collective-permute-start.1) | collective-permute-done | bytes 196640 | tf_op jit(solution)/shard_map/ppermute | solution.py:75
  132.4 4.1 %broadcast_in_dim.60 = bf16[16,2,128,768]{2,3,1,0:T(8,128)(2,1)} broadcast(bf16[2,128,768]{1,2,0:T(8,128)(2,1)S(1)} %pad_maximum_fusion), dimensions={1,2,3} | broadcast | bytes 6684672 | tf_op jit(solution)/shard_map/broadcast_in_dim | solution.py:78
  136.5 5.0 %all-to-all-start.3 = ((bf16[16,2,128,768]{2,3,1,0:T(8,128)(2,1)}), bf16[16,2,128,768]{2,3,1,0:T(8,128)(2,1)}, u32[]{:S(2)}, u32[]{:S(2)}) async-start(bf16[16,2,128,768]{2,3,1,0:T(8,128)(2,1)} %broadcast_in_dim.60), calls=%async_computation.3 | async-start | bytes 12582912 | tf_op jit(solution)/shard_map/all_to_all | solution.py:78
  142.0 4.5 %or_and_fusion = pred[128,4096]{0,1:T(8,128)(4,1)} fusion(s32[128]{0:T(128)S(1)} %fusion.63, s32[128]{0:T(128)S(1)} %convert_reduce_fusion.3, s32[4096]{0:T(1024)S(1)} %fusion.49, s32[4096]{0:T(1024)S(1)} %convert_reduce_fusion.1, pred[4096]{0:T(1024)(128)(4,1)S(1)} %eq.130), kind=kLoop, calls=%fused_computation.16 | loop fusion | flops 2097152 | bytes 562176 | tf_op jit(solution)/shard_map/and | solution.py:188
  146.5 0.2 pad_maximum_fusion.4
  146.8 80.9 %all-to-all-done.3 = bf16[16,2,128,768]{2,3,1,0:T(8,128)(2,1)} async-done(((bf16[16,2,128,768]{2,3,1,0:T(8,128)(2,1)}), bf16[16,2,128,768]{2,3,1,0:T(8,128)(2,1)}, u32[]{:S(2)}, u32[]{:S(2)}) %all-to-all-start.3) | async-done | bytes 6291488 | tf_op jit(solution)/shard_map/all_to_all | solution.py:78
  227.6 8.2 %fusion.75 = (bf16[3,4,2,4,128,128]{4,5,0,2,3,1:T(8,128)(2,1)}, bf16[3,4,2,4,128,128]{4,5,0,2,3,1:T(8,128)(2,1)}) fusion(bf16[6,4,2,4,128,128]{4,5,0,2,3,1:T(8,128)(2,1)} %bitcast.19), kind=kLoop, calls=%fused_computation.142 | loop fusion | bytes 12582912 | tf_op jit(solution)/shard_map/slice | solution.py:180
  235.8 4.7 %copy.75 = bf16[3,4,2,4,128,128]{5,4,3,2,1,0:T(8,128)(2,1)} copy(bf16[3,4,2,4,128,128]{4,5,0,2,3,1:T(8,128)(2,1)} %get-tuple-element.5) | data formatting | bytes 6291456 | tf_op jit(solution)/shard_map/slice | solution.py:180
  240.5 5.9 %fusion = (f32[128,3]{0,1:T(4,128)S(1)}, f32[3,4096,128]{2,1,0:T(8,128)}) fusion(pred[128,4096]{0,1:T(8,128)(4,1)} %or_and_fusion, bf16[3,4096,128]{2,1,0:T(8,128)(2,1)} %bitcast.96, bf16[128,3,128]{0,2,1:T(8,128)(2,1)S(1)} %bitcast.111), kind=kOutput, calls=%fused_computation.2 | convolution fusion | flops 407371392 | bytes 10061312 | tf_op jit(solution)/shard_map/qhd,hkd->qhk/dot_general | solution.py:192
  246.4 4.1 %copy.73 = bf16[3,4,2,4,128,128]{4,3,2,1,5,0:T(4,128)(2,1)} copy(bf16[3,4,2,4,128,128]{4,5,0,2,3,1:T(8,128)(2,1)S(1)} %copy-done.1) | data formatting | bytes 6291456 | tf_op jit(solution)/shard_map/slice | solution.py:181
  250.4 6.2 %slice.56 = bf16[3,4096,128]{1,2,0:T(8,128)(2,1)} reshape(bf16[3,4,2,4,128,128]{4,3,2,1,5,0:T(4,128)(2,1)} %copy.73) | data formatting | bytes 6291456 | tf_op jit(solution)/shard_map/slice | solution.py:181
  256.7 4.2 %fusion.3 = f32[128,3]{0,1:T(4,128)S(1)} fusion(f32[3,4096,128]{2,1,0:T(8,128)} %get-tuple-element.23, f32[128,3]{0,1:T(4,128)S(1)} %broadcast_maximum_fusion, pred[128,4096]{0,1:T(8,128)(4,1)} %or_and_fusion), kind=kLoop, calls=%fused_computation.8 | loop fusion | flops 4718208 | bytes 6818816 | tf_op jit(solution)/shard_map/reduce_sum | solution.py:198
  260.8 0.6 copy-done.2
  261.5 3.7 %fusion.18 = bf16[128,3,128]{0,2,1:T(8,128)(2,1)S(1)} fusion(bf16[3,4096,128]{1,2,0:T(8,128)(2,1)} %slice.56, f32[3,4096,128]{2,1,0:T(8,128)S(1)} %copy-done.2, f32[128,3]{0,1:T(4,128)S(1)} %broadcast_maximum_fusion, pred[128,4096]{0,1:T(8,128)(4,1)S(1)} %copy-done.5, f32[128,3]{0,1:T(4,128)S(1)} %fusion.3), kind=kOutput, calls=%fused_computation.21 | convolution fusion | flops 407470080 | bytes 10062848 | tf_op jit(solution)/shard_map/qhk,hkd->qhd/dot_general | solution.py:199
  265.4 19.6 %all_to_all.83 = bf16[8,16,384]{2,1,0:T(8,128)(2,1)S(1)} all-to-all(bf16[8,16,384]{2,1,0:T(8,128)(2,1)S(1)} %all_to_all.67), channel_id=1, replica_groups=mesh['zl'=4,'core'=2,'y'=4,'zh'=2,'x'=4] {'zl','core'}, dimensions={0} | all-to-all | bytes 196608 | tf_op jit(solution)/shard_map/all_to_all | solution.py:205
  285.1 0.7 copy.83
  285.8 5.9 %all-to-all-start.5 = ((bf16[16,32,96]{2,0,1:T(8,128)(2,1)}), bf16[16,32,96]{2,0,1:T(8,128)(2,1)S(1)}, u32[]{:S(2)}, u32[]{:S(2)}) async-start(bf16[16,32,96]{2,0,1:T(8,128)(2,1)} %bitcast.29), calls=%async_computation.5 | async-start | bytes 262144 | tf_op jit(solution)/shard_map/all_to_all | solution.py:207
  291.7 8.8 %fusion.29 = f32[512,3072]{1,0:T(8,128)} fusion(bf16[384,3072]{1,0:T(8,128)(2,1)S(1)} %copy-done, bf16[512,3072]{1,0:T(8,128)(2,1)} %bitcast.95, bf16[3072,384]{1,0:T(8,128)(2,1)} %param.19), kind=kOutput, calls=%fused_computation.30 | convolution fusion | flops 2417688576 | bytes 14155776 | tf_op jit(solution)/shard_map/dot_general | solution.py:209
  300.5 4.3 %all-to-all-done.5 = bf16[16,32,96]{2,0,1:T(8,128)(2,1)S(1)} async-done(((bf16[16,32,96]{2,0,1:T(8,128)(2,1)}), bf16[16,32,96]{2,0,1:T(8,128)(2,1)S(1)}, u32[]{:S(2)}, u32[]{:S(2)}) %all-to-all-start.5) | async-done | bytes 98336 | tf_op jit(solution)/shard_map/all_to_all | solution.py:207
  304.8 4.0 %add_convert_fusion = bf16[512,3072]{1,0:T(8,128)(2,1)S(1)} fusion(f32[512,3072]{1,0:T(8,128)} %fusion.29, bf16[512,96]{1,0:T(8,128)(2,1)S(1)} %bitcast.108, bf16[96,3072]{1,0:T(8,128)(2,1)} %param.22), kind=kOutput, calls=%fused_computation.6 | convolution fusion | flops 305135616 | bytes 10125312 | tf_op jit(solution)/shard_map/dot_general | solution.py:211
  308.8 42.6 %all_to_all.84 = bf16[16,2,16,3072]{3,2,1,0:T(8,128)(2,1)S(1)} all-to-all(bf16[16,2,16,3072]{3,2,1,0:T(8,128)(2,1)S(1)} %bitcast.93), channel_id=1, replica_groups=mesh['zl'=4,'core'=2,'y'=4,'zh'=2,'x'=4] {'y','x'}, dimensions={0} | all-to-all | bytes 6291456 | tf_op jit(solution)/shard_map/all_to_all | solution.py:85
  351.4 0.6 convert_reduce_fusion
  352.0 4.4 %collective-permute-start.2 = (f32[16,3072]{1,0:T(8,128)S(1)}, f32[16,3072]{1,0:T(8,128)S(1)}, u32[]{:S(2)}, u32[]{:S(2)}) collective-permute-start(f32[16,3072]{1,0:T(8,128)S(1)} %select_bitcast_fusion), channel_id=1, source_target_pairs={{0,4},{4,0},{1,5},{5,1},{2,6},{6,2},{3,7},{7,3},{8,12},{12,8},{9,1... | collective-permute-start | bytes 589832 | tf_op jit(solution)/shard_map/ppermute | solution.py:88
  356.4 7.8 %collective-permute-done.2 = f32[16,3072]{1,0:T(8,128)S(1)} collective-permute-done((f32[16,3072]{1,0:T(8,128)S(1)}, f32[16,3072]{1,0:T(8,128)S(1)}, u32[]{:S(2)}, u32[]{:S(2)}) %collective-permute-start.2) | collective-permute-done | bytes 196640 | tf_op jit(solution)/shard_map/ppermute | solution.py:88
  364.2 0.7 fusion.37
  (56 shorter events, 1.6 us)
Async XLA Ops:
  0.0 291.7 %copy-start = (bf16[384,3072]{1,0:T(8,128)(2,1)S(1)}, bf16[384,3072]{1,0:T(8,128)(2,1)}, u32[]{:S(2)}) copy-start(bf16[384,3072]{1,0:T(8,128)(2,1)} %param.23) | copy-start | bytes 7077892
  0.0 7.8 %copy-start.4 = (f32[16,3072]{1,0:T(8,128)S(1)}, f32[16,3072]{1,0:T(8,128)}, u32[]{:S(2)}) copy-start(f32[16,3072]{1,0:T(8,128)} %param.12) | copy-start | bytes 589828
  4.0 0.6 copy-start.12
  7.9 10.6 %collective-permute-start = (bf16[16,3072]{1,0:T(8,128)(2,1)S(1)}, bf16[16,3072]{1,0:T(8,128)(2,1)S(1)}, u32[]{:S(2)}, u32[]{:S(2)}) collective-permute-start(bf16[16,3072]{1,0:T(8,128)(2,1)S(1)} %fusion.35), channel_id=1, source_target_pairs={{0,4},{4,0},{1,5},{5,1},{2,6},{6,2},{3,7},{7,3},{8,12},{12,8},{9,1... | collective-permute-start | bytes 294920 | tf_op jit(solution)/shard_map/ppermute | solution.py:75
  19.0 46.5 %copy-start.14 = (bf16[3072,288]{0,1:T(8,128)(2,1)S(1)}, bf16[3072,288]{0,1:T(8,128)(2,1)}, u32[]{:S(2)}) copy-start(bf16[3072,288]{0,1:T(8,128)(2,1)} %param.18) | copy-start | bytes 5308420
  63.8 1.7 copy-start.3
  65.5 9.8 %copy-start.10 = (f32[128]{0:T(128)S(1)}, f32[128]{0:T(128)}, u32[]{:S(2)}) copy-start(f32[128]{0:T(128)} %param.21) | copy-start | bytes 1540
  65.5 10.6 %copy-start.11 = (f32[128]{0:T(128)S(1)}, f32[128]{0:T(128)}, u32[]{:S(2)}) copy-start(f32[128]{0:T(128)} %param.20) | copy-start | bytes 1540
  67.5 25.3 %all-to-all-start.1 = ((bf16[32,16,288]{2,1,0:T(8,128)(2,1)}), bf16[32,16,288]{2,1,0:T(8,128)(2,1)S(1)}, u32[]{:S(2)}, u32[]{:S(2)}) async-start(bf16[32,16,288]{2,1,0:T(8,128)(2,1)} %bitcast.99), calls=%async_computation.1 | async-start | bytes 786432 | tf_op jit(solution)/shard_map/all_to_all | solution.py:151
  95.9 12.3 %all-to-all-start.2 = ((bf16[16,8,1152]{2,0,1:T(8,128)(2,1)}), bf16[16,8,1152]{2,0,1:T(8,128)(2,1)S(1)}, u32[]{:S(2)}, u32[]{:S(2)}) async-start(bf16[16,8,1152]{2,0,1:T(8,128)(2,1)} %copy.67), calls=%async_computation.2 | async-start | bytes 589824 | tf_op jit(solution)/shard_map/all_to_all | solution.py:153
  108.1 0.7 copy-start.6
  120.0 12.3 %collective-permute-start.1 = (bf16[128,768]{0,1:T(8,128)(2,1)S(1)}, bf16[128,768]{0,1:T(8,128)(2,1)S(1)}, u32[]{:S(2)}, u32[]{:S(2)}) collective-permute-start(bf16[128,768]{0,1:T(8,128)(2,1)S(1)} %pad_maximum_fusion.2), channel_id=1, source_target_pairs={{0,4},{4,0},{1,5},{5,1},{2,6},{6,2},{3,7},{7,3},{8,12},{12,8},{9,1... | collective-permute-start | bytes 589832 | tf_op jit(solution)/shard_map/ppermute | solution.py:75
  136.4 5.0 %copy-start.9 = (s32[4096]{0:T(1024)S(1)}, s32[4096]{0:T(1024)}, u32[]{:S(2)}) copy-start(s32[4096]{0:T(1024)} %param.13) | copy-start | bytes 49156
  136.4 5.3 %copy-start.13 = (s32[4,1]{0,1:T(1,128)S(1)}, s32[4,1]{0,1:T(1,128)}, u32[]{:S(2)}) copy-start(s32[4,1]{0,1:T(1,128)} %copy-done.12) | copy-start | bytes 52
  136.5 10.1 %copy-start.7 = (bf16[128,3,64,1]{0,3,2,1:T(2,128)(2,1)S(1)}, bf16[128,3,64,1]{0,3,2,1:T(2,128)(2,1)}, u32[]{:S(2)}) copy-start(bf16[128,3,64,1]{0,3,2,1:T(2,128)(2,1)} %get-tuple-element.12) | copy-start | bytes 147460
  136.5 10.1 %copy-start.8 = (bf16[128,3,64,1]{0,3,2,1:T(2,128)(2,1)S(1)}, bf16[128,3,64,1]{0,3,2,1:T(2,128)(2,1)}, u32[]{:S(2)}) copy-start(bf16[128,3,64,1]{0,3,2,1:T(2,128)(2,1)} %get-tuple-element.13) | copy-start | bytes 147460
  136.5 91.2 %all-to-all-start.3 = ((bf16[16,2,128,768]{2,3,1,0:T(8,128)(2,1)}), bf16[16,2,128,768]{2,3,1,0:T(8,128)(2,1)}, u32[]{:S(2)}, u32[]{:S(2)}) async-start(bf16[16,2,128,768]{2,3,1,0:T(8,128)(2,1)} %broadcast_in_dim.60), calls=%async_computation.3 | async-start | bytes 12582912 | tf_op jit(solution)/shard_map/all_to_all | solution.py:78
  240.4 5.9 %copy-start.1 = (bf16[3,4,2,4,128,128]{4,5,0,2,3,1:T(8,128)(2,1)S(1)}, bf16[3,4,2,4,128,128]{4,5,0,2,3,1:T(8,128)(2,1)}, u32[]{:S(2)}) copy-start(bf16[3,4,2,4,128,128]{4,5,0,2,3,1:T(8,128)(2,1)} %get-tuple-element.6) | copy-start | bytes 9437188
  256.7 4.7 %copy-start.2 = (f32[3,4096,128]{2,1,0:T(8,128)S(1)}, f32[3,4096,128]{2,1,0:T(8,128)}, u32[]{:S(2)}) copy-start(f32[3,4096,128]{2,1,0:T(8,128)} %get-tuple-element.23) | copy-start | bytes 18874372
  256.7 4.8 %copy-start.5 = (pred[128,4096]{0,1:T(8,128)(4,1)S(1)}, pred[128,4096]{0,1:T(8,128)(4,1)}, u32[]{:S(2)}) copy-start(pred[128,4096]{0,1:T(8,128)(4,1)} %or_and_fusion) | copy-start | bytes 1572868
  285.8 19.0 %all-to-all-start.5 = ((bf16[16,32,96]{2,0,1:T(8,128)(2,1)}), bf16[16,32,96]{2,0,1:T(8,128)(2,1)S(1)}, u32[]{:S(2)}, u32[]{:S(2)}) async-start(bf16[16,32,96]{2,0,1:T(8,128)(2,1)} %bitcast.29), calls=%async_computation.5 | async-start | bytes 262144 | tf_op jit(solution)/shard_map/all_to_all | solution.py:207
  352.0 12.2 %collective-permute-start.2 = (f32[16,3072]{1,0:T(8,128)S(1)}, f32[16,3072]{1,0:T(8,128)S(1)}, u32[]{:S(2)}, u32[]{:S(2)}) collective-permute-start(f32[16,3072]{1,0:T(8,128)S(1)} %select_bitcast_fusion), channel_id=1, source_target_pairs={{0,4},{4,0},{1,5},{5,1},{2,6},{6,2},{3,7},{7,3},{8,12},{12,8},{9,1... | collective-permute-start | bytes 589832 | tf_op jit(solution)/shard_map/ppermute | solution.py:88

commit v4 on v3

--- a/solution.py
+++ b/solution.py
@@ -171,36 +171,38 @@
         jnp.bfloat16
     )
     value_rows = heads4[:, :, 2]
-    run_top = jnp.full((query_rows, local_heads), -1e30, jnp.float32)
-    kv_rows = jnp.concatenate(
-        [key_rot.reshape(query_rows, -1), value_rows.reshape(query_rows, -1)], axis=1
-    )
-    kv_all = gather_plane(kv_rows).reshape(ys, xs, 2, query_rows, 2 * local_heads, head_size)
-    kv_all = kv_all.transpose(4, 0, 2, 1, 3, 5).reshape(2 * local_heads, -1, head_size)
-    key_part = kv_all[:local_heads]
-    value_part = kv_all[local_heads:]
-    key_ids = spread_rows(
-        jnp.arange(key_part.shape[1], dtype=jnp.int32), query_rows, block_rows, tok_seq
-    )
+    kv_rows = jnp.concatenate([key_rot, value_rows], axis=2)
+    low, high = by_half(kv_rows, lax.ppermute(kv_rows, "zh", SWAP))
+    kv_pair = jnp.stack([low, high])
+    key_rank = jnp.arange(seq_count * tok_seq, dtype=jnp.int32)
+    key_y = key_rank // (xs * 2 * query_rows)
+    key_x = key_rank // (2 * query_rows) % xs
+    key_zh = key_rank // query_rows % 2
+    key_owner = (key_y * 2 + key_zh) * xs + key_x
+    key_ids = key_rank // block_rows % seq_count * tok_seq + key_owner * block_rows + key_rank % block_rows
     key_request = segment_of(key_ids, request_ends)
-    kept = key_keep.reshape(seq_count, blk_count, block_rows).swapaxes(0, 1).reshape(-1) == 1
-    visible = (
-        (query_request[:, None] == key_request[None, :])
-        & (kept[None, :] | (query_ids[:, None] == key_ids[None, :]))
-    )[:, None, :]
-    scores = (
-        jnp.einsum("qhd,hkd->qhk", query_rot, key_part, preferred_element_type=jnp.float32)
-        * inv_root
-    )
-    row_high = jnp.max(jnp.where(visible, scores, -1e30), axis=2)
-    new_top = jnp.maximum(run_top, row_high)
-    weights = jnp.where(visible, jnp.exp(scores - new_top[:, :, None]), 0.0)
-    run_norm = jnp.sum(weights, axis=2)
-    run_sum = jnp.einsum(
-        "qhk,hkd->qhd", weights.astype(jnp.bfloat16), value_part, preferred_element_type=jnp.float32
-    )
-    run_top, run_norm, run_sum = (new_top, run_norm, run_sum)
-    attended = (run_sum / run_norm[:, :, None]).astype(jnp.bfloat16)
+    kept = key_keep.reshape(seq_count, ys, 2, xs, block_rows).transpose(1, 3, 2, 0, 4).reshape(-1) == 1
+    visible = (query_request[:, None] == key_request[None, :]) & (
+        kept[None, :] | (query_ids[:, None] == key_ids[None, :])
+    )
+    head_out = []
+    for head in range(local_heads):
+        piece = kv_pair[:, :, head]
+        got = lax.all_to_all(
+            jnp.broadcast_to(piece[None], (ys * xs,) + piece.shape), PLANE, 0, 0, tiled=True
+        ).reshape(-1, 2 * head_size)
+        key_h = got[:, :head_size]
+        value_h = got[:, head_size:]
+        scores = (
+            jnp.einsum("qd,kd->qk", query_rot[:, head], key_h, preferred_element_type=jnp.float32)
+            * inv_root
+        )
+        row_high = jnp.max(jnp.where(visible, scores, -1e30), axis=1)
+        weights = jnp.where(visible, jnp.exp(scores - row_high[:, None]), 0.0)
+        totals = jnp.sum(weights, axis=1)
+        mixed = jnp.dot(weights.astype(jnp.bfloat16), value_h, preferred_element_type=jnp.float32)
+        head_out.append((mixed / totals[:, None]).astype(jnp.bfloat16))
+    attended = jnp.stack(head_out, axis=1)
     attended = attended.reshape(query_rows, local_heads * head_size)
     attn_feats = lax.all_to_all(attended, SEQ, split_axis=0, concat_axis=1, tiled=True)
     attn_feats = attn_feats.reshape(block_rows, ys, 2, xs, -1).swapaxes(2, 3).reshape(block_rows, -1)

time: 366 us -> 350 us (0.956)
  local copies, waits for them, and re-layouts: 46.3 us -> 24.1 us
  matrix products: 26.7 us -> 34.8 us
  starting transfers between devices: 35.1 us -> 42.4 us
  other arithmetic: 21 us -> 14.5 us
  waiting for transfers between devices: 128 us -> 124 us
    slice x5 -> x3, local copies, waits for them, and re-layouts: 24.2 us -> 1.23 us  [body(): piece = kv_pair[:, :, head]]
    ppermute x0 -> x1, waiting for transfers between devices: none -> 10.5 us  [body(): low, high = by_half(kv_rows, lax.ppermute(kv_rows, 'zh', SWAP))]
    ppermute x2 -> x1, waiting for transfers between devices: 14.8 us -> 4.25 us  [gather_plane(): low, high = by_half(x, lax.ppermute(x, 'zh', SWAP))]
    all_to_all x1 -> x3, starting transfers between devices: 4.95 us -> 13.9 us  [body(): lax.all_to_all(jnp.broadcast_to(piece[None], (ys * xs,) + piece.shape), P...]
    dot_general x2 -> x6, matrix products: 9.58 us -> 17.7 us  [the longest x3 10.9 us: body(): jnp.einsum('qd,kd->qk', query_rot[:, head], key_h, preferred_element_type...]
    all_to_all x1 -> x3, waiting for transfers between devices: 80.9 us -> 75.5 us  [body(): lax.all_to_all(jnp.broadcast_to(piece[None], (ys * xs,) + piece.shape), P...]
    broadcast_in_dim x0 -> x3, local copies, waits for them, and re-layouts: none -> 4.65 us  [body(): jnp.broadcast_to(piece[None], (ys * xs,) + piece.shape)]
    and x1 -> x0, other arithmetic: 4.55 us -> none  [body(): (query_request[:, None] == key_request[None, :]) & (kept[None, :] | (quer...]
  transfers between devices with their start and end apart: 7 -> 9, of which waited for: 7 -> 9; matrix products, arithmetic and copies ran while one was open for 5% -> 6% of each run, Pallas kernels for 0% -> 0%
where the time goes in v4:
time: 350 us; the launch traced here: 349 us
  waiting for transfers between devices  124 us (35%)
  blocking collectives  109 us (31%)
  starting transfers between devices  42.4 us (12%)
  matrix products  34.8 us (10%)
  local copies, waits for them, and re-layouts  24.1 us (7%)
  other arithmetic  14.5 us (4%)
    all_to_all x3, waiting for transfers between devices, body(): lax.all_to_all(jnp.broadcast_to(piece[None], (ys * xs,) + piece.shape), P...  75.5 us
    all_to_all x1, blocking collectives, gather_plane(): lax.all_to_all(jnp.broadcast_to(pair[None], (plane,) + pair.shape), PLANE...  44.8 us
    all_to_all x1, blocking collectives, reduce_blk(): got = lax.all_to_all(pieces, PLANE, 0, 0, tiled=True)  42.1 us
    all_to_all x1, blocking collectives, body(): lax.all_to_all(attended, SEQ, split_axis=0, concat_axis=1, tiled=True)  22 us
    all_to_all x3, starting transfers between devices, body(): lax.all_to_all(jnp.broadcast_to(piece[None], (ys * xs,) + piece.shape), P...  13.9 us
    all_to_all x1, waiting for transfers between devices, body(): lax.all_to_all(qkv_cols, ('y', 'x', 'zh'), split_axis=0, concat_axis=1, t...  13.3 us
    dot_general x3, matrix products, body(): jnp.einsum('qd,kd->qk', query_rot[:, head], key_h, preferred_element_type...  10.9 us
    ppermute x1, waiting for transfers between devices, body(): low, high = by_half(kv_rows, lax.ppermute(kv_rows, 'zh', SWAP))  10.5 us
  transfers between devices with their start and end apart: 9, of which 9 were waited for; matrix products, arithmetic and copies ran while one was open for 6% of the time, Pallas kernels for 0%

profile of v4, /device:TPU:32, one launch (start us, length us, event | category | flops | bytes accessed | tf_op | source)
XLA Modules:
  0.0 348.9 jit_solution(3489277269194234421)
XLA Ops:
  0.0 0.9 fusion.77
  0.9 1.1 reduce_sum.112
  2.0 1.1 multiply_reduce_fusion.2
  3.1 0.8 reduce-window.8
  4.6 2.8 fusion
  7.9 6.4 %collective-permute-start = (bf16[16,3072]{1,0:T(8,128)(2,1)S(1)}, bf16[16,3072]{1,0:T(8,128)(2,1)S(1)}, u32[]{:S(2)}, u32[]{:S(2)}) collective-permute-start(bf16[16,3072]{1,0:T(8,128)(2,1)S(1)} %fusion.43), channel_id=1, source_target_pairs={{0,4},{4,0},{1,5},{5,1},{2,6},{6,2},{3,7},{7,3},{8,12},{12,8},{9,1... | collective-permute-start | bytes 294920 | tf_op jit(solution)/shard_map/ppermute | solution.py:75
  14.3 4.3 %collective-permute-done = bf16[16,3072]{1,0:T(8,128)(2,1)S(1)} collective-permute-done((bf16[16,3072]{1,0:T(8,128)(2,1)S(1)}, bf16[16,3072]{1,0:T(8,128)(2,1)S(1)}, u32[]{:S(2)}, u32[]{:S(2)}) %collective-permute-start) | collective-permute-done | bytes 98336 | tf_op jit(solution)/shard_map/ppermute | solution.py:75
  19.0 44.8 %all_to_all.92 = bf16[16,2,16,3072]{3,2,1,0:T(8,128)(2,1)S(1)} all-to-all(bf16[16,2,16,3072]{3,2,1,0:T(8,128)(2,1)S(1)} %broadcast_in_dim.64), channel_id=1, replica_groups=mesh['zl'=4,'core'=2,'y'=4,'zh'=2,'x'=4] {'y','x'}, dimensions={0} | all-to-all | bytes 6291456 | tf_op jit(solution)/shard_map/all_to_all | solution.py:78
  63.8 1.7 copy-done.2
  65.5 1.1 convolution_convert_fusion
  66.7 0.9 copy.86
  67.6 7.8 %all-to-all-start.1 = ((bf16[32,16,288]{2,1,0:T(8,128)(2,1)}), bf16[32,16,288]{2,1,0:T(8,128)(2,1)S(1)}, u32[]{:S(2)}, u32[]{:S(2)}) async-start(bf16[32,16,288]{2,1,0:T(8,128)(2,1)} %bitcast.94), calls=%async_computation.1 | async-start | bytes 786432 | tf_op jit(solution)/shard_map/all_to_all | solution.py:151
  75.4 0.7 mul.299
  76.1 0.7 mul.310
  76.8 1.8 reshape.463
  78.6 0.9 convert_reduce_fusion.2
  79.6 13.3 %all-to-all-done.1 = bf16[32,16,288]{2,1,0:T(8,128)(2,1)S(1)} async-done(((bf16[32,16,288]{2,1,0:T(8,128)(2,1)}), bf16[32,16,288]{2,1,0:T(8,128)(2,1)S(1)}, u32[]{:S(2)}, u32[]{:S(2)}) %all-to-all-start.1) | async-done | bytes 294944 | tf_op jit(solution)/shard_map/all_to_all | solution.py:151
  92.9 0.9 copy.130
  93.8 1.3 all_to_all.69
  95.2 0.7 copy.88
  95.9 4.0 %all-to-all-start.2 = ((bf16[16,8,1152]{2,0,1:T(8,128)(2,1)}), bf16[16,8,1152]{2,0,1:T(8,128)(2,1)S(1)}, u32[]{:S(2)}, u32[]{:S(2)}) async-start(bf16[16,8,1152]{2,0,1:T(8,128)(2,1)} %copy.88), calls=%async_computation.2 | async-start | bytes 589824 | tf_op jit(solution)/shard_map/all_to_all | solution.py:153
  100.0 0.7 fusion.94
  100.8 7.4 %all-to-all-done.2 = bf16[16,8,1152]{2,0,1:T(8,128)(2,1)S(1)} async-done(((bf16[16,8,1152]{2,0,1:T(8,128)(2,1)}), bf16[16,8,1152]{2,0,1:T(8,128)(2,1)S(1)}, u32[]{:S(2)}, u32[]{:S(2)}) %all-to-all-start.2) | async-done | bytes 294944 | tf_op jit(solution)/shard_map/all_to_all | solution.py:153
  108.2 0.7 copy-done.4
  108.9 1.0 reshape.465
  109.9 1.1 fusion.93
  111.2 0.7 copy_convert_fusion
  111.9 1.1 copy.110
  113.0 1.7 copy.95
  114.7 0.8 copy.90
  115.6 1.1 multiply_multiply_fusion.1
  116.6 1.1 multiply_multiply_fusion.2
  117.7 2.0 subtract_convert_fusion.1
  119.9 1.7 collective-permute-start.1
  121.7 10.5 %collective-permute-done.1 = bf16[128,3,256]{0,2,1:T(8,128)(2,1)S(1)} collective-permute-done((bf16[128,3,256]{0,2,1:T(8,128)(2,1)S(1)}, bf16[128,3,256]{0,2,1:T(8,128)(2,1)S(1)}, u32[]{:S(2)}, u32[]{:S(2)}) %collective-permute-start.1) | collective-permute-done | bytes 196640 | tf_op jit(solution)/shard_map/ppermute | solution.py:175
  132.3 0.7 fusion.49
  133.0 1.0 copy.104
  134.0 1.5 broadcast_in_dim.121
  135.6 4.6 %all-to-all-start.5 = ((bf16[16,2,128,256]{3,2,1,0:T(8,128)(2,1)}), bf16[16,2,128,256]{3,2,1,0:T(8,128)(2,1)}, u32[]{:S(2)}, u32[]{:S(2)}) async-start(bf16[16,2,128,256]{3,2,1,0:T(8,128)(2,1)} %broadcast_in_dim.121), calls=%async_computation.5 | async-start | bytes 4194304 | tf_op jit(solution)/shard_map/all_to_all | solution.py:191
  140.3 27.5 %all-to-all-done.5 = bf16[16,2,128,256]{3,2,1,0:T(8,128)(2,1)} async-done(((bf16[16,2,128,256]{3,2,1,0:T(8,128)(2,1)}), bf16[16,2,128,256]{3,2,1,0:T(8,128)(2,1)}, u32[]{:S(2)}, u32[]{:S(2)}) %all-to-all-start.5) | async-done | bytes 2097184 | tf_op jit(solution)/shard_map/all_to_all | solution.py:191
  167.7 1.6 broadcast_in_dim.66
  169.3 4.6 %all-to-all-start.3 = ((bf16[16,2,128,256]{3,2,1,0:T(8,128)(2,1)}), bf16[16,2,128,256]{3,2,1,0:T(8,128)(2,1)}, u32[]{:S(2)}, u32[]{:S(2)}) async-start(bf16[16,2,128,256]{3,2,1,0:T(8,128)(2,1)} %broadcast_in_dim.66), calls=%async_computation.3 | async-start | bytes 4194304 | tf_op jit(solution)/shard_map/all_to_all | solution.py:191
  174.0 27.1 %all-to-all-done.3 = bf16[16,2,128,256]{3,2,1,0:T(8,128)(2,1)} async-done(((bf16[16,2,128,256]{3,2,1,0:T(8,128)(2,1)}), bf16[16,2,128,256]{3,2,1,0:T(8,128)(2,1)}, u32[]{:S(2)}, u32[]{:S(2)}) %all-to-all-start.3) | async-done | bytes 2097184 | tf_op jit(solution)/shard_map/all_to_all | solution.py:191
  201.1 1.6 broadcast_in_dim.119
  202.7 4.8 %all-to-all-start.4 = ((bf16[16,2,128,256]{3,2,1,0:T(8,128)(2,1)}), bf16[16,2,128,256]{3,2,1,0:T(8,128)(2,1)}, u32[]{:S(2)}, u32[]{:S(2)}) async-start(bf16[16,2,128,256]{3,2,1,0:T(8,128)(2,1)} %broadcast_in_dim.119), calls=%async_computation.4 | async-start | bytes 4194304 | tf_op jit(solution)/shard_map/all_to_all | solution.py:191
  208.3 3.1 convolution_multiply_fusion
  211.4 3.5 select_reduce_fusion.2
  214.8 20.9 %all-to-all-done.4 = bf16[16,2,128,256]{3,2,1,0:T(8,128)(2,1)} async-done(((bf16[16,2,128,256]{3,2,1,0:T(8,128)(2,1)}), bf16[16,2,128,256]{3,2,1,0:T(8,128)(2,1)}, u32[]{:S(2)}, u32[]{:S(2)}) %all-to-all-start.4) | async-done | bytes 2097184 | tf_op jit(solution)/shard_map/all_to_all | solution.py:191
  235.7 4.3 %fusion.2 = (f32[128]{0:T(128)S(1)}, f32[128]{0:T(128)S(1)}, f32[128]{0:T(128)S(1)}, f32[128,4096]{1,0:T(8,128)S(1)}) fusion(f32[128,4096]{1,0:T(8,128)} %get-tuple-element.29, f32[128]{0:T(128)S(1)} %get-tuple-element.28, s32[4096]{0:T(1024)S(1)} %fusion.60, s32[128]{0:T(128)S(1)} %fusion.79, pred[4096]{0:T(1024)(128)(4,1)S(1)} %eq.120, ...), kind=kOutput, calls=%fused_computation.14 | convolution fusion | flops 140508800 | bytes 7412736 | tf_op jit(solution)/shard_map/qd,kd->qk/dot_general | solution.py:197
  240.1 2.4 fusion.13
  242.5 1.4 fusion.4
  243.9 2.2 fusion.11
  246.1 2.2 fusion.12
  248.6 22.0 %all_to_all.93 = bf16[8,16,384]{2,1,0:T(8,128)(2,1)S(1)} all-to-all(bf16[8,16,384]{2,1,0:T(8,128)(2,1)S(1)} %all_to_all.75), channel_id=1, replica_groups=mesh['zl'=4,'core'=2,'y'=4,'zh'=2,'x'=4] {'zl','core'}, dimensions={0} | all-to-all | bytes 196608 | tf_op jit(solution)/shard_map/all_to_all | solution.py:207
  270.7 0.7 copy.106
  271.3 3.9 %all-to-all-start.7 = ((bf16[16,32,96]{2,0,1:T(8,128)(2,1)}), bf16[16,32,96]{2,0,1:T(8,128)(2,1)S(1)}, u32[]{:S(2)}, u32[]{:S(2)}) async-start(bf16[16,32,96]{2,0,1:T(8,128)(2,1)} %bitcast.36), calls=%async_computation.7 | async-start | bytes 262144 | tf_op jit(solution)/shard_map/all_to_all | solution.py:209
  275.2 8.8 %fusion.37 = f32[512,3072]{1,0:T(8,128)} fusion(bf16[384,3072]{1,0:T(8,128)(2,1)S(1)} %copy-done, bf16[512,3072]{1,0:T(8,128)(2,1)} %bitcast.91, bf16[3072,384]{1,0:T(8,128)(2,1)} %param.19), kind=kOutput, calls=%fused_computation.55 | convolution fusion | flops 2417688576 | bytes 14155776 | tf_op jit(solution)/shard_map/dot_general | solution.py:211
  284.0 4.6 %all-to-all-done.7 = bf16[16,32,96]{2,0,1:T(8,128)(2,1)S(1)} async-done(((bf16[16,32,96]{2,0,1:T(8,128)(2,1)}), bf16[16,32,96]{2,0,1:T(8,128)(2,1)S(1)}, u32[]{:S(2)}, u32[]{:S(2)}) %all-to-all-start.7) | async-done | bytes 98336 | tf_op jit(solution)/shard_map/all_to_all | solution.py:209
  288.7 4.0 %add_convert_fusion = bf16[512,3072]{1,0:T(8,128)(2,1)S(1)} fusion(f32[512,3072]{1,0:T(8,128)} %fusion.37, bf16[512,96]{1,0:T(8,128)(2,1)S(1)} %bitcast.103, bf16[96,3072]{1,0:T(8,128)(2,1)} %param.22), kind=kOutput, calls=%fused_computation.1 | convolution fusion | flops 305135616 | bytes 10125312 | tf_op jit(solution)/shard_map/dot_general | solution.py:213
  292.6 42.1 %all_to_all.94 = bf16[16,2,16,3072]{3,2,1,0:T(8,128)(2,1)S(1)} all-to-all(bf16[16,2,16,3072]{3,2,1,0:T(8,128)(2,1)S(1)} %bitcast.89), channel_id=1, replica_groups=mesh['zl'=4,'core'=2,'y'=4,'zh'=2,'x'=4] {'y','x'}, dimensions={0} | all-to-all | bytes 6291456 | tf_op jit(solution)/shard_map/all_to_all | solution.py:85
  334.7 0.6 convert_reduce_fusion
  335.3 4.8 %collective-permute-start.2 = (f32[16,3072]{1,0:T(8,128)S(1)}, f32[16,3072]{1,0:T(8,128)S(1)}, u32[]{:S(2)}, u32[]{:S(2)}) collective-permute-start(f32[16,3072]{1,0:T(8,128)S(1)} %select_bitcast_fusion), channel_id=1, source_target_pairs={{0,4},{4,0},{1,5},{5,1},{2,6},{6,2},{3,7},{7,3},{8,12},{12,8},{9,1... | collective-permute-start | bytes 589832 | tf_op jit(solution)/shard_map/ppermute | solution.py:88
  340.1 8.0 %collective-permute-done.2 = f32[16,3072]{1,0:T(8,128)S(1)} collective-permute-done((f32[16,3072]{1,0:T(8,128)S(1)}, f32[16,3072]{1,0:T(8,128)S(1)}, u32[]{:S(2)}, u32[]{:S(2)}) %collective-permute-start.2) | collective-permute-done | bytes 196640 | tf_op jit(solution)/shard_map/ppermute | solution.py:88
  348.1 0.7 fusion.45
  (70 shorter events, 3.6 us)
Async XLA Ops:
  0.0 275.2 %copy-start = (bf16[384,3072]{1,0:T(8,128)(2,1)S(1)}, bf16[384,3072]{1,0:T(8,128)(2,1)}, u32[]{:S(2)}) copy-start(bf16[384,3072]{1,0:T(8,128)(2,1)} %param.23) | copy-start | bytes 7077892
  0.0 7.8 %copy-start.3 = (f32[16,3072]{1,0:T(8,128)S(1)}, f32[16,3072]{1,0:T(8,128)}, u32[]{:S(2)}) copy-start(f32[16,3072]{1,0:T(8,128)} %param.12) | copy-start | bytes 589828
  4.0 0.6 copy-start.14
  7.9 10.6 %collective-permute-start = (bf16[16,3072]{1,0:T(8,128)(2,1)S(1)}, bf16[16,3072]{1,0:T(8,128)(2,1)S(1)}, u32[]{:S(2)}, u32[]{:S(2)}) collective-permute-start(bf16[16,3072]{1,0:T(8,128)(2,1)S(1)} %fusion.43), channel_id=1, source_target_pairs={{0,4},{4,0},{1,5},{5,1},{2,6},{6,2},{3,7},{7,3},{8,12},{12,8},{9,1... | collective-permute-start | bytes 294920 | tf_op jit(solution)/shard_map/ppermute | solution.py:75
  19.0 46.5 %copy-start.16 = (bf16[3072,288]{0,1:T(8,128)(2,1)S(1)}, bf16[3072,288]{0,1:T(8,128)(2,1)}, u32[]{:S(2)}) copy-start(bf16[3072,288]{0,1:T(8,128)(2,1)} %param.18) | copy-start | bytes 5308420
  63.8 1.7 copy-start.2
  65.5 9.8 %copy-start.12 = (f32[128]{0:T(128)S(1)}, f32[128]{0:T(128)}, u32[]{:S(2)}) copy-start(f32[128]{0:T(128)} %param.20) | copy-start | bytes 1540
  65.5 10.6 %copy-start.13 = (f32[128]{0:T(128)S(1)}, f32[128]{0:T(128)}, u32[]{:S(2)}) copy-start(f32[128]{0:T(128)} %param.21) | copy-start | bytes 1540
  67.6 25.3 %all-to-all-start.1 = ((bf16[32,16,288]{2,1,0:T(8,128)(2,1)}), bf16[32,16,288]{2,1,0:T(8,128)(2,1)S(1)}, u32[]{:S(2)}, u32[]{:S(2)}) async-start(bf16[32,16,288]{2,1,0:T(8,128)(2,1)} %bitcast.94), calls=%async_computation.1 | async-start | bytes 786432 | tf_op jit(solution)/shard_map/all_to_all | solution.py:151
  95.9 12.3 %all-to-all-start.2 = ((bf16[16,8,1152]{2,0,1:T(8,128)(2,1)}), bf16[16,8,1152]{2,0,1:T(8,128)(2,1)S(1)}, u32[]{:S(2)}, u32[]{:S(2)}) async-start(bf16[16,8,1152]{2,0,1:T(8,128)(2,1)} %copy.88), calls=%async_computation.2 | async-start | bytes 589824 | tf_op jit(solution)/shard_map/all_to_all | solution.py:153
  108.2 0.7 copy-start.4
  111.0 4.5 %copy-start.10 = (f32[64,2]{1,0:T(8,128)S(1)}, f32[64,2]{1,0:T(8,128)}, u32[]{:S(2)}) copy-start(f32[64,2]{1,0:T(8,128)} %mul.310) | copy-start | bytes 1540
  111.0 5.6 %copy-start.9 = (f32[64,2]{1,0:T(8,128)S(1)}, f32[64,2]{1,0:T(8,128)}, u32[]{:S(2)}) copy-start(f32[64,2]{1,0:T(8,128)} %mul.299) | copy-start | bytes 1540
  119.9 12.3 %collective-permute-start.1 = (bf16[128,3,256]{0,2,1:T(8,128)(2,1)S(1)}, bf16[128,3,256]{0,2,1:T(8,128)(2,1)S(1)}, u32[]{:S(2)}, u32[]{:S(2)}) collective-permute-start(bf16[128,3,256]{0,2,1:T(8,128)(2,1)S(1)} %pad_maximum_fusion.1), channel_id=1, source_target_pairs={{0,4},{4,0},{1,5},{5,1},{2,6},{6,2},{3,7},{7,3},{8,12},{12,8},{9,1... | collective-permute-start | bytes 589832 | tf_op jit(solution)/shard_map/ppermute | solution.py:175
  135.6 4.6 %copy-start.6 = (bf16[2,128,1,256]{1,3,2,0:T(8,128)(2,1)S(1)}, bf16[2,128,1,256]{1,3,2,0:T(8,128)(2,1)}, u32[]{:S(2)}) copy-start(bf16[2,128,1,256]{1,3,2,0:T(8,128)(2,1)} %get-tuple-element.11) | copy-start | bytes 393220
  135.6 32.2 %all-to-all-start.5 = ((bf16[16,2,128,256]{3,2,1,0:T(8,128)(2,1)}), bf16[16,2,128,256]{3,2,1,0:T(8,128)(2,1)}, u32[]{:S(2)}, u32[]{:S(2)}) async-start(bf16[16,2,128,256]{3,2,1,0:T(8,128)(2,1)} %broadcast_in_dim.121), calls=%async_computation.5 | async-start | bytes 4194304 | tf_op jit(solution)/shard_map/all_to_all | solution.py:191
  169.3 4.6 %copy-start.5 = (bf16[2,128,1,256]{1,3,2,0:T(8,128)(2,1)S(1)}, bf16[2,128,1,256]{1,3,2,0:T(8,128)(2,1)}, u32[]{:S(2)}) copy-start(bf16[2,128,1,256]{1,3,2,0:T(8,128)(2,1)} %get-tuple-element.10) | copy-start | bytes 393220
  169.3 31.9 %all-to-all-start.3 = ((bf16[16,2,128,256]{3,2,1,0:T(8,128)(2,1)}), bf16[16,2,128,256]{3,2,1,0:T(8,128)(2,1)}, u32[]{:S(2)}, u32[]{:S(2)}) async-start(bf16[16,2,128,256]{3,2,1,0:T(8,128)(2,1)} %broadcast_in_dim.66), calls=%async_computation.3 | async-start | bytes 4194304 | tf_op jit(solution)/shard_map/all_to_all | solution.py:191
  202.7 4.8 %copy-start.11 = (s32[4096]{0:T(1024)S(1)}, s32[4096]{0:T(1024)}, u32[]{:S(2)}) copy-start(s32[4096]{0:T(1024)} %param.13) | copy-start | bytes 49156
  202.7 5.1 %copy-start.15 = (s32[4,1]{0,1:T(1,128)S(1)}, s32[4,1]{0,1:T(1,128)}, u32[]{:S(2)}) copy-start(s32[4,1]{0,1:T(1,128)} %copy-done.14) | copy-start | bytes 52
  202.7 5.3 %copy-start.7 = (bf16[128,3,64,1]{0,3,2,1:T(2,128)(2,1)S(1)}, bf16[128,3,64,1]{0,3,2,1:T(2,128)(2,1)}, u32[]{:S(2)}) copy-start(bf16[128,3,64,1]{0,3,2,1:T(2,128)(2,1)} %get-tuple-element.18) | copy-start | bytes 147460
  202.7 5.3 %copy-start.8 = (bf16[128,3,64,1]{0,3,2,1:T(2,128)(2,1)S(1)}, bf16[128,3,64,1]{0,3,2,1:T(2,128)(2,1)}, u32[]{:S(2)}) copy-start(bf16[128,3,64,1]{0,3,2,1:T(2,128)(2,1)} %get-tuple-element.19) | copy-start | bytes 147460
  202.7 33.0 %all-to-all-start.4 = ((bf16[16,2,128,256]{3,2,1,0:T(8,128)(2,1)}), bf16[16,2,128,256]{3,2,1,0:T(8,128)(2,1)}, u32[]{:S(2)}, u32[]{:S(2)}) async-start(bf16[16,2,128,256]{3,2,1,0:T(8,128)(2,1)} %broadcast_in_dim.119), calls=%async_computation.4 | async-start | bytes 4194304 | tf_op jit(solution)/shard_map/all_to_all | solution.py:191
  235.7 4.3 %copy-start.17 = (f32[128,4096]{1,0:T(8,128)S(1)}, f32[128,4096]{1,0:T(8,128)}, u32[]{:S(2)}) copy-start(f32[128,4096]{1,0:T(8,128)} %get-tuple-element.29) | copy-start | bytes 6291460
  240.1 2.4 copy-start.1
  271.3 17.3 %all-to-all-start.7 = ((bf16[16,32,96]{2,0,1:T(8,128)(2,1)}), bf16[16,32,96]{2,0,1:T(8,128)(2,1)S(1)}, u32[]{:S(2)}, u32[]{:S(2)}) async-start(bf16[16,32,96]{2,0,1:T(8,128)(2,1)} %bitcast.36), calls=%async_computation.7 | async-start | bytes 262144 | tf_op jit(solution)/shard_map/all_to_all | solution.py:209
  335.3 12.8 %collective-permute-start.2 = (f32[16,3072]{1,0:T(8,128)S(1)}, f32[16,3072]{1,0:T(8,128)S(1)}, u32[]{:S(2)}, u32[]{:S(2)}) collective-permute-start(f32[16,3072]{1,0:T(8,128)S(1)} %select_bitcast_fusion), channel_id=1, source_target_pairs={{0,4},{4,0},{1,5},{5,1},{2,6},{6,2},{3,7},{7,3},{8,12},{12,8},{9,1... | collective-permute-start | bytes 589832 | tf_op jit(solution)/shard_map/ppermute | solution.py:88

commit v5 on v4

--- a/solution.py
+++ b/solution.py
@@ -71,12 +71,11 @@
     return jnp.where(first, mine, other), jnp.where(first, other, mine)
 
 
-def gather_plane(x):
-    low, high = by_half(x, lax.ppermute(x, "zh", SWAP))
+def gather_plane(low, high):
     pair = jnp.stack([low, high])
     plane = lax.axis_size("y") * lax.axis_size("x")
     got = lax.all_to_all(jnp.broadcast_to(pair[None], (plane,) + pair.shape), PLANE, 0, 0, tiled=True)
-    return got.reshape((lax.axis_size("y"), lax.axis_size("x"), 2) + x.shape)
+    return got.reshape((lax.axis_size("y"), lax.axis_size("x"), 2) + low.shape)
 
 
 def reduce_blk(y):
@@ -115,8 +114,8 @@
     step_total = mod_table.shape[1]
     inv_root = 1.0 / math.sqrt(head_size)
     request_ends = jnp.cumsum(lengths)
-    own_rows = seq_at * tok_seq + blk_at * block_rows + jnp.arange(block_rows, dtype=jnp.int32)
-    own_request = segment_of(own_rows, request_ends)
+    partner_blk = blk_at + lax.axis_size("x") * (1 - 2 * lax.axis_index("zh"))
+    partner_stream = lax.ppermute(stream, "zh", SWAP)
     step_pick = (jnp.arange(step_total, dtype=jnp.int32)[None, :] == step_index[:, None]).astype(
         jnp.bfloat16
     )
@@ -126,20 +125,26 @@
         mod_table.reshape(requests, step_total, 3 * width),
         preferred_element_type=jnp.float32,
     )
-    member = (own_request[:, None] == jnp.arange(requests, dtype=jnp.int32)[None, :]).astype(
-        jnp.float32
-    )
-    token_mod = jnp.dot(member, modulation, precision=lax.Precision.HIGHEST)
-    mod_shift = token_mod[:, :width]
-    mod_scale = token_mod[:, width : 2 * width]
-    mod_gate = token_mod[:, 2 * width :]
-    row_mean = jnp.mean(stream, axis=1, keepdims=True)
-    centered = stream - row_mean
-    row_var = jnp.mean(centered * centered, axis=1, keepdims=True)
-    normed = centered * lax.rsqrt(row_var + 1e-06)
-    modin = ((1.0 + mod_scale) * normed + mod_shift).astype(jnp.bfloat16)
+
+    def modulated(rows, row_blk):
+        row_ids = seq_at * tok_seq + row_blk * block_rows + jnp.arange(block_rows, dtype=jnp.int32)
+        row_request = segment_of(row_ids, request_ends)
+        member = (row_request[:, None] == jnp.arange(requests, dtype=jnp.int32)[None, :]).astype(
+            jnp.float32
+        )
+        token_mod = jnp.dot(member, modulation, precision=lax.Precision.HIGHEST)
+        mod_shift = token_mod[:, :width]
+        mod_scale = token_mod[:, width : 2 * width]
+        row_mean = jnp.mean(rows, axis=1, keepdims=True)
+        centered = rows - row_mean
+        row_var = jnp.mean(centered * centered, axis=1, keepdims=True)
+        normed = centered * lax.rsqrt(row_var + 1e-06)
+        return ((1.0 + mod_scale) * normed + mod_shift).astype(jnp.bfloat16), token_mod[:, 2 * width :]
+
+    modin, mod_gate = modulated(stream, blk_at)
+    partner_modin, _ = modulated(partner_stream, partner_blk)
     qkv_width = w_qkv.shape[1]
-    shard_rows = gather_plane(modin).reshape(blk_count * block_rows, width)
+    shard_rows = gather_plane(*by_half(modin, partner_modin)).reshape(blk_count * block_rows, width)
     qkv_part = jnp.dot(shard_rows, w_qkv, preferred_element_type=jnp.float32).astype(jnp.bfloat16)
     mlp_part = jax.nn.gelu(
         jnp.dot(shard_rows, w_mlp_in, preferred_element_type=jnp.float32), approximate=True
@@ -172,8 +177,16 @@
     )
     value_rows = heads4[:, :, 2]
     kv_rows = jnp.concatenate([key_rot, value_rows], axis=2)
-    low, high = by_half(kv_rows, lax.ppermute(kv_rows, "zh", SWAP))
-    kv_pair = jnp.stack([low, high])
+    partner_raw = lax.ppermute(heads4[:, :, 1:], "zh", SWAP)
+    partner_places = lax.dynamic_index_in_dim(
+        positions.reshape(seq_count, blk_count, block_rows, -1), partner_blk, axis=1, keepdims=False
+    ).reshape(query_rows, -1)
+    partner_key = rotate(
+        rms_scale(partner_raw[:, :, 0].astype(jnp.float32), k_gain),
+        angles_of(partner_places, rope_table(head_size)),
+    ).astype(jnp.bfloat16)
+    partner_rows = jnp.concatenate([partner_key, partner_raw[:, :, 1]], axis=2)
+    kv_pair = jnp.stack(by_half(kv_rows, partner_rows))
     key_rank = jnp.arange(seq_count * tok_seq, dtype=jnp.int32)
     key_y = key_rank // (xs * 2 * query_rows)
     key_x = key_rank // (2 * query_rows) % xs

time: 350 us -> 347 us (level)
  blocking collectives: 109 us -> 99.9 us
  other arithmetic: 14.5 us -> 20.1 us
  waiting for transfers between devices: 124 us -> 120 us
  local copies, waits for them, and re-layouts: 24.1 us -> 27.8 us
    all_to_all x1, blocking collectives: 22 us -> 11.4 us  [body(): lax.all_to_all(attended, SEQ, split_axis=0, concat_axis=1, tiled=True)]
    all_to_all x1, waiting for transfers between devices: 13.3 us -> 8.39 us  [body(): lax.all_to_all(qkv_cols, ('y', 'x', 'zh'), split_axis=0, concat_axis=1, t...]
    all_to_all x3, waiting for transfers between devices: 75.5 us -> 80.4 us  [body(): lax.all_to_all(jnp.broadcast_to(piece[None], (ys * xs,) + piece.shape), P...]
  transfers between devices with their start and end apart: 9 -> 9, of which waited for: 9 -> 9; matrix products, arithmetic and copies ran while one was open for 6% -> 10% of each run, Pallas kernels for 0% -> 0%
where the time goes in v5:
time: 347 us; the launch traced here: 346 us
  waiting for transfers between devices  120 us (35%)
  blocking collectives  99.9 us (29%)
  starting transfers between devices  41.7 us (12%)
  matrix products  36.1 us (10%)
  local copies, waits for them, and re-layouts  27.8 us (8%)
  other arithmetic  20.1 us (6%)
    all_to_all x3, waiting for transfers between devices, body(): lax.all_to_all(jnp.broadcast_to(piece[None], (ys * xs,) + piece.shape), P...  80.4 us
    all_to_all x1, blocking collectives, gather_plane(): lax.all_to_all(jnp.broadcast_to(pair[None], (plane,) + pair.shape), PLANE...  46.4 us
    all_to_all x1, blocking collectives, reduce_blk(): got = lax.all_to_all(pieces, PLANE, 0, 0, tiled=True)  42.1 us
    all_to_all x3, starting transfers between devices, body(): lax.all_to_all(jnp.broadcast_to(piece[None], (ys * xs,) + piece.shape), P...  13.6 us
    all_to_all x1, blocking collectives, body(): lax.all_to_all(attended, SEQ, split_axis=0, concat_axis=1, tiled=True)  11.4 us
    dot_general x3, matrix products, body(): jnp.einsum('qd,kd->qk', query_rot[:, head], key_h, preferred_element_type...  10.9 us
    ppermute x1, waiting for transfers between devices, body(): partner_raw = lax.ppermute(heads4[:, :, 1:], 'zh', SWAP)  10.8 us
    dot_general x1, matrix products, body(): jnp.dot(mlp_act, w_mlp_out, preferred_element_type=jnp.float32)  8.81 us
  transfers between devices with their start and end apart: 9, of which 9 were waited for; matrix products, arithmetic and copies ran while one was open for 10% of the time, Pallas kernels for 0%

profile of v5, /device:TPU:32, one launch (start us, length us, event | category | flops | bytes accessed | tf_op | source)
XLA Modules:
  0.0 345.8 jit_solution(12778194179039454220)
XLA Ops:
  0.0 6.3 %collective-permute-start = (f32[16,3072]{1,0:T(8,128)}, f32[16,3072]{1,0:T(8,128)S(1)}, u32[]{:S(2)}, u32[]{:S(2)}) collective-permute-start(f32[16,3072]{1,0:T(8,128)} %param.12), channel_id=1, source_target_pairs={{0,4},{4,0},{1,5},{5,1},{2,6},{6,2},{3,7},{7,3},{8,12},{12,8},{9,1... | collective-permute-start | bytes 589832 | tf_op jit(solution)/shard_map/ppermute | solution.py:118
  6.3 0.8 reduce-window.8
  7.8 1.1 reduce_sum.157
  8.9 1.1 multiply_reduce_fusion.4
  10.1 2.9 fusion
  13.5 1.3 fusion.48
  14.7 0.9 collective-permute-done
  16.0 1.2 select_bitcast_fusion.2
  17.7 46.4 %all_to_all.92 = bf16[16,2,16,3072]{3,2,1,0:T(8,128)(2,1)S(1)} all-to-all(bf16[16,2,16,3072]{3,2,1,0:T(8,128)(2,1)S(1)} %broadcast_in_dim.75), channel_id=1, replica_groups=mesh['zl'=4,'core'=2,'y'=4,'zh'=2,'x'=4] {'y','x'}, dimensions={0} | all-to-all | bytes 6291456 | tf_op jit(solution)/shard_map/all_to_all | solution.py:77
  64.1 1.7 copy-done.2
  65.8 1.1 convolution_convert_fusion
  66.9 0.9 copy.123
  67.8 7.0 %all-to-all-start.1 = ((bf16[32,16,288]{2,1,0:T(8,128)(2,1)}), bf16[32,16,288]{2,1,0:T(8,128)(2,1)S(1)}, u32[]{:S(2)}, u32[]{:S(2)}) async-start(bf16[32,16,288]{2,1,0:T(8,128)(2,1)} %bitcast.98), calls=%async_computation.1 | async-start | bytes 786432 | tf_op jit(solution)/shard_map/all_to_all | solution.py:156
  74.8 0.7 mul.397
  75.5 0.7 mul.408
  76.3 1.8 reshape.622
  78.0 1.6 convert_reduce_fusion.3
  79.7 0.8 convert_element_type.151
  81.7 8.4 %all-to-all-done.1 = bf16[32,16,288]{2,1,0:T(8,128)(2,1)S(1)} async-done(((bf16[32,16,288]{2,1,0:T(8,128)(2,1)}), bf16[32,16,288]{2,1,0:T(8,128)(2,1)S(1)}, u32[]{:S(2)}, u32[]{:S(2)}) %all-to-all-start.1) | async-done | bytes 294944 | tf_op jit(solution)/shard_map/all_to_all | solution.py:156
  90.1 0.9 copy.178
  91.0 1.3 all_to_all.69
  92.4 0.7 copy.125
  93.1 5.4 %all-to-all-start.2 = ((bf16[16,8,1152]{2,0,1:T(8,128)(2,1)}), bf16[16,8,1152]{2,0,1:T(8,128)(2,1)S(1)}, u32[]{:S(2)}, u32[]{:S(2)}) async-start(bf16[16,8,1152]{2,0,1:T(8,128)(2,1)} %copy.125), calls=%async_computation.2 | async-start | bytes 589824 | tf_op jit(solution)/shard_map/all_to_all | solution.py:158
  99.3 0.9 fusion.102
  100.2 6.6 %all-to-all-done.2 = bf16[16,8,1152]{2,0,1:T(8,128)(2,1)S(1)} async-done(((bf16[16,8,1152]{2,0,1:T(8,128)(2,1)}), bf16[16,8,1152]{2,0,1:T(8,128)(2,1)S(1)}, u32[]{:S(2)}, u32[]{:S(2)}) %all-to-all-start.2) | async-done | bytes 294944 | tf_op jit(solution)/shard_map/all_to_all | solution.py:158
  107.5 1.0 reshape.624
  108.8 1.1 fusion.101
  110.9 1.7 copy.152
  112.6 0.8 copy.127
  113.5 0.8 collective-permute-start.1
  114.3 1.7 multiply_multiply_fusion.3
  116.0 10.8 %collective-permute-done.1 = bf16[128,3,2,128]{3,0,2,1:T(8,128)(2,1)S(1)} collective-permute-done((bf16[128,3,2,128]{3,0,2,1:T(8,128)(2,1)}, bf16[128,3,2,128]{3,0,2,1:T(8,128)(2,1)S(1)}, u32[]{:S(2)}, u32[]{:S(2)}) %collective-permute-start.1) | collective-permute-done | bytes 196640 | tf_op jit(solution)/shard_map/ppermute | solution.py:180
  127.0 0.7 slice_convert_fusion
  127.7 1.1 copy.138
  128.8 1.6 copy.141
  130.4 1.0 multiply_multiply_fusion.2
  131.5 2.2 subtract_convert_fusion.2
  133.9 1.0 subtract_convert_fusion
  136.0 1.0 copy.146
  137.0 1.5 broadcast_in_dim.83
  138.5 4.4 %all-to-all-start.5 = ((bf16[16,2,128,256]{3,2,1,0:T(8,128)(2,1)}), bf16[16,2,128,256]{3,2,1,0:T(8,128)(2,1)}, u32[]{:S(2)}, u32[]{:S(2)}) async-start(bf16[16,2,128,256]{3,2,1,0:T(8,128)(2,1)} %broadcast_in_dim.83), calls=%async_computation.5 | async-start | bytes 4194304 | tf_op jit(solution)/shard_map/all_to_all | solution.py:204
  143.1 29.6 %all-to-all-done.5 = bf16[16,2,128,256]{3,2,1,0:T(8,128)(2,1)} async-done(((bf16[16,2,128,256]{3,2,1,0:T(8,128)(2,1)}), bf16[16,2,128,256]{3,2,1,0:T(8,128)(2,1)}, u32[]{:S(2)}, u32[]{:S(2)}) %all-to-all-start.5) | async-done | bytes 2097184 | tf_op jit(solution)/shard_map/all_to_all | solution.py:204
  172.6 1.6 broadcast_in_dim.77
  174.2 4.4 %all-to-all-start.3 = ((bf16[16,2,128,256]{3,2,1,0:T(8,128)(2,1)}), bf16[16,2,128,256]{3,2,1,0:T(8,128)(2,1)}, u32[]{:S(2)}, u32[]{:S(2)}) async-start(bf16[16,2,128,256]{3,2,1,0:T(8,128)(2,1)} %broadcast_in_dim.77), calls=%async_computation.3 | async-start | bytes 4194304 | tf_op jit(solution)/shard_map/all_to_all | solution.py:204
  178.8 29.1 %all-to-all-done.3 = bf16[16,2,128,256]{3,2,1,0:T(8,128)(2,1)} async-done(((bf16[16,2,128,256]{3,2,1,0:T(8,128)(2,1)}), bf16[16,2,128,256]{3,2,1,0:T(8,128)(2,1)}, u32[]{:S(2)}, u32[]{:S(2)}) %all-to-all-start.3) | async-done | bytes 2097184 | tf_op jit(solution)/shard_map/all_to_all | solution.py:204
  207.9 1.6 broadcast_in_dim.81
  209.4 4.8 %all-to-all-start.4 = ((bf16[16,2,128,256]{3,2,1,0:T(8,128)(2,1)}), bf16[16,2,128,256]{3,2,1,0:T(8,128)(2,1)}, u32[]{:S(2)}, u32[]{:S(2)}) async-start(bf16[16,2,128,256]{3,2,1,0:T(8,128)(2,1)} %broadcast_in_dim.81), calls=%async_computation.4 | async-start | bytes 4194304 | tf_op jit(solution)/shard_map/all_to_all | solution.py:204
  215.0 3.1 convolution_multiply_fusion
  218.1 3.5 %select_reduce_fusion.2 = (f32[128]{0:T(128)S(1)}, f32[128,4096]{1,0:T(8,128)}) fusion(s32[4096]{0:T(1024)S(1)} %fusion.65, s32[128]{0:T(128)S(1)} %fusion.85, pred[4096]{0:T(1024)(128)(4,1)S(1)} %eq.148, s32[4096]{0:T(1024)S(1)} %convert_reduce_fusion.1, s32[128]{0:T(128)S(1)} %convert_reduce_fusion.5, bf16[4096,256]{1,0:T(8,128)(2,1)} %bitcast.25, ...), kind=kOutput, calls=%fused_computation.12 | convolution fusion | flops 137887616 | bytes 3216896 | tf_op jit(solution)/shard_map/qd,kd->qk/dot_general | solution.py:210
  221.6 21.7 %all-to-all-done.4 = bf16[16,2,128,256]{3,2,1,0:T(8,128)(2,1)} async-done(((bf16[16,2,128,256]{3,2,1,0:T(8,128)(2,1)}), bf16[16,2,128,256]{3,2,1,0:T(8,128)(2,1)}, u32[]{:S(2)}, u32[]{:S(2)}) %all-to-all-start.4) | async-done | bytes 2097184 | tf_op jit(solution)/shard_map/all_to_all | solution.py:204
  243.3 4.3 %fusion.2 = (f32[128]{0:T(128)S(1)}, f32[128]{0:T(128)S(1)}, f32[128]{0:T(128)S(1)}, f32[128,4096]{1,0:T(8,128)S(1)}) fusion(f32[128,4096]{1,0:T(8,128)} %get-tuple-element.44, f32[128]{0:T(128)S(1)} %get-tuple-element.43, s32[4096]{0:T(1024)S(1)} %fusion.65, s32[128]{0:T(128)S(1)} %fusion.85, pred[4096]{0:T(1024)(128)(4,1)S(1)} %eq.148, ...), kind=kOutput, calls=%fused_computation.14 | convolution fusion | flops 140508800 | bytes 7412736 | tf_op jit(solution)/shard_map/qd,kd->qk/dot_general | solution.py:210
  247.6 2.4 fusion.13
  250.0 1.4 fusion.4
  251.4 2.2 fusion.11
  253.7 2.2 fusion.12
  256.1 11.4 %all_to_all.93 = bf16[8,16,384]{2,1,0:T(8,128)(2,1)S(1)} all-to-all(bf16[8,16,384]{2,1,0:T(8,128)(2,1)S(1)} %all_to_all.75), channel_id=1, replica_groups=mesh['zl'=4,'core'=2,'y'=4,'zh'=2,'x'=4] {'zl','core'}, dimensions={0} | all-to-all | bytes 196608 | tf_op jit(solution)/shard_map/all_to_all | solution.py:220
  268.3 3.9 %all-to-all-start.7 = ((bf16[16,32,96]{2,0,1:T(8,128)(2,1)}), bf16[16,32,96]{2,0,1:T(8,128)(2,1)S(1)}, u32[]{:S(2)}, u32[]{:S(2)}) async-start(bf16[16,32,96]{2,0,1:T(8,128)(2,1)} %bitcast.37), calls=%async_computation.7 | async-start | bytes 262144 | tf_op jit(solution)/shard_map/all_to_all | solution.py:222
  272.2 8.8 %fusion.37 = f32[512,3072]{1,0:T(8,128)} fusion(bf16[384,3072]{1,0:T(8,128)(2,1)S(1)} %copy-done, bf16[512,3072]{1,0:T(8,128)(2,1)} %bitcast.95, bf16[3072,384]{1,0:T(8,128)(2,1)} %param.19), kind=kOutput, calls=%fused_computation.55 | convolution fusion | flops 2417688576 | bytes 14155776 | tf_op jit(solution)/shard_map/dot_general | solution.py:224
  281.0 4.6 %all-to-all-done.7 = bf16[16,32,96]{2,0,1:T(8,128)(2,1)S(1)} async-done(((bf16[16,32,96]{2,0,1:T(8,128)(2,1)}), bf16[16,32,96]{2,0,1:T(8,128)(2,1)S(1)}, u32[]{:S(2)}, u32[]{:S(2)}) %all-to-all-start.7) | async-done | bytes 98336 | tf_op jit(solution)/shard_map/all_to_all | solution.py:222
  285.6 4.0 %add_convert_fusion = bf16[512,3072]{1,0:T(8,128)(2,1)S(1)} fusion(f32[512,3072]{1,0:T(8,128)} %fusion.37, bf16[512,96]{1,0:T(8,128)(2,1)S(1)} %bitcast.104, bf16[96,3072]{1,0:T(8,128)(2,1)} %param.22), kind=kOutput, calls=%fused_computation.1 | convolution fusion | flops 305135616 | bytes 10125312 | tf_op jit(solution)/shard_map/dot_general | solution.py:226
  289.6 42.1 %all_to_all.94 = bf16[16,2,16,3072]{3,2,1,0:T(8,128)(2,1)S(1)} all-to-all(bf16[16,2,16,3072]{3,2,1,0:T(8,128)(2,1)S(1)} %bitcast.93), channel_id=1, replica_groups=mesh['zl'=4,'core'=2,'y'=4,'zh'=2,'x'=4] {'y','x'}, dimensions={0} | all-to-all | bytes 6291456 | tf_op jit(solution)/shard_map/all_to_all | solution.py:84
  332.3 4.8 %collective-permute-start.2 = (f32[16,3072]{1,0:T(8,128)S(1)}, f32[16,3072]{1,0:T(8,128)S(1)}, u32[]{:S(2)}, u32[]{:S(2)}) collective-permute-start(f32[16,3072]{1,0:T(8,128)S(1)} %select_bitcast_fusion), channel_id=1, source_target_pairs={{0,4},{4,0},{1,5},{5,1},{2,6},{6,2},{3,7},{7,3},{8,12},{12,8},{9,1... | collective-permute-start | bytes 589832 | tf_op jit(solution)/shard_map/ppermute | solution.py:87
  337.1 8.0 %collective-permute-done.2 = f32[16,3072]{1,0:T(8,128)S(1)} collective-permute-done((f32[16,3072]{1,0:T(8,128)S(1)}, f32[16,3072]{1,0:T(8,128)S(1)}, u32[]{:S(2)}, u32[]{:S(2)}) %collective-permute-start.2) | collective-permute-done | bytes 196640 | tf_op jit(solution)/shard_map/ppermute | solution.py:87
  345.1 0.7 fusion.47
  (84 shorter events, 10.1 us)
Async XLA Ops:
  0.0 272.2 %copy-start = (bf16[384,3072]{1,0:T(8,128)(2,1)S(1)}, bf16[384,3072]{1,0:T(8,128)(2,1)}, u32[]{:S(2)}) copy-start(bf16[384,3072]{1,0:T(8,128)(2,1)} %param.23) | copy-start | bytes 7077892
  0.0 15.7 %collective-permute-start = (f32[16,3072]{1,0:T(8,128)}, f32[16,3072]{1,0:T(8,128)S(1)}, u32[]{:S(2)}, u32[]{:S(2)}) collective-permute-start(f32[16,3072]{1,0:T(8,128)} %param.12), channel_id=1, source_target_pairs={{0,4},{4,0},{1,5},{5,1},{2,6},{6,2},{3,7},{7,3},{8,12},{12,8},{9,1... | collective-permute-start | bytes 589832 | tf_op jit(solution)/shard_map/ppermute | solution.py:118
  7.1 7.6 %copy-start.11 = (s32[4,1]{0,1:T(1,128)}, s32[4,1]{0,1:T(1,128)S(1)}, u32[]{:S(2)}) copy-start(s32[4,1]{0,1:T(1,128)S(1)} %reduce-window.8) | copy-start | bytes 52
  10.1 6.0 %copy-start.3 = (f32[16,3072]{1,0:T(8,128)S(1)}, f32[16,3072]{1,0:T(8,128)}, u32[]{:S(2)}) copy-start(f32[16,3072]{1,0:T(8,128)} %param.12) | copy-start | bytes 589828
  17.6 48.1 %copy-start.15 = (bf16[3072,288]{0,1:T(8,128)(2,1)S(1)}, bf16[3072,288]{0,1:T(8,128)(2,1)}, u32[]{:S(2)}) copy-start(bf16[3072,288]{0,1:T(8,128)(2,1)} %param.18) | copy-start | bytes 5308420
  64.1 1.7 copy-start.2
  65.8 9.0 %copy-start.13 = (f32[128]{0:T(128)S(1)}, f32[128]{0:T(128)}, u32[]{:S(2)}) copy-start(f32[128]{0:T(128)} %param.20) | copy-start | bytes 1540
  65.8 9.7 %copy-start.14 = (f32[128]{0:T(128)S(1)}, f32[128]{0:T(128)}, u32[]{:S(2)}) copy-start(f32[128]{0:T(128)} %param.21) | copy-start | bytes 1540
  67.8 22.3 %all-to-all-start.1 = ((bf16[32,16,288]{2,1,0:T(8,128)(2,1)}), bf16[32,16,288]{2,1,0:T(8,128)(2,1)S(1)}, u32[]{:S(2)}, u32[]{:S(2)}) async-start(bf16[32,16,288]{2,1,0:T(8,128)(2,1)} %bitcast.98), calls=%async_computation.1 | async-start | bytes 786432 | tf_op jit(solution)/shard_map/all_to_all | solution.py:156
  81.1 18.1 %copy-start.10 = (f32[128,3]{0,1:T(4,128)S(1)}, f32[128,3]{0,1:T(4,128)}, u32[]{:S(2)}) copy-start(f32[128,3]{0,1:T(4,128)} %convert_element_type.166) | copy-start | bytes 4612
  93.1 13.7 %all-to-all-start.2 = ((bf16[16,8,1152]{2,0,1:T(8,128)(2,1)}), bf16[16,8,1152]{2,0,1:T(8,128)(2,1)S(1)}, u32[]{:S(2)}, u32[]{:S(2)}) async-start(bf16[16,8,1152]{2,0,1:T(8,128)(2,1)} %copy.125), calls=%async_computation.2 | async-start | bytes 589824 | tf_op jit(solution)/shard_map/all_to_all | solution.py:158
  106.8 0.7 copy-start.4
  113.5 13.3 %collective-permute-start.1 = (bf16[128,3,2,128]{3,0,2,1:T(8,128)(2,1)}, bf16[128,3,2,128]{3,0,2,1:T(8,128)(2,1)S(1)}, u32[]{:S(2)}, u32[]{:S(2)}) collective-permute-start(bf16[128,3,2,128]{3,0,2,1:T(8,128)(2,1)} %copy.158), channel_id=1, source_target_pairs={{0,4},{4,0},{1,5},{5,1},{2,6},{6,2},{3,7},{7,3},{8,12},{12,8},{9,1... | collective-permute-start | bytes 589832 | tf_op jit(solution)/shard_map/ppermute | solution.py:180
  130.4 4.7 %copy-start.5 = (bf16[1,128,3,128]{1,3,2,0:T(8,128)(2,1)S(1)}, bf16[1,128,3,128]{1,3,2,0:T(8,128)(2,1)}, u32[]{:S(2)}) copy-start(bf16[1,128,3,128]{1,3,2,0:T(8,128)(2,1)} %copy.141) | copy-start | bytes 294916
  130.4 4.7 %copy-start.8 = (bf16[128,3,1,128]{0,3,1,2:T(8,128)(2,1)S(1)}, bf16[128,3,1,128]{0,3,1,2:T(8,128)(2,1)}, u32[]{:S(2)}) copy-start(bf16[128,3,1,128]{0,3,1,2:T(8,128)(2,1)} %copy.152) | copy-start | bytes 294916
  138.5 34.1 %all-to-all-start.5 = ((bf16[16,2,128,256]{3,2,1,0:T(8,128)(2,1)}), bf16[16,2,128,256]{3,2,1,0:T(8,128)(2,1)}, u32[]{:S(2)}, u32[]{:S(2)}) async-start(bf16[16,2,128,256]{3,2,1,0:T(8,128)(2,1)} %broadcast_in_dim.83), calls=%async_computation.5 | async-start | bytes 4194304 | tf_op jit(solution)/shard_map/all_to_all | solution.py:204
  174.2 33.7 %all-to-all-start.3 = ((bf16[16,2,128,256]{3,2,1,0:T(8,128)(2,1)}), bf16[16,2,128,256]{3,2,1,0:T(8,128)(2,1)}, u32[]{:S(2)}, u32[]{:S(2)}) async-start(bf16[16,2,128,256]{3,2,1,0:T(8,128)(2,1)} %broadcast_in_dim.77), calls=%async_computation.3 | async-start | bytes 4194304 | tf_op jit(solution)/shard_map/all_to_all | solution.py:204
  209.4 4.8 %copy-start.9 = (s32[4096]{0:T(1024)S(1)}, s32[4096]{0:T(1024)}, u32[]{:S(2)}) copy-start(s32[4096]{0:T(1024)} %param.13) | copy-start | bytes 49156
  209.4 5.1 %copy-start.12 = (s32[4,1]{0,1:T(1,128)S(1)}, s32[4,1]{0,1:T(1,128)}, u32[]{:S(2)}) copy-start(s32[4,1]{0,1:T(1,128)} %copy-done.11) | copy-start | bytes 52
  209.4 5.3 %copy-start.6 = (bf16[128,3,64,1]{0,3,2,1:T(2,128)(2,1)S(1)}, bf16[128,3,64,1]{0,3,2,1:T(2,128)(2,1)}, u32[]{:S(2)}) copy-start(bf16[128,3,64,1]{0,3,2,1:T(2,128)(2,1)} %get-tuple-element.27) | copy-start | bytes 147460
  209.4 5.3 %copy-start.7 = (bf16[128,3,64,1]{0,3,2,1:T(2,128)(2,1)S(1)}, bf16[128,3,64,1]{0,3,2,1:T(2,128)(2,1)}, u32[]{:S(2)}) copy-start(bf16[128,3,64,1]{0,3,2,1:T(2,128)(2,1)} %get-tuple-element.28) | copy-start | bytes 147460
  209.4 33.9 %all-to-all-start.4 = ((bf16[16,2,128,256]{3,2,1,0:T(8,128)(2,1)}), bf16[16,2,128,256]{3,2,1,0:T(8,128)(2,1)}, u32[]{:S(2)}, u32[]{:S(2)}) async-start(bf16[16,2,128,256]{3,2,1,0:T(8,128)(2,1)} %broadcast_in_dim.81), calls=%async_computation.4 | async-start | bytes 4194304 | tf_op jit(solution)/shard_map/all_to_all | solution.py:204
  243.3 4.3 %copy-start.16 = (f32[128,4096]{1,0:T(8,128)S(1)}, f32[128,4096]{1,0:T(8,128)}, u32[]{:S(2)}) copy-start(f32[128,4096]{1,0:T(8,128)} %get-tuple-element.44) | copy-start | bytes 6291460
  247.6 2.4 copy-start.1
  268.3 17.3 %all-to-all-start.7 = ((bf16[16,32,96]{2,0,1:T(8,128)(2,1)}), bf16[16,32,96]{2,0,1:T(8,128)(2,1)S(1)}, u32[]{:S(2)}, u32[]{:S(2)}) async-start(bf16[16,32,96]{2,0,1:T(8,128)(2,1)} %bitcast.37), calls=%async_computation.7 | async-start | bytes 262144 | tf_op jit(solution)/shard_map/all_to_all | solution.py:222
  332.3 12.8 %collective-permute-start.2 = (f32[16,3072]{1,0:T(8,128)S(1)}, f32[16,3072]{1,0:T(8,128)S(1)}, u32[]{:S(2)}, u32[]{:S(2)}) collective-permute-start(f32[16,3072]{1,0:T(8,128)S(1)} %select_bitcast_fusion), channel_id=1, source_target_pairs={{0,4},{4,0},{1,5},{5,1},{2,6},{6,2},{3,7},{7,3},{8,12},{12,8},{9,1... | collective-permute-start | bytes 589832 | tf_op jit(solution)/shard_map/ppermute | solution.py:87

commit v6 on v5

--- a/solution.py
+++ b/solution.py
@@ -155,20 +155,23 @@
     ys, xs = lax.axis_size("y"), lax.axis_size("x")
     by_token = lax.all_to_all(qkv_cols, ("y", "x", "zh"), split_axis=0, concat_axis=1, tiled=True)
     by_token = by_token.reshape(block_rows, ys, xs, 2, -1).swapaxes(2, 3).reshape(block_rows, -1)
-    heads_in = lax.all_to_all(by_token, SEQ, split_axis=1, concat_axis=0, tiled=True)
+    group = ("zl", "zh")
+    heads_in = lax.all_to_all(by_token, group, split_axis=1, concat_axis=0, tiled=True)
     query_rows = heads_in.shape[0]
     heads4 = heads_in.reshape(query_rows, local_heads, 3, head_size)
-    query_ids = spread_rows(
-        blk_at * query_rows + jnp.arange(query_rows, dtype=jnp.int32),
-        query_rows,
-        block_rows,
-        tok_seq,
-    )
+    core_at, y_at, x_at = lax.axis_index("core"), lax.axis_index("y"), lax.axis_index("x")
+    digits = (lax.axis_size("zl"), 2, ys, 2, xs, block_rows)
+    token_grid = jnp.arange(seq_count * tok_seq, dtype=jnp.int32).reshape(digits)
+
+    def own_queries(grid):
+        grid = lax.dynamic_index_in_dim(grid, core_at, axis=1, keepdims=False)
+        grid = lax.dynamic_index_in_dim(grid, y_at, axis=1, keepdims=False)
+        grid = lax.dynamic_index_in_dim(grid, x_at, axis=2, keepdims=False)
+        return grid.reshape((query_rows,) + grid.shape[3:])
+
+    query_ids = own_queries(token_grid)
     query_request = segment_of(query_ids, request_ends)
-    query_places = lax.dynamic_index_in_dim(
-        positions.reshape(seq_count, blk_count, block_rows, -1), blk_at, axis=1, keepdims=False
-    ).reshape(query_rows, -1)
-    angles = angles_of(query_places, rope_table(head_size))
+    angles = angles_of(own_queries(positions.reshape(digits + (-1,))), rope_table(head_size))
     query_rot = rotate(rms_scale(heads4[:, :, 0].astype(jnp.float32), q_gain), angles).astype(
         jnp.bfloat16
     )
@@ -177,35 +180,25 @@
     )
     value_rows = heads4[:, :, 2]
     kv_rows = jnp.concatenate([key_rot, value_rows], axis=2)
-    partner_raw = lax.ppermute(heads4[:, :, 1:], "zh", SWAP)
-    partner_places = lax.dynamic_index_in_dim(
-        positions.reshape(seq_count, blk_count, block_rows, -1), partner_blk, axis=1, keepdims=False
-    ).reshape(query_rows, -1)
-    partner_key = rotate(
-        rms_scale(partner_raw[:, :, 0].astype(jnp.float32), k_gain),
-        angles_of(partner_places, rope_table(head_size)),
-    ).astype(jnp.bfloat16)
-    partner_rows = jnp.concatenate([partner_key, partner_raw[:, :, 1]], axis=2)
-    kv_pair = jnp.stack(by_half(kv_rows, partner_rows))
-    key_rank = jnp.arange(seq_count * tok_seq, dtype=jnp.int32)
-    key_y = key_rank // (xs * 2 * query_rows)
-    key_x = key_rank // (2 * query_rows) % xs
-    key_zh = key_rank // query_rows % 2
-    key_owner = (key_y * 2 + key_zh) * xs + key_x
-    key_ids = key_rank // block_rows % seq_count * tok_seq + key_owner * block_rows + key_rank % block_rows
+    key_order = (1, 2, 4, 0, 3, 5)
+    key_ids = token_grid.transpose(key_order).reshape(-1)
     key_request = segment_of(key_ids, request_ends)
-    kept = key_keep.reshape(seq_count, ys, 2, xs, block_rows).transpose(1, 3, 2, 0, 4).reshape(-1) == 1
+    kept = key_keep.reshape(digits).transpose(key_order).reshape(-1) == 1
     visible = (query_request[:, None] == key_request[None, :]) & (
         kept[None, :] | (query_ids[:, None] == key_ids[None, :])
     )
+    first_core = core_at == 0
     head_out = []
     for head in range(local_heads):
-        piece = kv_pair[:, :, head]
+        piece = kv_rows[:, head]
         got = lax.all_to_all(
             jnp.broadcast_to(piece[None], (ys * xs,) + piece.shape), PLANE, 0, 0, tiled=True
-        ).reshape(-1, 2 * head_size)
-        key_h = got[:, :head_size]
-        value_h = got[:, head_size:]
+        )
+        sibling = lax.ppermute(got, "core", SWAP)
+        both = jnp.stack([jnp.where(first_core, got, sibling), jnp.where(first_core, sibling, got)])
+        both = both.reshape(-1, 2 * head_size)
+        key_h = both[:, :head_size]
+        value_h = both[:, head_size:]
         scores = (
             jnp.einsum("qd,kd->qk", query_rot[:, head], key_h, preferred_element_type=jnp.float32)
             * inv_root
@@ -217,7 +210,7 @@
         head_out.append((mixed / totals[:, None]).astype(jnp.bfloat16))
     attended = jnp.stack(head_out, axis=1)
     attended = attended.reshape(query_rows, local_heads * head_size)
-    attn_feats = lax.all_to_all(attended, SEQ, split_axis=0, concat_axis=1, tiled=True)
+    attn_feats = lax.all_to_all(attended, group, split_axis=0, concat_axis=1, tiled=True)
     attn_feats = attn_feats.reshape(block_rows, ys, 2, xs, -1).swapaxes(2, 3).reshape(block_rows, -1)
     attn_local = lax.all_to_all(attn_feats, ("y", "x", "zh"), split_axis=1, concat_axis=0, tiled=True)
     mlp_out = lax.optimization_barrier(

time: 347 us -> 273 us (0.79)
  waiting for transfers between devices: 120 us -> 69.9 us
  local copies, waits for them, and re-layouts: 27.8 us -> 13.3 us
  matrix products: 36.1 us -> 24.5 us
    all_to_all x3, waiting for transfers between devices: 80.4 us -> 36.7 us  [body(): lax.all_to_all(jnp.broadcast_to(piece[None], (ys * xs,) + piece.shape), P...]
    ppermute x1 -> x3, waiting for transfers between devices: 10.8 us -> 0.01 us  [body(): sibling = lax.ppermute(got, 'core', SWAP)]
    dot_general x3, matrix products: 10.9 us -> 3.23 us  [body(): jnp.einsum('qd,kd->qk', query_rot[:, head], key_h, preferred_element_type...]
    all_to_all x1, waiting for transfers between devices: 8.39 us -> 14.5 us  [body(): lax.all_to_all(qkv_cols, ('y', 'x', 'zh'), split_axis=0, concat_axis=1, t...]
    dot_general x3, matrix products: 6.79 us -> 2.96 us  [body(): jnp.dot(weights.astype(jnp.bfloat16), value_h, preferred_element_type=jnp...]
    another operation x4 -> x8, other arithmetic: 4.76 us -> 7.04 us  [the longest x6 5 us: body(): jnp.stack([jnp.where(first_core, got, sibling), jnp.where(first_core, sib...]
  transfers between devices with their start and end apart: 9 -> 11, of which waited for: 9 -> 8; matrix products, arithmetic and copies ran while one was open for 10% -> 10% of each run, Pallas kernels for 0% -> 0%
where the time goes in v6:
time: 273 us; the launch traced here: 270 us
  blocking collectives  100 us (37%)
  waiting for transfers between devices  69.9 us (26%)
  starting transfers between devices  41.9 us (15%)
  matrix products  24.5 us (9%)
  other arithmetic  19.7 us (7%)
  local copies, waits for them, and re-layouts  13.3 us (5%)
    all_to_all x1, blocking collectives, gather_plane(): lax.all_to_all(jnp.broadcast_to(pair[None], (plane,) + pair.shape), PLANE...  46.4 us
    all_to_all x1, blocking collectives, reduce_blk(): got = lax.all_to_all(pieces, PLANE, 0, 0, tiled=True)  42.1 us
    all_to_all x3, waiting for transfers between devices, body(): lax.all_to_all(jnp.broadcast_to(piece[None], (ys * xs,) + piece.shape), P...  36.7 us
    all_to_all x1, waiting for transfers between devices, body(): lax.all_to_all(qkv_cols, ('y', 'x', 'zh'), split_axis=0, concat_axis=1, t...  14.5 us
    all_to_all x3, starting transfers between devices, body(): lax.all_to_all(jnp.broadcast_to(piece[None], (ys * xs,) + piece.shape), P...  12.3 us
    all_to_all x1, blocking collectives, body(): lax.all_to_all(attended, group, split_axis=0, concat_axis=1, tiled=True)  11.9 us
    dot_general x1, matrix products, body(): jnp.dot(mlp_act, w_mlp_out, preferred_element_type=jnp.float32)  8.86 us
    all_to_all x1, waiting for transfers between devices, body(): lax.all_to_all(by_token, group, split_axis=1, concat_axis=0, tiled=True)  8.75 us
  transfers between devices with their start and end apart: 11, of which 8 were waited for; matrix products, arithmetic and copies ran while one was open for 10% of the time, Pallas kernels for 0%

profile of v6, /device:TPU:32, one launch (start us, length us, event | category | flops | bytes accessed | tf_op | source)
XLA Modules:
  0.0 270.3 jit_solution(14748614455475708779)
XLA Ops:
  0.0 6.3 %collective-permute-start = (f32[16,3072]{1,0:T(8,128)}, f32[16,3072]{1,0:T(8,128)S(1)}, u32[]{:S(2)}, u32[]{:S(2)}) collective-permute-start(f32[16,3072]{1,0:T(8,128)} %param.12), channel_id=1, source_target_pairs={{0,4},{4,0},{1,5},{5,1},{2,6},{6,2},{3,7},{7,3},{8,12},{12,8},{9,1... | collective-permute-start | bytes 589832 | tf_op jit(solution)/shard_map/ppermute | solution.py:118
  6.3 0.8 reduce-window.8
  7.1 0.7 fusion.63
  7.8 1.1 reduce_sum.139
  8.9 1.1 multiply_reduce_fusion.3
  10.1 2.9 %fusion = f32[4,1,9216]{2,1,0:T(1,128)S(1)} fusion(bf16[4,28,9216]{2,0,1:T(4,128)(2,1)} %bitcast.104, pred[4,28,1]{1,0,2:T(4,128)(4,1)S(1)} %fusion.63), kind=kOutput, calls=%fused_computation.5 | convolution fusion | flops 2064384 | bytes 2211952 | tf_op jit(solution)/shard_map/rs,rsk->rk/dot_general | solution.py:122
  13.0 0.4 fusion.50
  13.5 1.3 fusion.48
  14.7 0.9 collective-permute-done
  15.8 0.2 multiply_reduce_fusion.2
  16.0 1.2 select_bitcast_fusion.8
  17.3 0.4 broadcast_in_dim.64
  17.7 46.4 %all_to_all.92 = bf16[16,2,16,3072]{3,2,1,0:T(8,128)(2,1)S(1)} all-to-all(bf16[16,2,16,3072]{3,2,1,0:T(8,128)(2,1)S(1)} %broadcast_in_dim.64), channel_id=1, replica_groups=mesh['zl'=4,'core'=2,'y'=4,'zh'=2,'x'=4] {'y','x'}, dimensions={0} | all-to-all | bytes 6291456 | tf_op jit(solution)/shard_map/all_to_all | solution.py:77
  64.1 1.7 copy-done.1
  65.8 1.1 convolution_convert_fusion
  66.9 0.9 copy.86
  67.8 7.0 %all-to-all-start.1 = ((bf16[32,16,288]{2,1,0:T(8,128)(2,1)}), bf16[32,16,288]{2,1,0:T(8,128)(2,1)S(1)}, u32[]{:S(2)}, u32[]{:S(2)}) async-start(bf16[32,16,288]{2,1,0:T(8,128)(2,1)} %bitcast.9), calls=%async_computation.1 | async-start | bytes 786432 | tf_op jit(solution)/shard_map/all_to_all | solution.py:156
  75.1 0.3 reshape.491
  75.6 14.5 %all-to-all-done.1 = bf16[32,16,288]{2,1,0:T(8,128)(2,1)S(1)} async-done(((bf16[32,16,288]{2,1,0:T(8,128)(2,1)}), bf16[32,16,288]{2,1,0:T(8,128)(2,1)S(1)}, u32[]{:S(2)}, u32[]{:S(2)}) %all-to-all-start.1) | async-done | bytes 294944 | tf_op jit(solution)/shard_map/all_to_all | solution.py:156
  90.3 0.3 all_to_all.69
  90.6 0.7 copy.88
  91.3 5.4 %all-to-all-start.2 = ((bf16[16,8,1152]{2,0,1:T(8,128)(2,1)}), bf16[16,8,1152]{2,0,1:T(8,128)(2,1)S(1)}, u32[]{:S(2)}, u32[]{:S(2)}) async-start(bf16[16,8,1152]{2,0,1:T(8,128)(2,1)} %copy.88), calls=%async_computation.2 | async-start | bytes 589824 | tf_op jit(solution)/shard_map/all_to_all | solution.py:159
  97.0 8.7 %all-to-all-done.2 = bf16[16,8,1152]{2,0,1:T(8,128)(2,1)S(1)} async-done(((bf16[16,8,1152]{2,0,1:T(8,128)(2,1)}), bf16[16,8,1152]{2,0,1:T(8,128)(2,1)S(1)}, u32[]{:S(2)}, u32[]{:S(2)}) %all-to-all-start.2) | async-done | bytes 294944 | tf_op jit(solution)/shard_map/all_to_all | solution.py:159
  105.8 0.4 fusion.80
  107.3 1.2 subtract_convert_fusion.1
  108.5 0.2 pad_maximum_fusion.5
  108.7 0.6 fusion.54
  109.5 1.1 broadcast_in_dim.66
  110.6 3.7 %all-to-all-start.3 = ((bf16[16,128,256]{2,1,0:T(8,128)(2,1)}), bf16[16,128,256]{2,1,0:T(8,128)(2,1)S(1)}, u32[]{:S(2)}, u32[]{:S(2)}) async-start(bf16[16,128,256]{2,1,0:T(8,128)(2,1)} %broadcast_in_dim.66), calls=%async_computation.3 | async-start | bytes 2097152 | tf_op jit(solution)/shard_map/all_to_all | solution.py:194
  114.2 0.9 copy.102
  115.2 13.7 %all-to-all-done.3 = bf16[16,128,256]{2,1,0:T(8,128)(2,1)S(1)} async-done(((bf16[16,128,256]{2,1,0:T(8,128)(2,1)}), bf16[16,128,256]{2,1,0:T(8,128)(2,1)S(1)}, u32[]{:S(2)}, u32[]{:S(2)}) %all-to-all-start.3) | async-done | bytes 1048608 | tf_op jit(solution)/shard_map/all_to_all | solution.py:194
  128.9 1.1 broadcast_in_dim.70
  130.0 4.3 %all-to-all-start.4 = ((bf16[16,128,256]{2,1,0:T(8,128)(2,1)}), bf16[16,128,256]{2,1,0:T(8,128)(2,1)}, u32[]{:S(2)}, u32[]{:S(2)}) async-start(bf16[16,128,256]{2,1,0:T(8,128)(2,1)} %broadcast_in_dim.70), calls=%async_computation.4 | async-start | bytes 2097152 | tf_op jit(solution)/shard_map/all_to_all | solution.py:194
  134.5 13.9 %all-to-all-done.4 = bf16[16,128,256]{2,1,0:T(8,128)(2,1)} async-done(((bf16[16,128,256]{2,1,0:T(8,128)(2,1)}), bf16[16,128,256]{2,1,0:T(8,128)(2,1)}, u32[]{:S(2)}, u32[]{:S(2)}) %all-to-all-start.4) | async-done | bytes 1048608 | tf_op jit(solution)/shard_map/all_to_all | solution.py:194
  148.3 1.1 broadcast_in_dim.123
  149.4 4.3 %all-to-all-start.5 = ((bf16[16,128,256]{2,1,0:T(8,128)(2,1)}), bf16[16,128,256]{2,1,0:T(8,128)(2,1)}, u32[]{:S(2)}, u32[]{:S(2)}) async-start(bf16[16,128,256]{2,1,0:T(8,128)(2,1)} %broadcast_in_dim.123), calls=%async_computation.5 | async-start | bytes 2097152 | tf_op jit(solution)/shard_map/all_to_all | solution.py:194
  153.9 0.6 collective-permute-start.1
  154.5 0.7 ge.27
  155.3 0.7 eq.130
  156.3 0.8 convert_reduce_fusion.4
  157.1 0.7 convert_reduce_fusion.1
  157.8 9.2 %all-to-all-done.5 = bf16[16,128,256]{2,1,0:T(8,128)(2,1)} async-done(((bf16[16,128,256]{2,1,0:T(8,128)(2,1)}), bf16[16,128,256]{2,1,0:T(8,128)(2,1)}, u32[]{:S(2)}, u32[]{:S(2)}) %all-to-all-start.5) | async-done | bytes 1048608 | tf_op jit(solution)/shard_map/all_to_all | solution.py:194
  167.0 1.2 pad_maximum_fusion.4
  168.1 1.7 select_bitcast_fusion.3
  170.0 1.4 select_bitcast_fusion.5
  171.6 1.4 select_bitcast_fusion.1
  173.2 0.5 convolution_multiply_fusion
  173.9 1.0 select_reduce_fusion.2
  174.9 1.7 fusion.2
  176.7 1.0 fusion.13
  177.7 1.4 fusion.4
  179.1 1.0 fusion.11
  180.1 1.0 fusion.12
  181.3 11.9 %all_to_all.93 = bf16[8,16,384]{2,1,0:T(8,128)(2,1)S(1)} all-to-all(bf16[8,16,384]{2,1,0:T(8,128)(2,1)S(1)} %all_to_all.75), channel_id=1, replica_groups=mesh['zl'=4,'core'=2,'y'=4,'zh'=2,'x'=4] {'zl','zh'}, dimensions={0} | all-to-all | bytes 196608 | tf_op jit(solution)/shard_map/all_to_all | solution.py:213
  193.3 0.7 copy.106
  194.0 4.8 %all-to-all-start.7 = ((bf16[16,32,96]{2,0,1:T(8,128)(2,1)}), bf16[16,32,96]{2,0,1:T(8,128)(2,1)S(1)}, u32[]{:S(2)}, u32[]{:S(2)}) async-start(bf16[16,32,96]{2,0,1:T(8,128)(2,1)} %bitcast.40), calls=%async_computation.7 | async-start | bytes 262144 | tf_op jit(solution)/shard_map/all_to_all | solution.py:215
  198.8 8.9 %fusion.37 = f32[512,3072]{1,0:T(8,128)} fusion(bf16[384,3072]{1,0:T(8,128)(2,1)S(1)} %copy-done, bf16[512,3072]{1,0:T(8,128)(2,1)} %bitcast.103, bf16[3072,384]{1,0:T(8,128)(2,1)} %param.19), kind=kOutput, calls=%fused_computation.60 | convolution fusion | flops 2417688576 | bytes 14155776 | tf_op jit(solution)/shard_map/dot_general | solution.py:217
  207.7 3.5 %all-to-all-done.7 = bf16[16,32,96]{2,0,1:T(8,128)(2,1)S(1)} async-done(((bf16[16,32,96]{2,0,1:T(8,128)(2,1)}), bf16[16,32,96]{2,0,1:T(8,128)(2,1)S(1)}, u32[]{:S(2)}, u32[]{:S(2)}) %all-to-all-start.7) | async-done | bytes 98336 | tf_op jit(solution)/shard_map/all_to_all | solution.py:215
  211.2 3.7 %add_convert_fusion = bf16[512,3072]{1,0:T(8,128)(2,1)S(1)} fusion(f32[512,3072]{1,0:T(8,128)} %fusion.37, bf16[512,96]{1,0:T(8,128)(2,1)S(1)} %bitcast.114, bf16[96,3072]{1,0:T(8,128)(2,1)S(1)} %copy-done.5), kind=kOutput, calls=%fused_computation.1 | convolution fusion | flops 305135616 | bytes 10125312 | tf_op jit(solution)/shard_map/dot_general | solution.py:219
  215.0 42.1 %all_to_all.94 = bf16[16,2,16,3072]{3,2,1,0:T(8,128)(2,1)S(1)} all-to-all(bf16[16,2,16,3072]{3,2,1,0:T(8,128)(2,1)S(1)} %bitcast.99), channel_id=1, replica_groups=mesh['zl'=4,'core'=2,'y'=4,'zh'=2,'x'=4] {'y','x'}, dimensions={0} | all-to-all | bytes 6291456 | tf_op jit(solution)/shard_map/all_to_all | solution.py:84
  257.1 0.6 convert_reduce_fusion
  257.7 5.5 %collective-permute-start.4 = (f32[16,3072]{1,0:T(8,128)S(1)}, f32[16,3072]{1,0:T(8,128)S(1)}, u32[]{:S(2)}, u32[]{:S(2)}) collective-permute-start(f32[16,3072]{1,0:T(8,128)S(1)} %select_bitcast_fusion.6), channel_id=1, source_target_pairs={{0,4},{4,0},{1,5},{5,1},{2,6},{6,2},{3,7},{7,3},{8,12},{12,8},{9,1... | collective-permute-start | bytes 589832 | tf_op jit(solution)/shard_map/ppermute | solution.py:87
  263.1 5.5 %collective-permute-done.4 = f32[16,3072]{1,0:T(8,128)S(1)} collective-permute-done((f32[16,3072]{1,0:T(8,128)S(1)}, f32[16,3072]{1,0:T(8,128)S(1)}, u32[]{:S(2)}, u32[]{:S(2)}) %collective-permute-start.4) | collective-permute-done | bytes 196640 | tf_op jit(solution)/shard_map/ppermute | solution.py:87
  268.6 1.7 fusion.47
  (79 shorter events, 4.1 us)
Async XLA Ops:
  0.0 198.8 %copy-start = (bf16[384,3072]{1,0:T(8,128)(2,1)S(1)}, bf16[384,3072]{1,0:T(8,128)(2,1)}, u32[]{:S(2)}) copy-start(bf16[384,3072]{1,0:T(8,128)(2,1)} %param.23) | copy-start | bytes 7077892
  0.0 15.7 %collective-permute-start = (f32[16,3072]{1,0:T(8,128)}, f32[16,3072]{1,0:T(8,128)S(1)}, u32[]{:S(2)}, u32[]{:S(2)}) collective-permute-start(f32[16,3072]{1,0:T(8,128)} %param.12), channel_id=1, source_target_pairs={{0,4},{4,0},{1,5},{5,1},{2,6},{6,2},{3,7},{7,3},{8,12},{12,8},{9,1... | collective-permute-start | bytes 589832 | tf_op jit(solution)/shard_map/ppermute | solution.py:118
  7.1 5.9 %copy-start.9 = (s32[4,1]{0,1:T(1,128)}, s32[4,1]{0,1:T(1,128)S(1)}, u32[]{:S(2)}) copy-start(s32[4,1]{0,1:T(1,128)S(1)} %reduce-window.8) | copy-start | bytes 52
  10.1 6.0 %copy-start.2 = (f32[16,3072]{1,0:T(8,128)S(1)}, f32[16,3072]{1,0:T(8,128)}, u32[]{:S(2)}) copy-start(f32[16,3072]{1,0:T(8,128)} %param.12) | copy-start | bytes 589828
  13.5 4.2 %copy-start.4 = (f32[16,9216]{1,0:T(8,128)}, f32[16,9216]{1,0:T(8,128)S(1)}, u32[]{:S(2)}) copy-start(f32[16,9216]{1,0:T(8,128)S(1)} %fusion.50) | copy-start | bytes 1769476
  17.7 48.1 %copy-start.13 = (bf16[3072,288]{0,1:T(8,128)(2,1)S(1)}, bf16[3072,288]{0,1:T(8,128)(2,1)}, u32[]{:S(2)}) copy-start(bf16[3072,288]{0,1:T(8,128)(2,1)} %param.18) | copy-start | bytes 5308420
  64.1 1.7 copy-start.1
  65.8 9.0 %copy-start.11 = (f32[128]{0:T(128)S(1)}, f32[128]{0:T(128)}, u32[]{:S(2)}) copy-start(f32[128]{0:T(128)} %param.20) | copy-start | bytes 1540
  65.8 9.2 %copy-start.12 = (f32[128]{0:T(128)S(1)}, f32[128]{0:T(128)}, u32[]{:S(2)}) copy-start(f32[128]{0:T(128)} %param.21) | copy-start | bytes 1540
  65.8 9.3 %copy-start.6 = (s32[4096,3]{0,1:T(4,128)S(1)}, s32[4096,3]{0,1:T(4,128)}, u32[]{:S(2)}) copy-start(s32[4096,3]{0,1:T(4,128)} %param.14) | copy-start | bytes 147460
  67.8 22.3 %all-to-all-start.1 = ((bf16[32,16,288]{2,1,0:T(8,128)(2,1)}), bf16[32,16,288]{2,1,0:T(8,128)(2,1)S(1)}, u32[]{:S(2)}, u32[]{:S(2)}) async-start(bf16[32,16,288]{2,1,0:T(8,128)(2,1)} %bitcast.9), calls=%async_computation.1 | async-start | bytes 786432 | tf_op jit(solution)/shard_map/all_to_all | solution.py:156
  91.3 14.4 %all-to-all-start.2 = ((bf16[16,8,1152]{2,0,1:T(8,128)(2,1)}), bf16[16,8,1152]{2,0,1:T(8,128)(2,1)S(1)}, u32[]{:S(2)}, u32[]{:S(2)}) async-start(bf16[16,8,1152]{2,0,1:T(8,128)(2,1)} %copy.88), calls=%async_computation.2 | async-start | bytes 589824 | tf_op jit(solution)/shard_map/all_to_all | solution.py:159
  110.6 18.3 %all-to-all-start.3 = ((bf16[16,128,256]{2,1,0:T(8,128)(2,1)}), bf16[16,128,256]{2,1,0:T(8,128)(2,1)S(1)}, u32[]{:S(2)}, u32[]{:S(2)}) async-start(bf16[16,128,256]{2,1,0:T(8,128)(2,1)} %broadcast_in_dim.66), calls=%async_computation.3 | async-start | bytes 2097152 | tf_op jit(solution)/shard_map/all_to_all | solution.py:194
  130.0 18.3 %all-to-all-start.4 = ((bf16[16,128,256]{2,1,0:T(8,128)(2,1)}), bf16[16,128,256]{2,1,0:T(8,128)(2,1)}, u32[]{:S(2)}, u32[]{:S(2)}) async-start(bf16[16,128,256]{2,1,0:T(8,128)(2,1)} %broadcast_in_dim.70), calls=%async_computation.4 | async-start | bytes 2097152 | tf_op jit(solution)/shard_map/all_to_all | solution.py:194
  134.4 19.5 %copy-start.8 = (s32[4096]{0:T(1024)S(1)}, s32[4096]{0:T(1024)}, u32[]{:S(2)}) copy-start(s32[4096]{0:T(1024)} %param.13) | copy-start | bytes 49156
  149.4 17.5 %all-to-all-start.5 = ((bf16[16,128,256]{2,1,0:T(8,128)(2,1)}), bf16[16,128,256]{2,1,0:T(8,128)(2,1)}, u32[]{:S(2)}, u32[]{:S(2)}) async-start(bf16[16,128,256]{2,1,0:T(8,128)(2,1)} %broadcast_in_dim.123), calls=%async_computation.5 | async-start | bytes 2097152 | tf_op jit(solution)/shard_map/all_to_all | solution.py:194
  153.8 14.4 %collective-permute-start.2 = (bf16[16,128,256]{2,1,0:T(8,128)(2,1)}, bf16[16,128,256]{2,1,0:T(8,128)(2,1)}, u32[]{:S(2)}, u32[]{:S(2)}) collective-permute-start(bf16[16,128,256]{2,1,0:T(8,128)(2,1)} %all-to-all-done.4), channel_id=1, source_target_pairs={{0,32},{32,0},{1,33},{33,1},{2,34},{34,2},{3,35},{35,3},{4,36},{36... | collective-permute-start | bytes 3145736 | tf_op jit(solution)/shard_map/ppermute | solution.py:197
  153.9 16.1 %collective-permute-start.1 = (bf16[16,128,256]{2,1,0:T(8,128)(2,1)S(1)}, bf16[16,128,256]{2,1,0:T(8,128)(2,1)}, u32[]{:S(2)}, u32[]{:S(2)}) collective-permute-start(bf16[16,128,256]{2,1,0:T(8,128)(2,1)S(1)} %all-to-all-done.3), channel_id=1, source_target_pairs={{0,32},{32,0},{1,33},{33,1},{2,34},{34,2},{3,35},{35,3},{4,36},{36... | collective-permute-start | bytes 3145736 | tf_op jit(solution)/shard_map/ppermute | solution.py:197
  167.0 4.7 %collective-permute-start.3 = (bf16[16,128,256]{2,1,0:T(8,128)(2,1)}, bf16[16,128,256]{2,1,0:T(8,128)(2,1)S(1)}, u32[]{:S(2)}, u32[]{:S(2)}) collective-permute-start(bf16[16,128,256]{2,1,0:T(8,128)(2,1)} %all-to-all-done.5), channel_id=1, source_target_pairs={{0,32},{32,0},{1,33},{33,1},{2,34},{34,2},{3,35},{35,3},{4,36},{36... | collective-permute-start | bytes 3145736 | tf_op jit(solution)/shard_map/ppermute | solution.py:197
  173.2 0.7 copy-start.7
  173.2 0.7 copy-start.10
  194.0 17.2 %all-to-all-start.7 = ((bf16[16,32,96]{2,0,1:T(8,128)(2,1)}), bf16[16,32,96]{2,0,1:T(8,128)(2,1)S(1)}, u32[]{:S(2)}, u32[]{:S(2)}) async-start(bf16[16,32,96]{2,0,1:T(8,128)(2,1)} %bitcast.40), calls=%async_computation.7 | async-start | bytes 262144 | tf_op jit(solution)/shard_map/all_to_all | solution.py:215
  198.8 12.4 %copy-start.5 = (bf16[96,3072]{1,0:T(8,128)(2,1)S(1)}, bf16[96,3072]{1,0:T(8,128)(2,1)}, u32[]{:S(2)}) copy-start(bf16[96,3072]{1,0:T(8,128)(2,1)} %param.22) | copy-start | bytes 1769476
  257.1 11.6 %copy-start.3 = (f32[16,3072]{1,0:T(8,128)S(1)}, f32[16,3072]{1,0:T(8,128)}, u32[]{:S(2)}) copy-start(f32[16,3072]{1,0:T(8,128)} %param.12) | copy-start | bytes 589828
  257.7 11.0 %collective-permute-start.4 = (f32[16,3072]{1,0:T(8,128)S(1)}, f32[16,3072]{1,0:T(8,128)S(1)}, u32[]{:S(2)}, u32[]{:S(2)}) collective-permute-start(f32[16,3072]{1,0:T(8,128)S(1)} %select_bitcast_fusion.6), channel_id=1, source_target_pairs={{0,4},{4,0},{1,5},{5,1},{2,6},{6,2},{3,7},{7,3},{8,12},{12,8},{9,1... | collective-permute-start | bytes 589832 | tf_op jit(solution)/shard_map/ppermute | solution.py:87

commit v7 on v6

--- a/solution.py
+++ b/solution.py
@@ -153,10 +153,11 @@
     qkv_cols = joined[:, :qkv_width]
     mlp_act = joined[:, qkv_width:]
     ys, xs = lax.axis_size("y"), lax.axis_size("x")
-    by_token = lax.all_to_all(qkv_cols, ("y", "x", "zh"), split_axis=0, concat_axis=1, tiled=True)
-    by_token = by_token.reshape(block_rows, ys, xs, 2, -1).swapaxes(2, 3).reshape(block_rows, -1)
-    group = ("zl", "zh")
-    heads_in = lax.all_to_all(by_token, group, split_axis=1, concat_axis=0, tiled=True)
+    zl_count = lax.axis_size("zl")
+    flip = [(a * ys + b, b * zl_count + a) for a in range(zl_count) for b in range(ys)]
+    quarters = lax.all_to_all(qkv_cols.reshape(xs, -1, qkv_cols.shape[1]), "x", 0, 0, tiled=True)
+    quarters = quarters.swapaxes(0, 1).reshape(quarters.shape[1], -1)
+    heads_in = lax.ppermute(quarters, ("zl", "y"), flip)
     query_rows = heads_in.shape[0]
     heads4 = heads_in.reshape(query_rows, local_heads, 3, head_size)
     core_at, y_at, x_at = lax.axis_index("core"), lax.axis_index("y"), lax.axis_index("x")
@@ -164,10 +165,10 @@
     token_grid = jnp.arange(seq_count * tok_seq, dtype=jnp.int32).reshape(digits)
 
     def own_queries(grid):
+        grid = lax.dynamic_index_in_dim(grid, x_at, axis=2, keepdims=False)
         grid = lax.dynamic_index_in_dim(grid, core_at, axis=1, keepdims=False)
-        grid = lax.dynamic_index_in_dim(grid, y_at, axis=1, keepdims=False)
-        grid = lax.dynamic_index_in_dim(grid, x_at, axis=2, keepdims=False)
-        return grid.reshape((query_rows,) + grid.shape[3:])
+        grid = lax.dynamic_index_in_dim(grid, y_at, axis=0, keepdims=False)
+        return grid.swapaxes(0, 1).reshape((query_rows,) + grid.shape[3:])
 
     query_ids = own_queries(token_grid)
     query_request = segment_of(query_ids, request_ends)
@@ -180,7 +181,7 @@
     )
     value_rows = heads4[:, :, 2]
     kv_rows = jnp.concatenate([key_rot, value_rows], axis=2)
-    key_order = (1, 2, 4, 0, 3, 5)
+    key_order = (1, 0, 2, 4, 3, 5)
     key_ids = token_grid.transpose(key_order).reshape(-1)
     key_request = segment_of(key_ids, request_ends)
     kept = key_keep.reshape(digits).transpose(key_order).reshape(-1) == 1
@@ -210,9 +211,10 @@
         head_out.append((mixed / totals[:, None]).astype(jnp.bfloat16))
     attended = jnp.stack(head_out, axis=1)
     attended = attended.reshape(query_rows, local_heads * head_size)
-    attn_feats = lax.all_to_all(attended, group, split_axis=0, concat_axis=1, tiled=True)
-    attn_feats = attn_feats.reshape(block_rows, ys, 2, xs, -1).swapaxes(2, 3).reshape(block_rows, -1)
-    attn_local = lax.all_to_all(attn_feats, ("y", "x", "zh"), split_axis=1, concat_axis=0, tiled=True)
+    attn_back = lax.ppermute(attended, ("zl", "y"), flip)
+    attn_local = lax.all_to_all(
+        attn_back.reshape(query_rows, xs, -1), "x", 1, 0, tiled=True
+    ).reshape(xs * query_rows, -1)
     mlp_out = lax.optimization_barrier(
         jnp.dot(mlp_act, w_mlp_out, preferred_element_type=jnp.float32)
     )

time: 273 us -> 275 us (level); the launches traced: 270 us -> 270 us
  blocking collectives: 100 us -> 46.4 us
  waiting for transfers between devices: 69.9 us -> 121 us
  local copies, waits for them, and re-layouts: 13.3 us -> 10.1 us
  starting transfers between devices: 41.9 us -> 45 us
  matrix products: 24.5 us -> 27.4 us
    all_to_all x2 -> x0, blocking collectives: 58.3 us -> none  [the longest x1 46.4 us: gather_plane(): lax.all_to_all(jnp.broadcast_to(pair[None], (plane,) + pair.shape), PLANE...]
    all_to_all x3, waiting for transfers between devices: 26.8 us -> 50.1 us  [the longest x1 43.3 us: gather_plane(): lax.all_to_all(jnp.broadcast_to(pair[None], (plane,) + pair.shape), PLANE...]
    ppermute x0 -> x2, waiting for transfers between devices: none -> 22.9 us  [the longest x1 16.1 us: body(): heads_in = lax.ppermute(quarters, ('zl', 'y'), flip)]
    ppermute x0 -> x2, starting transfers between devices: none -> 6.9 us  [the longest x1 4.27 us: body(): heads_in = lax.ppermute(quarters, ('zl', 'y'), flip)]
    all_to_all x1, blocking collectives: 42.1 us -> 46.4 us  [reduce_blk(): got = lax.all_to_all(pieces, PLANE, 0, 0, tiled=True)]
    all_to_all x3, waiting for transfers between devices: 36.7 us -> 40.7 us  [body(): lax.all_to_all(jnp.broadcast_to(piece[None], (ys * xs,) + piece.shape), P...]
    all_to_all x3, starting transfers between devices: 17.2 us -> 14.2 us  [the longest x1 7.22 us: gather_plane(): lax.all_to_all(jnp.broadcast_to(pair[None], (plane,) + pair.shape), PLANE...]
  transfers between devices with their start and end apart: 11 -> 13, of which waited for: 8 -> 9; matrix products, arithmetic and copies ran while one was open for 10% -> 10% of each run, Pallas kernels for 0% -> 0%
where the time goes in v7:
time: 275 us; the launch traced here: 270 us
  waiting for transfers between devices  121 us (44%)
  blocking collectives  46.4 us (17%)
  starting transfers between devices  45 us (16%)
  matrix products  27.4 us (10%)
  other arithmetic  19.4 us (7%)
  local copies, waits for them, and re-layouts  10.1 us (4%)
    all_to_all x1, blocking collectives, reduce_blk(): got = lax.all_to_all(pieces, PLANE, 0, 0, tiled=True)  46.4 us
    all_to_all x1, waiting for transfers between devices, gather_plane(): lax.all_to_all(jnp.broadcast_to(pair[None], (plane,) + pair.shape), PLANE...  43.3 us
    all_to_all x3, waiting for transfers between devices, body(): lax.all_to_all(jnp.broadcast_to(piece[None], (ys * xs,) + piece.shape), P...  40.7 us
    ppermute x1, waiting for transfers between devices, body(): heads_in = lax.ppermute(quarters, ('zl', 'y'), flip)  16.1 us
    all_to_all x3, starting transfers between devices, body(): lax.all_to_all(jnp.broadcast_to(piece[None], (ys * xs,) + piece.shape), P...  12.3 us
    dot_general x1, matrix products, body(): jnp.dot(mlp_act, w_mlp_out, preferred_element_type=jnp.float32)  8.86 us
    all_to_all x1, starting transfers between devices, gather_plane(): lax.all_to_all(jnp.broadcast_to(pair[None], (plane,) + pair.shape), PLANE...  7.22 us
    ppermute x1, waiting for transfers between devices, body(): attn_back = lax.ppermute(attended, ('zl', 'y'), flip)  6.81 us
  transfers between devices with their start and end apart: 13, of which 9 were waited for; matrix products, arithmetic and copies ran while one was open for 10% of the time, Pallas kernels for 0%

profile of v7, /device:TPU:32, one launch (start us, length us, event | category | flops | bytes accessed | tf_op | source)
XLA Modules:
  0.0 269.6 jit_solution(9660229504417696252)
XLA Ops:
  0.0 6.3 %collective-permute-start = (f32[16,3072]{1,0:T(8,128)}, f32[16,3072]{1,0:T(8,128)S(1)}, u32[]{:S(2)}, u32[]{:S(2)}) collective-permute-start(f32[16,3072]{1,0:T(8,128)} %param.12), channel_id=1, source_target_pairs={{0,4},{4,0},{1,5},{5,1},{2,6},{6,2},{3,7},{7,3},{8,12},{12,8},{9,1... | collective-permute-start | bytes 589832 | tf_op jit(solution)/shard_map/ppermute | solution.py:118
  6.3 0.8 reduce-window.8
  7.1 0.7 fusion.67
  7.8 1.1 reduce_sum.139
  8.9 1.1 multiply_reduce_fusion.3
  10.1 2.9 %fusion = f32[4,1,9216]{2,1,0:T(1,128)S(1)} fusion(bf16[4,28,9216]{2,0,1:T(4,128)(2,1)} %bitcast.112, pred[4,28,1]{1,0,2:T(4,128)(4,1)S(1)} %fusion.67), kind=kOutput, calls=%fused_computation.5 | convolution fusion | flops 2064384 | bytes 2211952 | tf_op jit(solution)/shard_map/rs,rsk->rk/dot_general | solution.py:122
  13.0 0.4 fusion.51
  13.5 1.3 fusion.49
  14.7 0.9 collective-permute-done
  15.8 0.2 multiply_reduce_fusion.2
  16.0 1.2 select_bitcast_fusion.8
  17.3 2.0 broadcast_in_dim.64
  19.3 7.2 %all-to-all-start = ((bf16[16,2,16,3072]{3,2,1,0:T(8,128)(2,1)}), bf16[16,2,16,3072]{3,2,1,0:T(8,128)(2,1)}, u32[]{:S(2)}, u32[]{:S(2)}) async-start(bf16[16,2,16,3072]{3,2,1,0:T(8,128)(2,1)} %broadcast_in_dim.64), calls=%async_computation | async-start | bytes 6291456 | tf_op jit(solution)/shard_map/all_to_all | solution.py:77
  26.9 0.3 reshape.479
  27.3 43.3 %all-to-all-done = bf16[16,2,16,3072]{3,2,1,0:T(8,128)(2,1)} async-done(((bf16[16,2,16,3072]{3,2,1,0:T(8,128)(2,1)}), bf16[16,2,16,3072]{3,2,1,0:T(8,128)(2,1)}, u32[]{:S(2)}, u32[]{:S(2)}) %all-to-all-start) | async-done | bytes 3145760 | tf_op jit(solution)/shard_map/all_to_all | solution.py:77
  70.7 3.5 %fusion.8 = bf16[36,4,8,128]{3,2,1,0:T(8,128)(2,1)S(1)} fusion(bf16[512,3072]{1,0:T(8,128)(2,1)} %bitcast.12, bf16[3072,288]{0,1:T(8,128)(2,1)} %param.18), kind=kOutput, calls=%fused_computation.25 | convolution fusion | flops 906117120 | bytes 5210112 | tf_op jit(solution)/shard_map/dot_general | solution.py:148
  74.2 0.8 copy.75
  75.0 3.5 %all-to-all-start.1 = ((bf16[4,128,288]{1,2,0:T(8,128)(2,1)}), bf16[4,128,288]{1,2,0:T(8,128)(2,1)S(1)}, u32[]{:S(2)}, u32[]{:S(2)}) async-start(bf16[4,128,288]{1,2,0:T(8,128)(2,1)} %bitcast.107), calls=%async_computation.1 | async-start | bytes 589824 | tf_op jit(solution)/shard_map/all_to_all | solution.py:158
  78.4 6.8 %all-to-all-done.1 = bf16[4,128,288]{1,2,0:T(8,128)(2,1)S(1)} async-done(((bf16[4,128,288]{1,2,0:T(8,128)(2,1)}), bf16[4,128,288]{1,2,0:T(8,128)(2,1)S(1)}, u32[]{:S(2)}, u32[]{:S(2)}) %all-to-all-start.1) | async-done | bytes 294944 | tf_op jit(solution)/shard_map/all_to_all | solution.py:158
  85.2 4.3 %collective-permute-start.1 = (bf16[128,1152]{0,1:T(8,128)(2,1)S(1)}, bf16[128,1152]{0,1:T(8,128)(2,1)S(1)}, u32[]{:S(2)}, u32[]{:S(2)}) collective-permute-start(bf16[128,1152]{0,1:T(8,128)(2,1)S(1)} %bitcast.124), channel_id=1, source_target_pairs={{0,0},{8,64},{16,128},{24,192},{64,8},{72,72},{80,136},{88,200},{1... | collective-permute-start | bytes 884744 | tf_op jit(solution)/shard_map/ppermute | solution.py:160
  89.7 16.1 %collective-permute-done.1 = bf16[128,1152]{0,1:T(8,128)(2,1)S(1)} collective-permute-done((bf16[128,1152]{0,1:T(8,128)(2,1)S(1)}, bf16[128,1152]{0,1:T(8,128)(2,1)S(1)}, u32[]{:S(2)}, u32[]{:S(2)}) %collective-permute-start.1) | collective-permute-done | bytes 294944 | tf_op jit(solution)/shard_map/ppermute | solution.py:160
  106.3 1.2 subtract_convert_fusion.1
  107.5 0.2 pad_maximum_fusion.5
  107.7 0.6 fusion.57
  108.5 1.1 broadcast_in_dim.66
  109.5 3.7 %all-to-all-start.2 = ((bf16[16,128,256]{2,1,0:T(8,128)(2,1)}), bf16[16,128,256]{2,1,0:T(8,128)(2,1)S(1)}, u32[]{:S(2)}, u32[]{:S(2)}) async-start(bf16[16,128,256]{2,1,0:T(8,128)(2,1)} %broadcast_in_dim.66), calls=%async_computation.2 | async-start | bytes 2097152 | tf_op jit(solution)/shard_map/all_to_all | solution.py:195
  113.2 0.9 copy.46
  114.2 15.3 %all-to-all-done.2 = bf16[16,128,256]{2,1,0:T(8,128)(2,1)S(1)} async-done(((bf16[16,128,256]{2,1,0:T(8,128)(2,1)}), bf16[16,128,256]{2,1,0:T(8,128)(2,1)S(1)}, u32[]{:S(2)}, u32[]{:S(2)}) %all-to-all-start.2) | async-done | bytes 1048608 | tf_op jit(solution)/shard_map/all_to_all | solution.py:195
  129.4 1.1 broadcast_in_dim.70
  130.5 4.3 %all-to-all-start.3 = ((bf16[16,128,256]{2,1,0:T(8,128)(2,1)}), bf16[16,128,256]{2,1,0:T(8,128)(2,1)}, u32[]{:S(2)}, u32[]{:S(2)}) async-start(bf16[16,128,256]{2,1,0:T(8,128)(2,1)} %broadcast_in_dim.70), calls=%async_computation.3 | async-start | bytes 2097152 | tf_op jit(solution)/shard_map/all_to_all | solution.py:195
  135.0 15.2 %all-to-all-done.3 = bf16[16,128,256]{2,1,0:T(8,128)(2,1)} async-done(((bf16[16,128,256]{2,1,0:T(8,128)(2,1)}), bf16[16,128,256]{2,1,0:T(8,128)(2,1)}, u32[]{:S(2)}, u32[]{:S(2)}) %all-to-all-start.3) | async-done | bytes 1048608 | tf_op jit(solution)/shard_map/all_to_all | solution.py:195
  150.2 1.1 broadcast_in_dim.123
  151.3 4.3 %all-to-all-start.4 = ((bf16[16,128,256]{2,1,0:T(8,128)(2,1)}), bf16[16,128,256]{2,1,0:T(8,128)(2,1)}, u32[]{:S(2)}, u32[]{:S(2)}) async-start(bf16[16,128,256]{2,1,0:T(8,128)(2,1)} %broadcast_in_dim.123), calls=%async_computation.4 | async-start | bytes 2097152 | tf_op jit(solution)/shard_map/all_to_all | solution.py:195
  155.7 0.6 collective-permute-start.2
  156.3 0.7 ge.27
  157.2 0.7 eq.130
  158.1 0.8 convert_reduce_fusion.3
  158.9 0.7 convert_reduce_fusion.1
  159.6 10.2 %all-to-all-done.4 = bf16[16,128,256]{2,1,0:T(8,128)(2,1)} async-done(((bf16[16,128,256]{2,1,0:T(8,128)(2,1)}), bf16[16,128,256]{2,1,0:T(8,128)(2,1)}, u32[]{:S(2)}, u32[]{:S(2)}) %all-to-all-start.4) | async-done | bytes 1048608 | tf_op jit(solution)/shard_map/all_to_all | solution.py:195
  169.9 1.2 pad_maximum_fusion.4
  171.1 1.7 select_bitcast_fusion.3
  172.8 0.2 pad_maximum_fusion.1
  173.0 1.4 select_bitcast_fusion.5
  174.3 0.2 pad_maximum_fusion
  174.6 1.4 select_bitcast_fusion.1
  175.9 0.2 pad_maximum_fusion.2
  176.1 0.5 convolution_multiply_fusion
  176.6 0.2 copy-done.6
  176.8 1.0 select_reduce_fusion.2
  177.9 1.7 fusion.2
  179.6 1.1 fusion.14
  180.7 1.4 fusion.4
  182.2 1.1 fusion.12
  183.3 1.1 fusion.13
  184.5 2.6 collective-permute-start.5
  187.1 6.8 %collective-permute-done.5 = bf16[128,384]{0,1:T(8,128)(2,1)} collective-permute-done((bf16[128,384]{0,1:T(8,128)(2,1)S(1)}, bf16[128,384]{0,1:T(8,128)(2,1)}, u32[]{:S(2)}, u32[]{:S(2)}) %collective-permute-start.5) | collective-permute-done | bytes 98336 | tf_op jit(solution)/shard_map/ppermute | solution.py:214
  193.9 3.5 %all-to-all-start.5 = ((bf16[128,4,96]{0,2,1:T(8,128)(2,1)}), bf16[128,4,96]{0,2,1:T(8,128)(2,1)S(1)}, u32[]{:S(2)}, u32[]{:S(2)}) async-start(bf16[128,4,96]{0,2,1:T(8,128)(2,1)} %bitcast.40), calls=%async_computation.5 | async-start | bytes 196608 | tf_op jit(solution)/shard_map/all_to_all | solution.py:215
  197.5 8.9 %fusion.38 = f32[512,3072]{1,0:T(8,128)} fusion(bf16[384,3072]{1,0:T(8,128)(2,1)S(1)} %copy-done, bf16[512,3072]{1,0:T(8,128)(2,1)} %bitcast.12, bf16[3072,384]{1,0:T(8,128)(2,1)} %param.19), kind=kOutput, calls=%fused_computation.61 | convolution fusion | flops 2417688576 | bytes 14155776 | tf_op jit(solution)/shard_map/dot_general | solution.py:219
  206.4 3.8 %add_convert_fusion = bf16[512,3072]{1,0:T(8,128)(2,1)S(1)} fusion(f32[512,3072]{1,0:T(8,128)} %fusion.38, bf16[96,3072]{1,0:T(8,128)(2,1)S(1)} %copy-done.4, bf16[12,8,4,128]{3,2,1,0:T(4,128)(2,1)S(1)} %bitcast.121), kind=kOutput, calls=%fused_computation.1 | convolution fusion | flops 305135616 | bytes 10125312 | tf_op jit(solution)/shard_map/dot_general | solution.py:221
  210.2 46.4 %all_to_all.45 = bf16[16,2,16,3072]{3,2,1,0:T(8,128)(2,1)S(1)} all-to-all(bf16[16,2,16,3072]{3,2,1,0:T(8,128)(2,1)S(1)} %bitcast.109), channel_id=1, replica_groups=mesh['zl'=4,'core'=2,'y'=4,'zh'=2,'x'=4] {'y','x'}, dimensions={0} | all-to-all | bytes 6291456 | tf_op jit(solution)/shard_map/all_to_all | solution.py:84
  256.6 0.6 convert_reduce_fusion
  257.2 4.6 %collective-permute-start.6 = (f32[16,3072]{1,0:T(8,128)S(1)}, f32[16,3072]{1,0:T(8,128)S(1)}, u32[]{:S(2)}, u32[]{:S(2)}) collective-permute-start(f32[16,3072]{1,0:T(8,128)S(1)} %select_bitcast_fusion.6), channel_id=1, source_target_pairs={{0,4},{4,0},{1,5},{5,1},{2,6},{6,2},{3,7},{7,3},{8,12},{12,8},{9,1... | collective-permute-start | bytes 589832 | tf_op jit(solution)/shard_map/ppermute | solution.py:87
  261.8 6.1 %collective-permute-done.6 = f32[16,3072]{1,0:T(8,128)S(1)} collective-permute-done((f32[16,3072]{1,0:T(8,128)S(1)}, f32[16,3072]{1,0:T(8,128)S(1)}, u32[]{:S(2)}, u32[]{:S(2)}) %collective-permute-start.6) | collective-permute-done | bytes 196640 | tf_op jit(solution)/shard_map/ppermute | solution.py:87
  267.9 1.7 fusion.48
  (66 shorter events, 2.2 us)
Async XLA Ops:
  0.0 197.5 %copy-start = (bf16[384,3072]{1,0:T(8,128)(2,1)S(1)}, bf16[384,3072]{1,0:T(8,128)(2,1)}, u32[]{:S(2)}) copy-start(bf16[384,3072]{1,0:T(8,128)(2,1)} %param.23) | copy-start | bytes 7077892
  0.0 15.7 %collective-permute-start = (f32[16,3072]{1,0:T(8,128)}, f32[16,3072]{1,0:T(8,128)S(1)}, u32[]{:S(2)}, u32[]{:S(2)}) collective-permute-start(f32[16,3072]{1,0:T(8,128)} %param.12), channel_id=1, source_target_pairs={{0,4},{4,0},{1,5},{5,1},{2,6},{6,2},{3,7},{7,3},{8,12},{12,8},{9,1... | collective-permute-start | bytes 589832 | tf_op jit(solution)/shard_map/ppermute | solution.py:118
  7.1 5.9 %copy-start.8 = (s32[4,1]{0,1:T(1,128)}, s32[4,1]{0,1:T(1,128)S(1)}, u32[]{:S(2)}) copy-start(s32[4,1]{0,1:T(1,128)S(1)} %reduce-window.8) | copy-start | bytes 52
  10.1 6.0 %copy-start.1 = (f32[16,3072]{1,0:T(8,128)S(1)}, f32[16,3072]{1,0:T(8,128)}, u32[]{:S(2)}) copy-start(f32[16,3072]{1,0:T(8,128)} %param.12) | copy-start | bytes 589828
  13.5 5.8 %copy-start.3 = (f32[16,9216]{1,0:T(8,128)}, f32[16,9216]{1,0:T(8,128)S(1)}, u32[]{:S(2)}) copy-start(f32[16,9216]{1,0:T(8,128)S(1)} %fusion.51) | copy-start | bytes 1769476
  19.3 7.3 %copy-start.10 = (f32[128]{0:T(128)S(1)}, f32[128]{0:T(128)}, u32[]{:S(2)}) copy-start(f32[128]{0:T(128)} %param.20) | copy-start | bytes 1540
  19.3 7.4 %copy-start.11 = (f32[128]{0:T(128)S(1)}, f32[128]{0:T(128)}, u32[]{:S(2)}) copy-start(f32[128]{0:T(128)} %param.21) | copy-start | bytes 1540
  19.3 7.5 %copy-start.5 = (s32[4096,3]{0,1:T(4,128)S(1)}, s32[4096,3]{0,1:T(4,128)}, u32[]{:S(2)}) copy-start(s32[4096,3]{0,1:T(4,128)} %param.14) | copy-start | bytes 147460
  19.3 51.3 %all-to-all-start = ((bf16[16,2,16,3072]{3,2,1,0:T(8,128)(2,1)}), bf16[16,2,16,3072]{3,2,1,0:T(8,128)(2,1)}, u32[]{:S(2)}, u32[]{:S(2)}) async-start(bf16[16,2,16,3072]{3,2,1,0:T(8,128)(2,1)} %broadcast_in_dim.64), calls=%async_computation | async-start | bytes 6291456 | tf_op jit(solution)/shard_map/all_to_all | solution.py:77
  75.0 10.3 %all-to-all-start.1 = ((bf16[4,128,288]{1,2,0:T(8,128)(2,1)}), bf16[4,128,288]{1,2,0:T(8,128)(2,1)S(1)}, u32[]{:S(2)}, u32[]{:S(2)}) async-start(bf16[4,128,288]{1,2,0:T(8,128)(2,1)} %bitcast.107), calls=%async_computation.1 | async-start | bytes 589824 | tf_op jit(solution)/shard_map/all_to_all | solution.py:158
  85.2 20.6 %collective-permute-start.1 = (bf16[128,1152]{0,1:T(8,128)(2,1)S(1)}, bf16[128,1152]{0,1:T(8,128)(2,1)S(1)}, u32[]{:S(2)}, u32[]{:S(2)}) collective-permute-start(bf16[128,1152]{0,1:T(8,128)(2,1)S(1)} %bitcast.124), channel_id=1, source_target_pairs={{0,0},{8,64},{16,128},{24,192},{64,8},{72,72},{80,136},{88,200},{1... | collective-permute-start | bytes 884744 | tf_op jit(solution)/shard_map/ppermute | solution.py:160
  109.5 19.9 %all-to-all-start.2 = ((bf16[16,128,256]{2,1,0:T(8,128)(2,1)}), bf16[16,128,256]{2,1,0:T(8,128)(2,1)S(1)}, u32[]{:S(2)}, u32[]{:S(2)}) async-start(bf16[16,128,256]{2,1,0:T(8,128)(2,1)} %broadcast_in_dim.66), calls=%async_computation.2 | async-start | bytes 2097152 | tf_op jit(solution)/shard_map/all_to_all | solution.py:195
  130.5 19.7 %all-to-all-start.3 = ((bf16[16,128,256]{2,1,0:T(8,128)(2,1)}), bf16[16,128,256]{2,1,0:T(8,128)(2,1)}, u32[]{:S(2)}, u32[]{:S(2)}) async-start(bf16[16,128,256]{2,1,0:T(8,128)(2,1)} %broadcast_in_dim.70), calls=%async_computation.3 | async-start | bytes 2097152 | tf_op jit(solution)/shard_map/all_to_all | solution.py:195
  134.9 20.8 %copy-start.7 = (s32[4096]{0:T(1024)S(1)}, s32[4096]{0:T(1024)}, u32[]{:S(2)}) copy-start(s32[4096]{0:T(1024)} %param.13) | copy-start | bytes 49156
  151.3 18.6 %all-to-all-start.4 = ((bf16[16,128,256]{2,1,0:T(8,128)(2,1)}), bf16[16,128,256]{2,1,0:T(8,128)(2,1)}, u32[]{:S(2)}, u32[]{:S(2)}) async-start(bf16[16,128,256]{2,1,0:T(8,128)(2,1)} %broadcast_in_dim.123), calls=%async_computation.4 | async-start | bytes 2097152 | tf_op jit(solution)/shard_map/all_to_all | solution.py:195
  155.6 15.4 %collective-permute-start.3 = (bf16[16,128,256]{2,1,0:T(8,128)(2,1)}, bf16[16,128,256]{2,1,0:T(8,128)(2,1)}, u32[]{:S(2)}, u32[]{:S(2)}) collective-permute-start(bf16[16,128,256]{2,1,0:T(8,128)(2,1)} %all-to-all-done.3), channel_id=1, source_target_pairs={{0,32},{32,0},{1,33},{33,1},{2,34},{34,2},{3,35},{35,3},{4,36},{36... | collective-permute-start | bytes 3145736 | tf_op jit(solution)/shard_map/ppermute | solution.py:198
  155.7 17.2 %collective-permute-start.2 = (bf16[16,128,256]{2,1,0:T(8,128)(2,1)S(1)}, bf16[16,128,256]{2,1,0:T(8,128)(2,1)}, u32[]{:S(2)}, u32[]{:S(2)}) collective-permute-start(bf16[16,128,256]{2,1,0:T(8,128)(2,1)S(1)} %all-to-all-done.2), channel_id=1, source_target_pairs={{0,32},{32,0},{1,33},{33,1},{2,34},{34,2},{3,35},{35,3},{4,36},{36... | collective-permute-start | bytes 3145736 | tf_op jit(solution)/shard_map/ppermute | solution.py:198
  169.9 4.7 %collective-permute-start.4 = (bf16[16,128,256]{2,1,0:T(8,128)(2,1)}, bf16[16,128,256]{2,1,0:T(8,128)(2,1)S(1)}, u32[]{:S(2)}, u32[]{:S(2)}) collective-permute-start(bf16[16,128,256]{2,1,0:T(8,128)(2,1)} %all-to-all-done.4), channel_id=1, source_target_pairs={{0,32},{32,0},{1,33},{33,1},{2,34},{34,2},{3,35},{35,3},{4,36},{36... | collective-permute-start | bytes 3145736 | tf_op jit(solution)/shard_map/ppermute | solution.py:198
  176.1 0.7 copy-start.6
  176.1 0.7 copy-start.9
  184.5 9.5 %collective-permute-start.5 = (bf16[128,384]{0,1:T(8,128)(2,1)S(1)}, bf16[128,384]{0,1:T(8,128)(2,1)}, u32[]{:S(2)}, u32[]{:S(2)}) collective-permute-start(bf16[128,384]{0,1:T(8,128)(2,1)S(1)} %bitcast.132), channel_id=1, source_target_pairs={{0,0},{8,64},{16,128},{24,192},{64,8},{72,72},{80,136},{88,200},{1... | collective-permute-start | bytes 294920 | tf_op jit(solution)/shard_map/ppermute | solution.py:214
  193.9 12.4 %all-to-all-start.5 = ((bf16[128,4,96]{0,2,1:T(8,128)(2,1)}), bf16[128,4,96]{0,2,1:T(8,128)(2,1)S(1)}, u32[]{:S(2)}, u32[]{:S(2)}) async-start(bf16[128,4,96]{0,2,1:T(8,128)(2,1)} %bitcast.40), calls=%async_computation.5 | async-start | bytes 196608 | tf_op jit(solution)/shard_map/all_to_all | solution.py:215
  197.5 8.9 %copy-start.4 = (bf16[96,3072]{1,0:T(8,128)(2,1)S(1)}, bf16[96,3072]{1,0:T(8,128)(2,1)}, u32[]{:S(2)}) copy-start(bf16[96,3072]{1,0:T(8,128)(2,1)} %param.22) | copy-start | bytes 1769476
  256.6 11.3 %copy-start.2 = (f32[16,3072]{1,0:T(8,128)S(1)}, f32[16,3072]{1,0:T(8,128)}, u32[]{:S(2)}) copy-start(f32[16,3072]{1,0:T(8,128)} %param.12) | copy-start | bytes 589828
  257.2 10.7 %collective-permute-start.6 = (f32[16,3072]{1,0:T(8,128)S(1)}, f32[16,3072]{1,0:T(8,128)S(1)}, u32[]{:S(2)}, u32[]{:S(2)}) collective-permute-start(f32[16,3072]{1,0:T(8,128)S(1)} %select_bitcast_fusion.6), channel_id=1, source_target_pairs={{0,4},{4,0},{1,5},{5,1},{2,6},{6,2},{3,7},{7,3},{8,12},{12,8},{9,1... | collective-permute-start | bytes 589832 | tf_op jit(solution)/shard_map/ppermute | solution.py:87

commit v8 on v6

--- a/solution.py
+++ b/solution.py
@@ -189,16 +189,15 @@
     )
     first_core = core_at == 0
     head_out = []
+    got = lax.all_to_all(
+        jnp.broadcast_to(kv_rows[None], (ys * xs,) + kv_rows.shape), PLANE, 0, 0, tiled=True
+    )
+    sibling = lax.ppermute(got, "core", SWAP)
+    both = jnp.stack([jnp.where(first_core, got, sibling), jnp.where(first_core, sibling, got)])
+    both = both.reshape((-1,) + kv_rows.shape[1:])
     for head in range(local_heads):
-        piece = kv_rows[:, head]
-        got = lax.all_to_all(
-            jnp.broadcast_to(piece[None], (ys * xs,) + piece.shape), PLANE, 0, 0, tiled=True
-        )
-        sibling = lax.ppermute(got, "core", SWAP)
-        both = jnp.stack([jnp.where(first_core, got, sibling), jnp.where(first_core, sibling, got)])
-        both = both.reshape(-1, 2 * head_size)
-        key_h = both[:, :head_size]
-        value_h = both[:, head_size:]
+        key_h = both[:, head, :head_size]
+        value_h = both[:, head, head_size:]
         scores = (
             jnp.einsum("qd,kd->qk", query_rot[:, head], key_h, preferred_element_type=jnp.float32)
             * inv_root

time: 273 us -> 270 us (0.989)
  blocking collectives: 100 us -> 140 us
  waiting for transfers between devices: 69.9 us -> 35.2 us
  starting transfers between devices: 41.9 us -> 29.8 us
  local copies, waits for them, and re-layouts: 13.3 us -> 19.3 us
    all_to_all x0 -> x1, blocking collectives: none -> 40.3 us  [body(): lax.all_to_all(jnp.broadcast_to(kv_rows[None], (ys * xs,) + kv_rows.shape...]
    all_to_all x3 -> x0, waiting for transfers between devices: 36.7 us -> none  [body(): lax.all_to_all(jnp.broadcast_to(piece[None], (ys * xs,) + piece.shape), P...]
    all_to_all x3 -> x0, starting transfers between devices: 12.3 us -> none  [body(): lax.all_to_all(jnp.broadcast_to(piece[None], (ys * xs,) + piece.shape), P...]
    ppermute x3 -> x1, waiting for transfers between devices: 0.01 us -> 4.86 us  [body(): sibling = lax.ppermute(got, 'core', SWAP)]
    all_to_all x1, waiting for transfers between devices: 14.5 us -> 11 us  [body(): lax.all_to_all(qkv_cols, ('y', 'x', 'zh'), split_axis=0, concat_axis=1, t...]
    broadcast_in_dim x3 -> x1, local copies, waits for them, and re-layouts: 3.31 us -> 0.36 us  [body(): jnp.broadcast_to(kv_rows[None], (ys * xs,) + kv_rows.shape)]
  transfers between devices with their start and end apart: 11 -> 6, of which waited for: 8 -> 6; matrix products, arithmetic and copies ran while one was open for 10% -> 8% of each run, Pallas kernels for 0% -> 0%
where the time goes in v8:
time: 270 us; the launch traced here: 267 us
  blocking collectives  140 us (52%)
  waiting for transfers between devices  35.2 us (13%)
  starting transfers between devices  29.8 us (11%)
  matrix products  24.6 us (9%)
  local copies, waits for them, and re-layouts  19.3 us (7%)
  other arithmetic  17.9 us (7%)
    all_to_all x1, blocking collectives, gather_plane(): lax.all_to_all(jnp.broadcast_to(pair[None], (plane,) + pair.shape), PLANE...  45.1 us
    all_to_all x1, blocking collectives, reduce_blk(): got = lax.all_to_all(pieces, PLANE, 0, 0, tiled=True)  42.4 us
    all_to_all x1, blocking collectives, body(): lax.all_to_all(jnp.broadcast_to(kv_rows[None], (ys * xs,) + kv_rows.shape...  40.3 us
    all_to_all x1, blocking collectives, body(): lax.all_to_all(attended, group, split_axis=0, concat_axis=1, tiled=True)  11.7 us
    all_to_all x1, waiting for transfers between devices, body(): lax.all_to_all(qkv_cols, ('y', 'x', 'zh'), split_axis=0, concat_axis=1, t...  11 us
    dot_general x1, matrix products, body(): jnp.dot(mlp_act, w_mlp_out, preferred_element_type=jnp.float32)  8.81 us
    all_to_all x1, starting transfers between devices, body(): lax.all_to_all(qkv_cols, ('y', 'x', 'zh'), split_axis=0, concat_axis=1, t...  8.2 us
    all_to_all x1, waiting for transfers between devices, body(): lax.all_to_all(by_token, group, split_axis=1, concat_axis=0, tiled=True)  8.13 us
  transfers between devices with their start and end apart: 6, of which 6 were waited for; matrix products, arithmetic and copies ran while one was open for 8% of the time, Pallas kernels for 0%

profile of v8, /device:TPU:32, one launch (start us, length us, event | category | flops | bytes accessed | tf_op | source)
XLA Modules:
  0.0 266.6 jit_solution(12972341677203676381)
XLA Ops:
  0.0 6.3 %collective-permute-start = (f32[16,3072]{1,0:T(8,128)}, f32[16,3072]{1,0:T(8,128)S(1)}, u32[]{:S(2)}, u32[]{:S(2)}) collective-permute-start(f32[16,3072]{1,0:T(8,128)} %param.12), channel_id=1, source_target_pairs={{0,4},{4,0},{1,5},{5,1},{2,6},{6,2},{3,7},{7,3},{8,12},{12,8},{9,1... | collective-permute-start | bytes 589832 | tf_op jit(solution)/shard_map/ppermute | solution.py:118
  6.3 0.8 reduce-window.8
  7.1 0.7 fusion.55
  7.9 2.8 %fusion = f32[4,1,9216]{2,1,0:T(1,128)S(1)} fusion(bf16[4,28,9216]{2,0,1:T(4,128)(2,1)} %bitcast.117, pred[4,28,1]{1,0,2:T(4,128)(4,1)S(1)} %fusion.55), kind=kOutput, calls=%fused_computation.8 | convolution fusion | flops 2064384 | bytes 2211952 | tf_op jit(solution)/shard_map/rs,rsk->rk/dot_general | solution.py:122
  10.8 0.4 fusion.44
  11.2 1.3 fusion.42
  12.6 0.2 multiply_reduce_fusion.3
  12.8 2.9 %collective-permute-done = f32[16,3072]{1,0:T(8,128)S(1)} collective-permute-done((f32[16,3072]{1,0:T(8,128)}, f32[16,3072]{1,0:T(8,128)S(1)}, u32[]{:S(2)}, u32[]{:S(2)}) %collective-permute-start) | collective-permute-done | bytes 196640 | tf_op jit(solution)/shard_map/ppermute | solution.py:118
  15.8 0.2 multiply_reduce_fusion.2
  16.1 1.2 select_bitcast_fusion.4
  17.3 0.4 broadcast_in_dim.53
  17.7 45.1 %all_to_all.82 = bf16[16,2,16,3072]{3,2,1,0:T(8,128)(2,1)S(1)} all-to-all(bf16[16,2,16,3072]{3,2,1,0:T(8,128)(2,1)S(1)} %broadcast_in_dim.53), channel_id=1, replica_groups=mesh['zl'=4,'core'=2,'y'=4,'zh'=2,'x'=4] {'y','x'}, dimensions={0} | all-to-all | bytes 6291456 | tf_op jit(solution)/shard_map/all_to_all | solution.py:77
  62.8 1.7 copy-done.1
  64.5 1.1 convolution_convert_fusion
  65.6 0.9 copy.85
  66.6 8.2 %all-to-all-start.1 = ((bf16[32,16,288]{2,1,0:T(8,128)(2,1)}), bf16[32,16,288]{2,1,0:T(8,128)(2,1)S(1)}, u32[]{:S(2)}, u32[]{:S(2)}) async-start(bf16[32,16,288]{2,1,0:T(8,128)(2,1)} %bitcast.119), calls=%async_computation.1 | async-start | bytes 786432 | tf_op jit(solution)/shard_map/all_to_all | solution.py:156
  74.8 0.7 mul.250
  75.5 0.7 mul.239
  76.3 1.9 reshape.483
  78.2 0.9 convert_reduce_fusion.2
  79.1 11.0 %all-to-all-done.1 = bf16[32,16,288]{2,1,0:T(8,128)(2,1)S(1)} async-done(((bf16[32,16,288]{2,1,0:T(8,128)(2,1)}), bf16[32,16,288]{2,1,0:T(8,128)(2,1)S(1)}, u32[]{:S(2)}, u32[]{:S(2)}) %all-to-all-start.1) | async-done | bytes 294944 | tf_op jit(solution)/shard_map/all_to_all | solution.py:156
  90.1 0.9 copy.132
  91.0 1.3 all_to_all.63
  92.4 0.7 copy.87
  93.1 5.4 %all-to-all-start.2 = ((bf16[16,8,1152]{2,0,1:T(8,128)(2,1)}), bf16[16,8,1152]{2,0,1:T(8,128)(2,1)S(1)}, u32[]{:S(2)}, u32[]{:S(2)}) async-start(bf16[16,8,1152]{2,0,1:T(8,128)(2,1)} %copy.87), calls=%async_computation.2 | async-start | bytes 589824 | tf_op jit(solution)/shard_map/all_to_all | solution.py:159
  98.6 0.7 fusion.73
  99.4 8.1 %all-to-all-done.2 = bf16[16,8,1152]{2,0,1:T(8,128)(2,1)S(1)} async-done(((bf16[16,8,1152]{2,0,1:T(8,128)(2,1)}), bf16[16,8,1152]{2,0,1:T(8,128)(2,1)S(1)}, u32[]{:S(2)}, u32[]{:S(2)}) %all-to-all-start.2) | async-done | bytes 294944 | tf_op jit(solution)/shard_map/all_to_all | solution.py:159
  107.5 0.7 copy-done.3
  108.2 1.0 reshape.485
  109.3 1.1 fusion.72
  110.3 0.7 copy_convert_fusion
  111.3 1.7 copy.94
  113.1 0.8 copy.89
  113.9 0.8 copy.108
  114.7 1.1 multiply_multiply_fusion.1
  115.7 1.1 multiply_multiply_fusion.2
  116.8 2.0 subtract_convert_fusion.1
  118.8 0.2 pad_maximum_fusion.4
  119.0 0.9 pad_maximum_fusion.2
  120.1 0.4 broadcast_in_dim.54
  120.5 40.3 %all_to_all.83 = bf16[16,128,3,256]{3,1,2,0:T(8,128)(2,1)} all-to-all(bf16[16,128,3,256]{3,1,2,0:T(8,128)(2,1)S(1)} %broadcast_in_dim.54), channel_id=1, replica_groups=mesh['zl'=4,'core'=2,'y'=4,'zh'=2,'x'=4] {'y','x'}, dimensions={0} | all-to-all | bytes 6291456 | tf_op jit(solution)/shard_map/all_to_all | solution.py:192
  161.7 0.2 pad_maximum_fusion.3
  161.9 4.9 %collective-permute-done.1 = bf16[16,128,3,256]{3,1,2,0:T(8,128)(2,1)} collective-permute-done((bf16[16,128,3,256]{3,1,2,0:T(8,128)(2,1)}, bf16[16,128,3,256]{3,1,2,0:T(8,128)(2,1)}, u32[]{:S(2)}, u32[]{:S(2)}) %collective-permute-start.1) | collective-permute-done | bytes 3145760 | tf_op jit(solution)/shard_map/ppermute | solution.py:195
  166.8 3.3 %select_bitcast_fusion.1 = (bf16[1,16,128,3,256]{4,2,3,1,0:T(8,128)(2,1)S(1)}, bf16[1,16,128,3,256]{4,2,3,1,0:T(8,128)(2,1)S(1)}) fusion(bf16[16,128,3,256]{3,1,2,0:T(8,128)(2,1)} %all_to_all.83, bf16[16,128,3,256]{3,1,2,0:T(8,128)(2,1)} %collective-permute-done.1, pred[]{:T(512)S(6)} %eq.141), kind=kLoop, calls=%fused_computation.7 | loop fusion | flops 3145728 | bytes 12582913 | tf_op jit(solution)/shard_map/stack | solution.py:196
  170.1 0.6 pad_maximum_fusion
  170.6 0.8 copy.100
  171.4 0.5 convolution_multiply_fusion
  171.9 1.0 select_reduce_fusion.2
  173.0 1.7 fusion.2
  174.7 1.0 fusion.13
  175.7 1.4 fusion.4
  177.1 1.0 fusion.12
  178.1 1.0 fusion.11
  179.3 11.7 %all_to_all.84 = bf16[8,16,384]{2,1,0:T(8,128)(2,1)S(1)} all-to-all(bf16[8,16,384]{2,1,0:T(8,128)(2,1)S(1)} %all_to_all.67), channel_id=1, replica_groups=mesh['zl'=4,'core'=2,'y'=4,'zh'=2,'x'=4] {'zl','zh'}, dimensions={0} | all-to-all | bytes 196608 | tf_op jit(solution)/shard_map/all_to_all | solution.py:212
  191.2 0.7 copy.104
  191.8 4.3 %all-to-all-start.5 = ((bf16[16,32,96]{2,0,1:T(8,128)(2,1)}), bf16[16,32,96]{2,0,1:T(8,128)(2,1)S(1)}, u32[]{:S(2)}, u32[]{:S(2)}) async-start(bf16[16,32,96]{2,0,1:T(8,128)(2,1)} %bitcast.37), calls=%async_computation.5 | async-start | bytes 262144 | tf_op jit(solution)/shard_map/all_to_all | solution.py:214
  196.2 8.8 %fusion.31 = f32[512,3072]{1,0:T(8,128)} fusion(bf16[384,3072]{1,0:T(8,128)(2,1)S(1)} %copy-done, bf16[512,3072]{1,0:T(8,128)(2,1)} %bitcast.116, bf16[3072,384]{1,0:T(8,128)(2,1)} %param.19), kind=kOutput, calls=%fused_computation.54 | convolution fusion | flops 2417688576 | bytes 14155776 | tf_op jit(solution)/shard_map/dot_general | solution.py:216
  205.0 3.6 %all-to-all-done.5 = bf16[16,32,96]{2,0,1:T(8,128)(2,1)S(1)} async-done(((bf16[16,32,96]{2,0,1:T(8,128)(2,1)}), bf16[16,32,96]{2,0,1:T(8,128)(2,1)S(1)}, u32[]{:S(2)}, u32[]{:S(2)}) %all-to-all-start.5) | async-done | bytes 98336 | tf_op jit(solution)/shard_map/all_to_all | solution.py:214
  208.6 4.0 %add_convert_fusion = bf16[512,3072]{1,0:T(8,128)(2,1)S(1)} fusion(f32[512,3072]{1,0:T(8,128)} %fusion.31, bf16[512,96]{1,0:T(8,128)(2,1)S(1)} %bitcast.124, bf16[96,3072]{1,0:T(8,128)(2,1)} %param.22), kind=kOutput, calls=%fused_computation.2 | convolution fusion | flops 305135616 | bytes 10125312 | tf_op jit(solution)/shard_map/dot_general | solution.py:218
  212.6 42.4 %all_to_all.85 = bf16[16,2,16,3072]{3,2,1,0:T(8,128)(2,1)S(1)} all-to-all(bf16[16,2,16,3072]{3,2,1,0:T(8,128)(2,1)S(1)} %bitcast.108), channel_id=1, replica_groups=mesh['zl'=4,'core'=2,'y'=4,'zh'=2,'x'=4] {'y','x'}, dimensions={0} | all-to-all | bytes 6291456 | tf_op jit(solution)/shard_map/all_to_all | solution.py:84
  254.9 0.6 convert_reduce_fusion
  255.5 5.6 %collective-permute-start.2 = (f32[16,3072]{1,0:T(8,128)S(1)}, f32[16,3072]{1,0:T(8,128)S(1)}, u32[]{:S(2)}, u32[]{:S(2)}) collective-permute-start(f32[16,3072]{1,0:T(8,128)S(1)} %select_bitcast_fusion.2), channel_id=1, source_target_pairs={{0,4},{4,0},{1,5},{5,1},{2,6},{6,2},{3,7},{7,3},{8,12},{12,8},{9,1... | collective-permute-start | bytes 589832 | tf_op jit(solution)/shard_map/ppermute | solution.py:87
  261.1 4.8 %collective-permute-done.2 = f32[16,3072]{1,0:T(8,128)S(1)} collective-permute-done((f32[16,3072]{1,0:T(8,128)S(1)}, f32[16,3072]{1,0:T(8,128)S(1)}, u32[]{:S(2)}, u32[]{:S(2)}) %collective-permute-start.2) | collective-permute-done | bytes 196640 | tf_op jit(solution)/shard_map/ppermute | solution.py:87
  265.9 0.7 fusion.41
  (61 shorter events, 2.3 us)
Async XLA Ops:
  0.0 196.2 %copy-start = (bf16[384,3072]{1,0:T(8,128)(2,1)S(1)}, bf16[384,3072]{1,0:T(8,128)(2,1)}, u32[]{:S(2)}) copy-start(bf16[384,3072]{1,0:T(8,128)(2,1)} %param.23) | copy-start | bytes 7077892
  0.0 12.5 %copy-start.2 = (f32[16,3072]{1,0:T(8,128)S(1)}, f32[16,3072]{1,0:T(8,128)}, u32[]{:S(2)}) copy-start(f32[16,3072]{1,0:T(8,128)} %param.12) | copy-start | bytes 589828
  0.0 15.7 %collective-permute-start = (f32[16,3072]{1,0:T(8,128)}, f32[16,3072]{1,0:T(8,128)S(1)}, u32[]{:S(2)}, u32[]{:S(2)}) collective-permute-start(f32[16,3072]{1,0:T(8,128)} %param.12), channel_id=1, source_target_pairs={{0,4},{4,0},{1,5},{5,1},{2,6},{6,2},{3,7},{7,3},{8,12},{12,8},{9,1... | collective-permute-start | bytes 589832 | tf_op jit(solution)/shard_map/ppermute | solution.py:118
  7.1 3.6 %copy-start.8 = (s32[4,1]{0,1:T(1,128)}, s32[4,1]{0,1:T(1,128)S(1)}, u32[]{:S(2)}) copy-start(s32[4,1]{0,1:T(1,128)S(1)} %reduce-window.8) | copy-start | bytes 52
  17.7 46.9 %copy-start.12 = (bf16[3072,288]{0,1:T(8,128)(2,1)S(1)}, bf16[3072,288]{0,1:T(8,128)(2,1)}, u32[]{:S(2)}) copy-start(bf16[3072,288]{0,1:T(8,128)(2,1)} %param.18) | copy-start | bytes 5308420
  62.8 1.7 copy-start.1
  64.5 10.2 %copy-start.10 = (f32[128]{0:T(128)S(1)}, f32[128]{0:T(128)}, u32[]{:S(2)}) copy-start(f32[128]{0:T(128)} %param.21) | copy-start | bytes 1540
  64.5 11.0 %copy-start.11 = (f32[128]{0:T(128)S(1)}, f32[128]{0:T(128)}, u32[]{:S(2)}) copy-start(f32[128]{0:T(128)} %param.20) | copy-start | bytes 1540
  66.6 23.5 %all-to-all-start.1 = ((bf16[32,16,288]{2,1,0:T(8,128)(2,1)}), bf16[32,16,288]{2,1,0:T(8,128)(2,1)S(1)}, u32[]{:S(2)}, u32[]{:S(2)}) async-start(bf16[32,16,288]{2,1,0:T(8,128)(2,1)} %bitcast.119), calls=%async_computation.1 | async-start | bytes 786432 | tf_op jit(solution)/shard_map/all_to_all | solution.py:156
  93.1 14.4 %all-to-all-start.2 = ((bf16[16,8,1152]{2,0,1:T(8,128)(2,1)}), bf16[16,8,1152]{2,0,1:T(8,128)(2,1)S(1)}, u32[]{:S(2)}, u32[]{:S(2)}) async-start(bf16[16,8,1152]{2,0,1:T(8,128)(2,1)} %copy.87), calls=%async_computation.2 | async-start | bytes 589824 | tf_op jit(solution)/shard_map/all_to_all | solution.py:159
  107.5 0.7 copy-start.3
  110.3 3.6 %copy-start.4 = (bf16[128,3,1,128]{3,2,1,0:T(2,128)(2,1)S(1)}, bf16[128,3,1,128]{3,2,1,0:T(2,128)(2,1)}, u32[]{:S(2)}) copy-start(bf16[128,3,1,128]{3,2,1,0:T(2,128)(2,1)} %get-tuple-element.18) | copy-start | bytes 294916
  120.5 40.7 %copy-start.7 = (s32[4096]{0:T(1024)S(1)}, s32[4096]{0:T(1024)}, u32[]{:S(2)}) copy-start(s32[4096]{0:T(1024)} %param.13) | copy-start | bytes 49156
  120.5 41.0 %copy-start.9 = (s32[4,1]{0,1:T(1,128)S(1)}, s32[4,1]{0,1:T(1,128)}, u32[]{:S(2)}) copy-start(s32[4,1]{0,1:T(1,128)} %copy-done.8) | copy-start | bytes 52
  120.5 41.2 %copy-start.5 = (bf16[128,3,64,1]{0,3,2,1:T(2,128)(2,1)S(1)}, bf16[128,3,64,1]{0,3,2,1:T(2,128)(2,1)}, u32[]{:S(2)}) copy-start(bf16[128,3,64,1]{0,3,2,1:T(2,128)(2,1)} %get-tuple-element.20) | copy-start | bytes 147460
  120.5 41.2 %copy-start.6 = (bf16[128,3,64,1]{0,3,2,1:T(2,128)(2,1)S(1)}, bf16[128,3,64,1]{0,3,2,1:T(2,128)(2,1)}, u32[]{:S(2)}) copy-start(bf16[128,3,64,1]{0,3,2,1:T(2,128)(2,1)} %get-tuple-element.21) | copy-start | bytes 147460
  160.8 6.0 %collective-permute-start.1 = (bf16[16,128,3,256]{3,1,2,0:T(8,128)(2,1)}, bf16[16,128,3,256]{3,1,2,0:T(8,128)(2,1)}, u32[]{:S(2)}, u32[]{:S(2)}) collective-permute-start(bf16[16,128,3,256]{3,1,2,0:T(8,128)(2,1)} %all_to_all.83), channel_id=1, source_target_pairs={{0,32},{32,0},{1,33},{33,1},{2,34},{34,2},{3,35},{35,3},{4,36},{36... | collective-permute-start | bytes 9437192 | tf_op jit(solution)/shard_map/ppermute | solution.py:195
  191.8 16.8 %all-to-all-start.5 = ((bf16[16,32,96]{2,0,1:T(8,128)(2,1)}), bf16[16,32,96]{2,0,1:T(8,128)(2,1)S(1)}, u32[]{:S(2)}, u32[]{:S(2)}) async-start(bf16[16,32,96]{2,0,1:T(8,128)(2,1)} %bitcast.37), calls=%async_computation.5 | async-start | bytes 262144 | tf_op jit(solution)/shard_map/all_to_all | solution.py:214
  255.5 10.4 %collective-permute-start.2 = (f32[16,3072]{1,0:T(8,128)S(1)}, f32[16,3072]{1,0:T(8,128)S(1)}, u32[]{:S(2)}, u32[]{:S(2)}) collective-permute-start(f32[16,3072]{1,0:T(8,128)S(1)} %select_bitcast_fusion.2), channel_id=1, source_target_pairs={{0,4},{4,0},{1,5},{5,1},{2,6},{6,2},{3,7},{7,3},{8,12},{12,8},{9,1... | collective-permute-start | bytes 589832 | tf_op jit(solution)/shard_map/ppermute | solution.py:87

commit v9 on v8

--- a/solution.py
+++ b/solution.py
@@ -80,11 +80,14 @@
 
 def reduce_blk(y):
     plane = lax.axis_size("y") * lax.axis_size("x")
-    pieces = y.reshape((plane, 2, y.shape[0] // (plane * 2)) + y.shape[1:])
-    got = lax.all_to_all(pieces, PLANE, 0, 0, tiled=True)
-    part = jnp.sum(got.astype(jnp.float32), axis=0)
-    mine, theirs = by_half(part[0], part[1])
-    return mine + lax.ppermute(theirs, "zh", SWAP)
+    done = []
+    for cols in jnp.split(y, 2, axis=1):
+        pieces = cols.reshape((plane, 2, y.shape[0] // (plane * 2)) + cols.shape[1:])
+        got = lax.all_to_all(pieces, PLANE, 0, 0, tiled=True)
+        part = jnp.sum(got.astype(jnp.float32), axis=0)
+        mine, theirs = by_half(part[0], part[1])
+        done.append(mine + lax.ppermute(theirs, "zh", SWAP))
+    return jnp.concatenate(done, axis=1)
 
 
 def body(

time: 270 us -> 278 us (1.030)
  blocking collectives: 140 us -> 122 us
  starting transfers between devices: 29.8 us -> 39.6 us
  waiting for transfers between devices: 35.2 us -> 44.6 us
  other arithmetic: 17.9 us -> 23.5 us
    all_to_all x1, blocking collectives: 42.4 us -> 25.3 us  [reduce_blk(): got = lax.all_to_all(pieces, PLANE, 0, 0, tiled=True)]
    all_to_all x0 -> x1, waiting for transfers between devices: none -> 13.9 us  [reduce_blk(): got = lax.all_to_all(pieces, PLANE, 0, 0, tiled=True)]
    ppermute x1 -> x2, starting transfers between devices: 5.6 us -> 11 us  [reduce_blk(): done.append(mine + lax.ppermute(theirs, 'zh', SWAP))]
    all_to_all x0 -> x1, starting transfers between devices: none -> 4.39 us  [reduce_blk(): got = lax.all_to_all(pieces, PLANE, 0, 0, tiled=True)]
  transfers between devices with their start and end apart: 6 -> 8, of which waited for: 6 -> 7; matrix products, arithmetic and copies ran while one was open for 8% -> 10% of each run, Pallas kernels for 0% -> 0%
where the time goes in v9:
time: 278 us; the launch traced here: 276 us
  blocking collectives  122 us (44%)
  waiting for transfers between devices  44.6 us (16%)
  starting transfers between devices  39.6 us (14%)
  matrix products  24.6 us (9%)
  other arithmetic  23.5 us (8%)
  local copies, waits for them, and re-layouts  21.3 us (8%)
    all_to_all x1, blocking collectives, gather_plane(): lax.all_to_all(jnp.broadcast_to(pair[None], (plane,) + pair.shape), PLANE...  45.1 us
    all_to_all x1, blocking collectives, body(): lax.all_to_all(jnp.broadcast_to(kv_rows[None], (ys * xs,) + kv_rows.shape...  40.3 us
    all_to_all x1, blocking collectives, reduce_blk(): got = lax.all_to_all(pieces, PLANE, 0, 0, tiled=True)  25.3 us
    all_to_all x1, waiting for transfers between devices, reduce_blk(): got = lax.all_to_all(pieces, PLANE, 0, 0, tiled=True)  13.9 us
    all_to_all x1, blocking collectives, body(): lax.all_to_all(attended, group, split_axis=0, concat_axis=1, tiled=True)  11.7 us
    all_to_all x1, waiting for transfers between devices, body(): lax.all_to_all(qkv_cols, ('y', 'x', 'zh'), split_axis=0, concat_axis=1, t...  11 us
    ppermute x2, starting transfers between devices, reduce_blk(): done.append(mine + lax.ppermute(theirs, 'zh', SWAP))  11 us
    dot_general x1, matrix products, body(): jnp.dot(mlp_act, w_mlp_out, preferred_element_type=jnp.float32)  8.81 us
  transfers between devices with their start and end apart: 8, of which 7 were waited for; matrix products, arithmetic and copies ran while one was open for 10% of the time, Pallas kernels for 0%

profile of v9, /device:TPU:32, one launch (start us, length us, event | category | flops | bytes accessed | tf_op | source)
XLA Modules:
  0.0 276.5 jit_solution(4839272121230374477)
XLA Ops:
  0.0 6.3 %collective-permute-start = (f32[16,3072]{1,0:T(8,128)}, f32[16,3072]{1,0:T(8,128)S(1)}, u32[]{:S(2)}, u32[]{:S(2)}) collective-permute-start(f32[16,3072]{1,0:T(8,128)} %param.12), channel_id=1, source_target_pairs={{0,4},{4,0},{1,5},{5,1},{2,6},{6,2},{3,7},{7,3},{8,12},{12,8},{9,1... | collective-permute-start | bytes 589832 | tf_op jit(solution)/shard_map/ppermute | solution.py:121
  6.3 0.8 reduce-window.8
  7.1 0.7 fusion.55
  7.9 2.8 %fusion = f32[4,1,9216]{2,1,0:T(1,128)S(1)} fusion(bf16[4,28,9216]{2,0,1:T(4,128)(2,1)} %bitcast.121, pred[4,28,1]{1,0,2:T(4,128)(4,1)S(1)} %fusion.55), kind=kOutput, calls=%fused_computation.9 | convolution fusion | flops 2064384 | bytes 2211952 | tf_op jit(solution)/shard_map/rs,rsk->rk/dot_general | solution.py:125
  11.2 1.3 fusion.42
  12.8 2.9 %collective-permute-done = f32[16,3072]{1,0:T(8,128)S(1)} collective-permute-done((f32[16,3072]{1,0:T(8,128)}, f32[16,3072]{1,0:T(8,128)S(1)}, u32[]{:S(2)}, u32[]{:S(2)}) %collective-permute-start) | collective-permute-done | bytes 196640 | tf_op jit(solution)/shard_map/ppermute | solution.py:121
  16.1 1.2 select_bitcast_fusion.5
  17.7 45.1 %all_to_all.87 = bf16[16,2,16,3072]{3,2,1,0:T(8,128)(2,1)S(1)} all-to-all(bf16[16,2,16,3072]{3,2,1,0:T(8,128)(2,1)S(1)} %broadcast_in_dim.53), channel_id=1, replica_groups=mesh['zl'=4,'core'=2,'y'=4,'zh'=2,'x'=4] {'y','x'}, dimensions={0} | all-to-all | bytes 6291456 | tf_op jit(solution)/shard_map/all_to_all | solution.py:77
  62.8 1.7 copy-done.1
  64.5 1.1 convolution_convert_fusion
  65.6 0.9 copy.85
  66.6 8.2 %all-to-all-start.1 = ((bf16[32,16,288]{2,1,0:T(8,128)(2,1)}), bf16[32,16,288]{2,1,0:T(8,128)(2,1)S(1)}, u32[]{:S(2)}, u32[]{:S(2)}) async-start(bf16[32,16,288]{2,1,0:T(8,128)(2,1)} %bitcast.123), calls=%async_computation.1 | async-start | bytes 786432 | tf_op jit(solution)/shard_map/all_to_all | solution.py:159
  74.8 0.7 mul.250
  75.5 0.7 mul.239
  76.3 1.9 reshape.490
  78.2 0.9 convert_reduce_fusion.3
  79.1 11.0 %all-to-all-done.1 = bf16[32,16,288]{2,1,0:T(8,128)(2,1)S(1)} async-done(((bf16[32,16,288]{2,1,0:T(8,128)(2,1)}), bf16[32,16,288]{2,1,0:T(8,128)(2,1)S(1)}, u32[]{:S(2)}, u32[]{:S(2)}) %all-to-all-start.1) | async-done | bytes 294944 | tf_op jit(solution)/shard_map/all_to_all | solution.py:159
  90.1 0.9 copy.132
  91.0 1.3 all_to_all.66
  92.4 0.7 copy.87
  93.1 5.4 %all-to-all-start.2 = ((bf16[16,8,1152]{2,0,1:T(8,128)(2,1)}), bf16[16,8,1152]{2,0,1:T(8,128)(2,1)S(1)}, u32[]{:S(2)}, u32[]{:S(2)}) async-start(bf16[16,8,1152]{2,0,1:T(8,128)(2,1)} %copy.87), calls=%async_computation.2 | async-start | bytes 589824 | tf_op jit(solution)/shard_map/all_to_all | solution.py:162
  98.6 0.7 fusion.74
  99.4 8.1 %all-to-all-done.2 = bf16[16,8,1152]{2,0,1:T(8,128)(2,1)S(1)} async-done(((bf16[16,8,1152]{2,0,1:T(8,128)(2,1)}), bf16[16,8,1152]{2,0,1:T(8,128)(2,1)S(1)}, u32[]{:S(2)}, u32[]{:S(2)}) %all-to-all-start.2) | async-done | bytes 294944 | tf_op jit(solution)/shard_map/all_to_all | solution.py:162
  107.5 0.7 copy-done.3
  108.2 1.0 reshape.492
  109.2 1.1 fusion.73
  110.3 0.7 copy_convert_fusion
  111.3 1.7 copy.94
  113.1 0.8 copy.89
  113.9 0.8 copy.108
  114.7 1.1 multiply_multiply_fusion.1
  115.7 1.1 multiply_multiply_fusion.2
  116.8 2.0 subtract_convert_fusion.1
  119.0 0.9 pad_maximum_fusion.2
  120.5 40.3 %all_to_all.88 = bf16[16,128,3,256]{3,1,2,0:T(8,128)(2,1)} all-to-all(bf16[16,128,3,256]{3,1,2,0:T(8,128)(2,1)S(1)} %broadcast_in_dim.54), channel_id=1, replica_groups=mesh['zl'=4,'core'=2,'y'=4,'zh'=2,'x'=4] {'y','x'}, dimensions={0} | all-to-all | bytes 6291456 | tf_op jit(solution)/shard_map/all_to_all | solution.py:195
  162.0 0.8 convert_reduce_fusion.5
  162.7 0.8 convert_reduce_fusion.2
  163.8 3.0 %collective-permute-done.1 = bf16[16,128,3,256]{3,1,2,0:T(8,128)(2,1)} collective-permute-done((bf16[16,128,3,256]{3,1,2,0:T(8,128)(2,1)}, bf16[16,128,3,256]{3,1,2,0:T(8,128)(2,1)}, u32[]{:S(2)}, u32[]{:S(2)}) %collective-permute-start.1) | collective-permute-done | bytes 3145760 | tf_op jit(solution)/shard_map/ppermute | solution.py:198
  166.8 3.3 %select_bitcast_fusion.1 = (bf16[1,16,128,3,256]{4,2,3,1,0:T(8,128)(2,1)S(1)}, bf16[1,16,128,3,256]{4,2,3,1,0:T(8,128)(2,1)S(1)}) fusion(bf16[16,128,3,256]{3,1,2,0:T(8,128)(2,1)} %all_to_all.88, bf16[16,128,3,256]{3,1,2,0:T(8,128)(2,1)} %collective-permute-done.1, pred[]{:T(512)S(6)} %eq.142), kind=kLoop, calls=%fused_computation.8 | loop fusion | flops 3145728 | bytes 12582913 | tf_op jit(solution)/shard_map/stack | solution.py:199
  170.6 0.8 copy.100
  172.1 1.0 select_reduce_fusion.2
  173.1 1.7 fusion.2
  174.9 1.0 fusion.13
  175.9 1.4 fusion.4
  177.3 1.0 fusion.12
  178.3 1.0 fusion.11
  179.5 11.7 %all_to_all.89 = bf16[8,16,384]{2,1,0:T(8,128)(2,1)S(1)} all-to-all(bf16[8,16,384]{2,1,0:T(8,128)(2,1)S(1)} %all_to_all.70), channel_id=1, replica_groups=mesh['zl'=4,'core'=2,'y'=4,'zh'=2,'x'=4] {'zl','zh'}, dimensions={0} | all-to-all | bytes 196608 | tf_op jit(solution)/shard_map/all_to_all | solution.py:215
  191.4 0.7 copy.104
  192.0 4.3 %all-to-all-start.5 = ((bf16[16,32,96]{2,0,1:T(8,128)(2,1)}), bf16[16,32,96]{2,0,1:T(8,128)(2,1)S(1)}, u32[]{:S(2)}, u32[]{:S(2)}) async-start(bf16[16,32,96]{2,0,1:T(8,128)(2,1)} %bitcast.37), calls=%async_computation.5 | async-start | bytes 262144 | tf_op jit(solution)/shard_map/all_to_all | solution.py:217
  196.4 8.8 %fusion.31 = f32[512,3072]{1,0:T(8,128)} fusion(bf16[384,3072]{1,0:T(8,128)(2,1)S(1)} %copy-done, bf16[512,3072]{1,0:T(8,128)(2,1)} %bitcast.120, bf16[3072,384]{1,0:T(8,128)(2,1)} %param.19), kind=kOutput, calls=%fused_computation.55 | convolution fusion | flops 2417688576 | bytes 14155776 | tf_op jit(solution)/shard_map/dot_general | solution.py:219
  205.2 3.6 %all-to-all-done.5 = bf16[16,32,96]{2,0,1:T(8,128)(2,1)S(1)} async-done(((bf16[16,32,96]{2,0,1:T(8,128)(2,1)}), bf16[16,32,96]{2,0,1:T(8,128)(2,1)S(1)}, u32[]{:S(2)}, u32[]{:S(2)}) %all-to-all-start.5) | async-done | bytes 98336 | tf_op jit(solution)/shard_map/all_to_all | solution.py:217
  208.8 4.0 %add_convert_fusion = bf16[512,3072]{1,0:T(8,128)(2,1)S(1)} fusion(f32[512,3072]{1,0:T(8,128)} %fusion.31, bf16[512,96]{1,0:T(8,128)(2,1)S(1)} %bitcast.128, bf16[96,3072]{1,0:T(8,128)(2,1)} %param.22), kind=kOutput, calls=%fused_computation.1 | convolution fusion | flops 305135616 | bytes 10125312 | tf_op jit(solution)/shard_map/dot_general | solution.py:221
  212.8 1.4 fusion.72
  214.1 25.3 %all_to_all.90 = bf16[16,2,16,1536]{3,2,1,0:T(8,128)(2,1)} all-to-all(bf16[16,2,16,1536]{3,2,1,0:T(8,128)(2,1)S(1)} %bitcast.118), channel_id=1, replica_groups=mesh['zl'=4,'core'=2,'y'=4,'zh'=2,'x'=4] {'y','x'}, dimensions={0} | all-to-all | bytes 3145728 | tf_op jit(solution)/shard_map/all_to_all | solution.py:86
  239.4 4.4 %all-to-all-start.7 = ((bf16[16,2,16,1536]{3,2,1,0:T(8,128)(2,1)}), bf16[16,2,16,1536]{3,2,1,0:T(8,128)(2,1)}, u32[]{:S(2)}, u32[]{:S(2)}) async-start(bf16[16,2,16,1536]{3,2,1,0:T(8,128)(2,1)} %bitcast.117), calls=%async_computation.7 | async-start | bytes 3145728 | tf_op jit(solution)/shard_map/all_to_all | solution.py:86
  243.8 1.7 convert_reduce_fusion.1
  245.5 0.7 select_bitcast_fusion.3
  246.1 5.4 %collective-permute-start.2 = (f32[16,1536]{1,0:T(8,128)}, f32[16,1536]{1,0:T(8,128)}, u32[]{:S(2)}, u32[]{:S(2)}) collective-permute-start(f32[16,1536]{1,0:T(8,128)} %select_bitcast_fusion.3), channel_id=1, source_target_pairs={{0,4},{4,0},{1,5},{5,1},{2,6},{6,2},{3,7},{7,3},{8,12},{12,8},{9,1... | collective-permute-start | bytes 294920 | tf_op jit(solution)/shard_map/ppermute | solution.py:89
  251.6 13.9 %all-to-all-done.7 = bf16[16,2,16,1536]{3,2,1,0:T(8,128)(2,1)} async-done(((bf16[16,2,16,1536]{3,2,1,0:T(8,128)(2,1)}), bf16[16,2,16,1536]{3,2,1,0:T(8,128)(2,1)}, u32[]{:S(2)}, u32[]{:S(2)}) %all-to-all-start.7) | async-done | bytes 1572896 | tf_op jit(solution)/shard_map/all_to_all | solution.py:86
  265.5 1.7 convert_reduce_fusion
  267.1 5.5 %collective-permute-start.3 = (f32[16,1536]{1,0:T(8,128)S(1)}, f32[16,1536]{1,0:T(8,128)S(1)}, u32[]{:S(2)}, u32[]{:S(2)}) collective-permute-start(f32[16,1536]{1,0:T(8,128)S(1)} %select_bitcast_fusion.2), channel_id=1, source_target_pairs={{0,4},{4,0},{1,5},{5,1},{2,6},{6,2},{3,7},{7,3},{8,12},{12,8},{9,1... | collective-permute-start | bytes 294920 | tf_op jit(solution)/shard_map/ppermute | solution.py:89
  272.7 0.9 bitcast_add_fusion.1
  273.6 2.2 collective-permute-done.3
  275.8 0.7 fusion.41
  (70 shorter events, 5.9 us)
Async XLA Ops:
  0.0 196.4 %copy-start = (bf16[384,3072]{1,0:T(8,128)(2,1)S(1)}, bf16[384,3072]{1,0:T(8,128)(2,1)}, u32[]{:S(2)}) copy-start(bf16[384,3072]{1,0:T(8,128)(2,1)} %param.23) | copy-start | bytes 7077892
  0.0 12.5 %copy-start.2 = (f32[16,3072]{1,0:T(8,128)S(1)}, f32[16,3072]{1,0:T(8,128)}, u32[]{:S(2)}) copy-start(f32[16,3072]{1,0:T(8,128)} %param.12) | copy-start | bytes 589828
  0.0 15.7 %collective-permute-start = (f32[16,3072]{1,0:T(8,128)}, f32[16,3072]{1,0:T(8,128)S(1)}, u32[]{:S(2)}, u32[]{:S(2)}) collective-permute-start(f32[16,3072]{1,0:T(8,128)} %param.12), channel_id=1, source_target_pairs={{0,4},{4,0},{1,5},{5,1},{2,6},{6,2},{3,7},{7,3},{8,12},{12,8},{9,1... | collective-permute-start | bytes 589832 | tf_op jit(solution)/shard_map/ppermute | solution.py:121
  7.1 5.5 %copy-start.8 = (s32[4,1]{0,1:T(1,128)}, s32[4,1]{0,1:T(1,128)S(1)}, u32[]{:S(2)}) copy-start(s32[4,1]{0,1:T(1,128)S(1)} %reduce-window.8) | copy-start | bytes 52
  17.7 46.9 %copy-start.12 = (bf16[3072,288]{0,1:T(8,128)(2,1)S(1)}, bf16[3072,288]{0,1:T(8,128)(2,1)}, u32[]{:S(2)}) copy-start(bf16[3072,288]{0,1:T(8,128)(2,1)} %param.18) | copy-start | bytes 5308420
  62.8 1.7 copy-start.1
  64.5 10.2 %copy-start.10 = (f32[128]{0:T(128)S(1)}, f32[128]{0:T(128)}, u32[]{:S(2)}) copy-start(f32[128]{0:T(128)} %param.21) | copy-start | bytes 1540
  64.5 11.0 %copy-start.11 = (f32[128]{0:T(128)S(1)}, f32[128]{0:T(128)}, u32[]{:S(2)}) copy-start(f32[128]{0:T(128)} %param.20) | copy-start | bytes 1540
  66.6 23.5 %all-to-all-start.1 = ((bf16[32,16,288]{2,1,0:T(8,128)(2,1)}), bf16[32,16,288]{2,1,0:T(8,128)(2,1)S(1)}, u32[]{:S(2)}, u32[]{:S(2)}) async-start(bf16[32,16,288]{2,1,0:T(8,128)(2,1)} %bitcast.123), calls=%async_computation.1 | async-start | bytes 786432 | tf_op jit(solution)/shard_map/all_to_all | solution.py:159
  93.1 14.4 %all-to-all-start.2 = ((bf16[16,8,1152]{2,0,1:T(8,128)(2,1)}), bf16[16,8,1152]{2,0,1:T(8,128)(2,1)S(1)}, u32[]{:S(2)}, u32[]{:S(2)}) async-start(bf16[16,8,1152]{2,0,1:T(8,128)(2,1)} %copy.87), calls=%async_computation.2 | async-start | bytes 589824 | tf_op jit(solution)/shard_map/all_to_all | solution.py:162
  107.5 0.7 copy-start.3
  110.3 3.6 %copy-start.4 = (bf16[128,3,1,128]{3,2,1,0:T(2,128)(2,1)S(1)}, bf16[128,3,1,128]{3,2,1,0:T(2,128)(2,1)}, u32[]{:S(2)}) copy-start(bf16[128,3,1,128]{3,2,1,0:T(2,128)(2,1)} %get-tuple-element.20) | copy-start | bytes 294916
  120.5 41.2 %copy-start.7 = (s32[4096]{0:T(1024)S(1)}, s32[4096]{0:T(1024)}, u32[]{:S(2)}) copy-start(s32[4096]{0:T(1024)} %param.13) | copy-start | bytes 49156
  120.5 43.0 %copy-start.5 = (bf16[128,3,64,1]{0,3,2,1:T(2,128)(2,1)S(1)}, bf16[128,3,64,1]{0,3,2,1:T(2,128)(2,1)}, u32[]{:S(2)}) copy-start(bf16[128,3,64,1]{0,3,2,1:T(2,128)(2,1)} %get-tuple-element.22) | copy-start | bytes 147460
  120.5 43.0 %copy-start.6 = (bf16[128,3,64,1]{0,3,2,1:T(2,128)(2,1)S(1)}, bf16[128,3,64,1]{0,3,2,1:T(2,128)(2,1)}, u32[]{:S(2)}) copy-start(bf16[128,3,64,1]{0,3,2,1:T(2,128)(2,1)} %get-tuple-element.23) | copy-start | bytes 147460
  160.8 6.0 %collective-permute-start.1 = (bf16[16,128,3,256]{3,1,2,0:T(8,128)(2,1)}, bf16[16,128,3,256]{3,1,2,0:T(8,128)(2,1)}, u32[]{:S(2)}, u32[]{:S(2)}) collective-permute-start(bf16[16,128,3,256]{3,1,2,0:T(8,128)(2,1)} %all_to_all.88), channel_id=1, source_target_pairs={{0,32},{32,0},{1,33},{33,1},{2,34},{34,2},{3,35},{35,3},{4,36},{36... | collective-permute-start | bytes 9437192 | tf_op jit(solution)/shard_map/ppermute | solution.py:198
  171.4 0.7 copy-start.9
  192.0 16.8 %all-to-all-start.5 = ((bf16[16,32,96]{2,0,1:T(8,128)(2,1)}), bf16[16,32,96]{2,0,1:T(8,128)(2,1)S(1)}, u32[]{:S(2)}, u32[]{:S(2)}) async-start(bf16[16,32,96]{2,0,1:T(8,128)(2,1)} %bitcast.37), calls=%async_computation.5 | async-start | bytes 262144 | tf_op jit(solution)/shard_map/all_to_all | solution.py:217
  239.4 26.0 %all-to-all-start.7 = ((bf16[16,2,16,1536]{3,2,1,0:T(8,128)(2,1)}), bf16[16,2,16,1536]{3,2,1,0:T(8,128)(2,1)}, u32[]{:S(2)}, u32[]{:S(2)}) async-start(bf16[16,2,16,1536]{3,2,1,0:T(8,128)(2,1)} %bitcast.117), calls=%async_computation.7 | async-start | bytes 3145728 | tf_op jit(solution)/shard_map/all_to_all | solution.py:86
  246.1 26.5 %collective-permute-start.2 = (f32[16,1536]{1,0:T(8,128)}, f32[16,1536]{1,0:T(8,128)}, u32[]{:S(2)}, u32[]{:S(2)}) collective-permute-start(f32[16,1536]{1,0:T(8,128)} %select_bitcast_fusion.3), channel_id=1, source_target_pairs={{0,4},{4,0},{1,5},{5,1},{2,6},{6,2},{3,7},{7,3},{8,12},{12,8},{9,1... | collective-permute-start | bytes 294920 | tf_op jit(solution)/shard_map/ppermute | solution.py:89
  267.1 8.6 %collective-permute-start.3 = (f32[16,1536]{1,0:T(8,128)S(1)}, f32[16,1536]{1,0:T(8,128)S(1)}, u32[]{:S(2)}, u32[]{:S(2)}) collective-permute-start(f32[16,1536]{1,0:T(8,128)S(1)} %select_bitcast_fusion.2), channel_id=1, source_target_pairs={{0,4},{4,0},{1,5},{5,1},{2,6},{6,2},{3,7},{7,3},{8,12},{12,8},{9,1... | collective-permute-start | bytes 294920 | tf_op jit(solution)/shard_map/ppermute | solution.py:89

commit v10 on v8

--- a/solution.py
+++ b/solution.py
@@ -84,7 +84,7 @@
     got = lax.all_to_all(pieces, PLANE, 0, 0, tiled=True)
     part = jnp.sum(got.astype(jnp.float32), axis=0)
     mine, theirs = by_half(part[0], part[1])
-    return mine + lax.ppermute(theirs, "zh", SWAP)
+    return mine + lax.ppermute(theirs.astype(jnp.bfloat16), "zh", SWAP).astype(jnp.float32)
 
 
 def body(

time: 270 us -> 267 us (0.989)
  no operation moved by 1% of the time
where the time goes in v10:
time: 267 us; the launch traced here: 265 us
  blocking collectives  140 us (52%)
  waiting for transfers between devices  33.4 us (13%)
  starting transfers between devices  29.8 us (11%)
  matrix products  24.6 us (9%)
  local copies, waits for them, and re-layouts  19.3 us (7%)
  other arithmetic  17.8 us (7%)
    all_to_all x1, blocking collectives, gather_plane(): lax.all_to_all(jnp.broadcast_to(pair[None], (plane,) + pair.shape), PLANE...  45.1 us
    all_to_all x1, blocking collectives, reduce_blk(): got = lax.all_to_all(pieces, PLANE, 0, 0, tiled=True)  42.4 us
    all_to_all x1, blocking collectives, body(): lax.all_to_all(jnp.broadcast_to(kv_rows[None], (ys * xs,) + kv_rows.shape...  40.3 us
    all_to_all x1, blocking collectives, body(): lax.all_to_all(attended, group, split_axis=0, concat_axis=1, tiled=True)  11.7 us
    all_to_all x1, waiting for transfers between devices, body(): lax.all_to_all(qkv_cols, ('y', 'x', 'zh'), split_axis=0, concat_axis=1, t...  11 us
    dot_general x1, matrix products, body(): jnp.dot(mlp_act, w_mlp_out, preferred_element_type=jnp.float32)  8.81 us
    all_to_all x1, starting transfers between devices, body(): lax.all_to_all(qkv_cols, ('y', 'x', 'zh'), split_axis=0, concat_axis=1, t...  8.2 us
    all_to_all x1, waiting for transfers between devices, body(): lax.all_to_all(by_token, group, split_axis=1, concat_axis=0, tiled=True)  8.13 us
  transfers between devices with their start and end apart: 6, of which 6 were waited for; matrix products, arithmetic and copies ran while one was open for 8% of the time, Pallas kernels for 0%

profile of v10, /device:TPU:32, one launch (start us, length us, event | category | flops | bytes accessed | tf_op | source)
XLA Modules:
  0.0 264.9 jit_solution(11420811903716783607)
XLA Ops:
  0.0 6.3 %collective-permute-start = (f32[16,3072]{1,0:T(8,128)}, f32[16,3072]{1,0:T(8,128)S(1)}, u32[]{:S(2)}, u32[]{:S(2)}) collective-permute-start(f32[16,3072]{1,0:T(8,128)} %param.12), channel_id=1, source_target_pairs={{0,4},{4,0},{1,5},{5,1},{2,6},{6,2},{3,7},{7,3},{8,12},{12,8},{9,1... | collective-permute-start | bytes 589832 | tf_op jit(solution)/shard_map/ppermute | solution.py:118
  6.3 0.8 reduce-window.8
  7.1 0.7 fusion.56
  7.9 2.8 %fusion = f32[4,1,9216]{2,1,0:T(1,128)S(1)} fusion(bf16[4,28,9216]{2,0,1:T(4,128)(2,1)} %bitcast.117, pred[4,28,1]{1,0,2:T(4,128)(4,1)S(1)} %fusion.56), kind=kOutput, calls=%fused_computation.8 | convolution fusion | flops 2064384 | bytes 2211952 | tf_op jit(solution)/shard_map/rs,rsk->rk/dot_general | solution.py:122
  10.8 0.4 fusion.44
  11.2 1.3 fusion.42
  12.6 0.2 multiply_reduce_fusion.3
  12.8 2.9 %collective-permute-done = f32[16,3072]{1,0:T(8,128)S(1)} collective-permute-done((f32[16,3072]{1,0:T(8,128)}, f32[16,3072]{1,0:T(8,128)S(1)}, u32[]{:S(2)}, u32[]{:S(2)}) %collective-permute-start) | collective-permute-done | bytes 196640 | tf_op jit(solution)/shard_map/ppermute | solution.py:118
  15.8 0.2 multiply_reduce_fusion.2
  16.1 1.2 select_bitcast_fusion.3
  17.3 0.4 broadcast_in_dim.53
  17.7 45.1 %all_to_all.82 = bf16[16,2,16,3072]{3,2,1,0:T(8,128)(2,1)S(1)} all-to-all(bf16[16,2,16,3072]{3,2,1,0:T(8,128)(2,1)S(1)} %broadcast_in_dim.53), channel_id=1, replica_groups=mesh['zl'=4,'core'=2,'y'=4,'zh'=2,'x'=4] {'y','x'}, dimensions={0} | all-to-all | bytes 6291456 | tf_op jit(solution)/shard_map/all_to_all | solution.py:77
  62.8 1.7 copy-done.1
  64.5 1.1 convolution_convert_fusion
  65.6 0.9 copy.85
  66.6 8.2 %all-to-all-start.1 = ((bf16[32,16,288]{2,1,0:T(8,128)(2,1)}), bf16[32,16,288]{2,1,0:T(8,128)(2,1)S(1)}, u32[]{:S(2)}, u32[]{:S(2)}) async-start(bf16[32,16,288]{2,1,0:T(8,128)(2,1)} %bitcast.119), calls=%async_computation.1 | async-start | bytes 786432 | tf_op jit(solution)/shard_map/all_to_all | solution.py:156
  74.8 0.7 mul.250
  75.5 0.7 mul.239
  76.3 1.9 reshape.484
  78.2 0.9 convert_reduce_fusion.2
  79.1 11.0 %all-to-all-done.1 = bf16[32,16,288]{2,1,0:T(8,128)(2,1)S(1)} async-done(((bf16[32,16,288]{2,1,0:T(8,128)(2,1)}), bf16[32,16,288]{2,1,0:T(8,128)(2,1)S(1)}, u32[]{:S(2)}, u32[]{:S(2)}) %all-to-all-start.1) | async-done | bytes 294944 | tf_op jit(solution)/shard_map/all_to_all | solution.py:156
  90.1 0.9 copy.132
  91.0 1.3 all_to_all.63
  92.4 0.7 copy.87
  93.1 5.4 %all-to-all-start.2 = ((bf16[16,8,1152]{2,0,1:T(8,128)(2,1)}), bf16[16,8,1152]{2,0,1:T(8,128)(2,1)S(1)}, u32[]{:S(2)}, u32[]{:S(2)}) async-start(bf16[16,8,1152]{2,0,1:T(8,128)(2,1)} %copy.87), calls=%async_computation.2 | async-start | bytes 589824 | tf_op jit(solution)/shard_map/all_to_all | solution.py:159
  98.6 0.7 fusion.74
  99.4 8.1 %all-to-all-done.2 = bf16[16,8,1152]{2,0,1:T(8,128)(2,1)S(1)} async-done(((bf16[16,8,1152]{2,0,1:T(8,128)(2,1)}), bf16[16,8,1152]{2,0,1:T(8,128)(2,1)S(1)}, u32[]{:S(2)}, u32[]{:S(2)}) %all-to-all-start.2) | async-done | bytes 294944 | tf_op jit(solution)/shard_map/all_to_all | solution.py:159
  107.5 0.7 copy-done.3
  108.2 1.0 reshape.486
  109.3 1.1 fusion.73
  110.3 0.7 copy_convert_fusion
  111.3 1.7 copy.94
  113.1 0.8 copy.89
  113.9 0.8 copy.108
  114.7 1.1 multiply_multiply_fusion.1
  115.7 1.1 multiply_multiply_fusion.2
  116.8 2.0 subtract_convert_fusion.1
  118.8 0.2 pad_maximum_fusion.4
  119.0 0.9 pad_maximum_fusion.2
  120.1 0.4 broadcast_in_dim.54
  120.5 40.3 %all_to_all.83 = bf16[16,128,3,256]{3,1,2,0:T(8,128)(2,1)} all-to-all(bf16[16,128,3,256]{3,1,2,0:T(8,128)(2,1)S(1)} %broadcast_in_dim.54), channel_id=1, replica_groups=mesh['zl'=4,'core'=2,'y'=4,'zh'=2,'x'=4] {'y','x'}, dimensions={0} | all-to-all | bytes 6291456 | tf_op jit(solution)/shard_map/all_to_all | solution.py:192
  161.7 0.2 pad_maximum_fusion.3
  161.9 4.9 %collective-permute-done.1 = bf16[16,128,3,256]{3,1,2,0:T(8,128)(2,1)} collective-permute-done((bf16[16,128,3,256]{3,1,2,0:T(8,128)(2,1)}, bf16[16,128,3,256]{3,1,2,0:T(8,128)(2,1)}, u32[]{:S(2)}, u32[]{:S(2)}) %collective-permute-start.1) | collective-permute-done | bytes 3145760 | tf_op jit(solution)/shard_map/ppermute | solution.py:195
  166.8 3.3 %select_bitcast_fusion.1 = (bf16[1,16,128,3,256]{4,2,3,1,0:T(8,128)(2,1)S(1)}, bf16[1,16,128,3,256]{4,2,3,1,0:T(8,128)(2,1)S(1)}) fusion(bf16[16,128,3,256]{3,1,2,0:T(8,128)(2,1)} %all_to_all.83, bf16[16,128,3,256]{3,1,2,0:T(8,128)(2,1)} %collective-permute-done.1, pred[]{:T(512)S(6)} %eq.141), kind=kLoop, calls=%fused_computation.7 | loop fusion | flops 3145728 | bytes 12582913 | tf_op jit(solution)/shard_map/stack | solution.py:196
  170.1 0.6 pad_maximum_fusion
  170.6 0.8 copy.100
  171.4 0.5 convolution_multiply_fusion
  171.9 1.0 select_reduce_fusion.2
  173.0 1.7 fusion.2
  174.7 1.0 fusion.13
  175.7 1.4 fusion.4
  177.1 1.0 fusion.12
  178.1 1.0 fusion.11
  179.3 11.7 %all_to_all.84 = bf16[8,16,384]{2,1,0:T(8,128)(2,1)S(1)} all-to-all(bf16[8,16,384]{2,1,0:T(8,128)(2,1)S(1)} %all_to_all.67), channel_id=1, replica_groups=mesh['zl'=4,'core'=2,'y'=4,'zh'=2,'x'=4] {'zl','zh'}, dimensions={0} | all-to-all | bytes 196608 | tf_op jit(solution)/shard_map/all_to_all | solution.py:212
  191.2 0.7 copy.104
  191.8 4.3 %all-to-all-start.5 = ((bf16[16,32,96]{2,0,1:T(8,128)(2,1)}), bf16[16,32,96]{2,0,1:T(8,128)(2,1)S(1)}, u32[]{:S(2)}, u32[]{:S(2)}) async-start(bf16[16,32,96]{2,0,1:T(8,128)(2,1)} %bitcast.37), calls=%async_computation.5 | async-start | bytes 262144 | tf_op jit(solution)/shard_map/all_to_all | solution.py:214
  196.2 8.8 %fusion.31 = f32[512,3072]{1,0:T(8,128)} fusion(bf16[384,3072]{1,0:T(8,128)(2,1)S(1)} %copy-done, bf16[512,3072]{1,0:T(8,128)(2,1)} %bitcast.116, bf16[3072,384]{1,0:T(8,128)(2,1)} %param.19), kind=kOutput, calls=%fused_computation.54 | convolution fusion | flops 2417688576 | bytes 14155776 | tf_op jit(solution)/shard_map/dot_general | solution.py:216
  205.0 3.6 %all-to-all-done.5 = bf16[16,32,96]{2,0,1:T(8,128)(2,1)S(1)} async-done(((bf16[16,32,96]{2,0,1:T(8,128)(2,1)}), bf16[16,32,96]{2,0,1:T(8,128)(2,1)S(1)}, u32[]{:S(2)}, u32[]{:S(2)}) %all-to-all-start.5) | async-done | bytes 98336 | tf_op jit(solution)/shard_map/all_to_all | solution.py:214
  208.6 4.0 %add_convert_fusion = bf16[512,3072]{1,0:T(8,128)(2,1)S(1)} fusion(f32[512,3072]{1,0:T(8,128)} %fusion.31, bf16[512,96]{1,0:T(8,128)(2,1)S(1)} %bitcast.124, bf16[96,3072]{1,0:T(8,128)(2,1)} %param.22), kind=kOutput, calls=%fused_computation.2 | convolution fusion | flops 305135616 | bytes 10125312 | tf_op jit(solution)/shard_map/dot_general | solution.py:218
  212.6 42.4 %all_to_all.85 = bf16[16,2,16,3072]{3,2,1,0:T(8,128)(2,1)S(1)} all-to-all(bf16[16,2,16,3072]{3,2,1,0:T(8,128)(2,1)S(1)} %bitcast.108), channel_id=1, replica_groups=mesh['zl'=4,'core'=2,'y'=4,'zh'=2,'x'=4] {'y','x'}, dimensions={0} | all-to-all | bytes 6291456 | tf_op jit(solution)/shard_map/all_to_all | solution.py:84
  254.9 0.6 convert_reduce_fusion
  255.5 5.6 %collective-permute-start.2 = (bf16[16,3072]{1,0:T(8,128)(2,1)S(1)}, bf16[16,3072]{1,0:T(8,128)(2,1)S(1)}, u32[]{:S(2)}, u32[]{:S(2)}) collective-permute-start(bf16[16,3072]{1,0:T(8,128)(2,1)S(1)} %fusion.48), channel_id=1, source_target_pairs={{0,4},{4,0},{1,5},{5,1},{2,6},{6,2},{3,7},{7,3},{8,12},{12,8},{9,1... | collective-permute-start | bytes 294920 | tf_op jit(solution)/shard_map/ppermute | solution.py:87
  261.1 3.0 %collective-permute-done.2 = bf16[16,3072]{1,0:T(8,128)(2,1)S(1)} collective-permute-done((bf16[16,3072]{1,0:T(8,128)(2,1)S(1)}, bf16[16,3072]{1,0:T(8,128)(2,1)S(1)}, u32[]{:S(2)}, u32[]{:S(2)}) %collective-permute-start.2) | collective-permute-done | bytes 98336 | tf_op jit(solution)/shard_map/ppermute | solution.py:87
  264.1 0.7 fusion.41
  (61 shorter events, 2.3 us)
Async XLA Ops:
  0.0 196.2 %copy-start = (bf16[384,3072]{1,0:T(8,128)(2,1)S(1)}, bf16[384,3072]{1,0:T(8,128)(2,1)}, u32[]{:S(2)}) copy-start(bf16[384,3072]{1,0:T(8,128)(2,1)} %param.23) | copy-start | bytes 7077892
  0.0 12.5 %copy-start.2 = (f32[16,3072]{1,0:T(8,128)S(1)}, f32[16,3072]{1,0:T(8,128)}, u32[]{:S(2)}) copy-start(f32[16,3072]{1,0:T(8,128)} %param.12) | copy-start | bytes 589828
  0.0 15.7 %collective-permute-start = (f32[16,3072]{1,0:T(8,128)}, f32[16,3072]{1,0:T(8,128)S(1)}, u32[]{:S(2)}, u32[]{:S(2)}) collective-permute-start(f32[16,3072]{1,0:T(8,128)} %param.12), channel_id=1, source_target_pairs={{0,4},{4,0},{1,5},{5,1},{2,6},{6,2},{3,7},{7,3},{8,12},{12,8},{9,1... | collective-permute-start | bytes 589832 | tf_op jit(solution)/shard_map/ppermute | solution.py:118
  7.1 3.6 %copy-start.8 = (s32[4,1]{0,1:T(1,128)}, s32[4,1]{0,1:T(1,128)S(1)}, u32[]{:S(2)}) copy-start(s32[4,1]{0,1:T(1,128)S(1)} %reduce-window.8) | copy-start | bytes 52
  17.7 46.9 %copy-start.12 = (bf16[3072,288]{0,1:T(8,128)(2,1)S(1)}, bf16[3072,288]{0,1:T(8,128)(2,1)}, u32[]{:S(2)}) copy-start(bf16[3072,288]{0,1:T(8,128)(2,1)} %param.18) | copy-start | bytes 5308420
  62.8 1.7 copy-start.1
  64.5 10.2 %copy-start.10 = (f32[128]{0:T(128)S(1)}, f32[128]{0:T(128)}, u32[]{:S(2)}) copy-start(f32[128]{0:T(128)} %param.21) | copy-start | bytes 1540
  64.5 11.0 %copy-start.11 = (f32[128]{0:T(128)S(1)}, f32[128]{0:T(128)}, u32[]{:S(2)}) copy-start(f32[128]{0:T(128)} %param.20) | copy-start | bytes 1540
  66.6 23.5 %all-to-all-start.1 = ((bf16[32,16,288]{2,1,0:T(8,128)(2,1)}), bf16[32,16,288]{2,1,0:T(8,128)(2,1)S(1)}, u32[]{:S(2)}, u32[]{:S(2)}) async-start(bf16[32,16,288]{2,1,0:T(8,128)(2,1)} %bitcast.119), calls=%async_computation.1 | async-start | bytes 786432 | tf_op jit(solution)/shard_map/all_to_all | solution.py:156
  93.1 14.4 %all-to-all-start.2 = ((bf16[16,8,1152]{2,0,1:T(8,128)(2,1)}), bf16[16,8,1152]{2,0,1:T(8,128)(2,1)S(1)}, u32[]{:S(2)}, u32[]{:S(2)}) async-start(bf16[16,8,1152]{2,0,1:T(8,128)(2,1)} %copy.87), calls=%async_computation.2 | async-start | bytes 589824 | tf_op jit(solution)/shard_map/all_to_all | solution.py:159
  107.5 0.7 copy-start.3
  110.3 3.6 %copy-start.4 = (bf16[128,3,1,128]{3,2,1,0:T(2,128)(2,1)S(1)}, bf16[128,3,1,128]{3,2,1,0:T(2,128)(2,1)}, u32[]{:S(2)}) copy-start(bf16[128,3,1,128]{3,2,1,0:T(2,128)(2,1)} %get-tuple-element.18) | copy-start | bytes 294916
  120.5 40.7 %copy-start.7 = (s32[4096]{0:T(1024)S(1)}, s32[4096]{0:T(1024)}, u32[]{:S(2)}) copy-start(s32[4096]{0:T(1024)} %param.13) | copy-start | bytes 49156
  120.5 41.0 %copy-start.9 = (s32[4,1]{0,1:T(1,128)S(1)}, s32[4,1]{0,1:T(1,128)}, u32[]{:S(2)}) copy-start(s32[4,1]{0,1:T(1,128)} %copy-done.8) | copy-start | bytes 52
  120.5 41.2 %copy-start.5 = (bf16[128,3,64,1]{0,3,2,1:T(2,128)(2,1)S(1)}, bf16[128,3,64,1]{0,3,2,1:T(2,128)(2,1)}, u32[]{:S(2)}) copy-start(bf16[128,3,64,1]{0,3,2,1:T(2,128)(2,1)} %get-tuple-element.20) | copy-start | bytes 147460
  120.5 41.2 %copy-start.6 = (bf16[128,3,64,1]{0,3,2,1:T(2,128)(2,1)S(1)}, bf16[128,3,64,1]{0,3,2,1:T(2,128)(2,1)}, u32[]{:S(2)}) copy-start(bf16[128,3,64,1]{0,3,2,1:T(2,128)(2,1)} %get-tuple-element.21) | copy-start | bytes 147460
  160.8 6.0 %collective-permute-start.1 = (bf16[16,128,3,256]{3,1,2,0:T(8,128)(2,1)}, bf16[16,128,3,256]{3,1,2,0:T(8,128)(2,1)}, u32[]{:S(2)}, u32[]{:S(2)}) collective-permute-start(bf16[16,128,3,256]{3,1,2,0:T(8,128)(2,1)} %all_to_all.83), channel_id=1, source_target_pairs={{0,32},{32,0},{1,33},{33,1},{2,34},{34,2},{3,35},{35,3},{4,36},{36... | collective-permute-start | bytes 9437192 | tf_op jit(solution)/shard_map/ppermute | solution.py:195
  191.8 16.8 %all-to-all-start.5 = ((bf16[16,32,96]{2,0,1:T(8,128)(2,1)}), bf16[16,32,96]{2,0,1:T(8,128)(2,1)S(1)}, u32[]{:S(2)}, u32[]{:S(2)}) async-start(bf16[16,32,96]{2,0,1:T(8,128)(2,1)} %bitcast.37), calls=%async_computation.5 | async-start | bytes 262144 | tf_op jit(solution)/shard_map/all_to_all | solution.py:214
  255.5 8.6 %collective-permute-start.2 = (bf16[16,3072]{1,0:T(8,128)(2,1)S(1)}, bf16[16,3072]{1,0:T(8,128)(2,1)S(1)}, u32[]{:S(2)}, u32[]{:S(2)}) collective-permute-start(bf16[16,3072]{1,0:T(8,128)(2,1)S(1)} %fusion.48), channel_id=1, source_target_pairs={{0,4},{4,0},{1,5},{5,1},{2,6},{6,2},{3,7},{7,3},{8,12},{12,8},{9,1... | collective-permute-start | bytes 294920 | tf_op jit(solution)/shard_map/ppermute | solution.py:87

commit v11 on v10

--- a/solution.py
+++ b/solution.py
@@ -181,19 +181,21 @@
     value_rows = heads4[:, :, 2]
     kv_rows = jnp.concatenate([key_rot, value_rows], axis=2)
     key_order = (1, 2, 4, 0, 3, 5)
-    key_ids = token_grid.transpose(key_order).reshape(-1)
+    first_core = core_at == 0
+    key_grid = token_grid.transpose(key_order)
+    key_ids = jnp.where(first_core, key_grid, key_grid[::-1]).reshape(-1)
     key_request = segment_of(key_ids, request_ends)
-    kept = key_keep.reshape(digits).transpose(key_order).reshape(-1) == 1
+    keep_grid = key_keep.reshape(digits).transpose(key_order)
+    kept = jnp.where(first_core, keep_grid, keep_grid[::-1]).reshape(-1) == 1
     visible = (query_request[:, None] == key_request[None, :]) & (
         kept[None, :] | (query_ids[:, None] == key_ids[None, :])
     )
-    first_core = core_at == 0
     head_out = []
     got = lax.all_to_all(
         jnp.broadcast_to(kv_rows[None], (ys * xs,) + kv_rows.shape), PLANE, 0, 0, tiled=True
     )
     sibling = lax.ppermute(got, "core", SWAP)
-    both = jnp.stack([jnp.where(first_core, got, sibling), jnp.where(first_core, sibling, got)])
+    both = jnp.stack([got, sibling])
     both = both.reshape((-1,) + kv_rows.shape[1:])
     for head in range(local_heads):
         key_h = both[:, head, :head_size]

time: 267 us -> 266 us (level)
    another operation x4 -> x3, other arithmetic: 6.63 us -> 6.22 us  [the longest x1 3.42 us: body(): both = jnp.stack([got, sibling])]
where the time goes in v11:
time: 266 us; the launch traced here: 264 us
  blocking collectives  140 us (53%)
  waiting for transfers between devices  33.3 us (13%)
  starting transfers between devices  29.8 us (11%)
  matrix products  24.6 us (9%)
  local copies, waits for them, and re-layouts  19.4 us (7%)
  other arithmetic  17.5 us (7%)
    all_to_all x1, blocking collectives, gather_plane(): lax.all_to_all(jnp.broadcast_to(pair[None], (plane,) + pair.shape), PLANE...  45.1 us
    all_to_all x1, blocking collectives, reduce_blk(): got = lax.all_to_all(pieces, PLANE, 0, 0, tiled=True)  42.4 us
    all_to_all x1, blocking collectives, body(): lax.all_to_all(jnp.broadcast_to(kv_rows[None], (ys * xs,) + kv_rows.shape...  40.3 us
    all_to_all x1, blocking collectives, body(): lax.all_to_all(attended, group, split_axis=0, concat_axis=1, tiled=True)  11.7 us
    all_to_all x1, waiting for transfers between devices, body(): lax.all_to_all(qkv_cols, ('y', 'x', 'zh'), split_axis=0, concat_axis=1, t...  11 us
    dot_general x1, matrix products, body(): jnp.dot(mlp_act, w_mlp_out, preferred_element_type=jnp.float32)  8.81 us
    all_to_all x1, starting transfers between devices, body(): lax.all_to_all(qkv_cols, ('y', 'x', 'zh'), split_axis=0, concat_axis=1, t...  8.2 us
    all_to_all x1, waiting for transfers between devices, body(): lax.all_to_all(by_token, group, split_axis=1, concat_axis=0, tiled=True)  8.13 us
  transfers between devices with their start and end apart: 6, of which 6 were waited for; matrix products, arithmetic and copies ran while one was open for 8% of the time, Pallas kernels for 0%

profile of v11, /device:TPU:32, one launch (start us, length us, event | category | flops | bytes accessed | tf_op | source)
XLA Modules:
  0.0 264.4 jit_solution(6887375808433064709)
XLA Ops:
  0.0 6.3 %collective-permute-start = (f32[16,3072]{1,0:T(8,128)}, f32[16,3072]{1,0:T(8,128)S(1)}, u32[]{:S(2)}, u32[]{:S(2)}) collective-permute-start(f32[16,3072]{1,0:T(8,128)} %param.12), channel_id=1, source_target_pairs={{0,4},{4,0},{1,5},{5,1},{2,6},{6,2},{3,7},{7,3},{8,12},{12,8},{9,1... | collective-permute-start | bytes 589832 | tf_op jit(solution)/shard_map/ppermute | solution.py:118
  6.3 0.8 reduce-window.8
  7.1 0.7 fusion.57
  7.9 2.8 %fusion = f32[4,1,9216]{2,1,0:T(1,128)S(1)} fusion(bf16[4,28,9216]{2,0,1:T(4,128)(2,1)} %bitcast.115, pred[4,28,1]{1,0,2:T(4,128)(4,1)S(1)} %fusion.57), kind=kOutput, calls=%fused_computation.6 | convolution fusion | flops 2064384 | bytes 2211952 | tf_op jit(solution)/shard_map/rs,rsk->rk/dot_general | solution.py:122
  10.8 0.4 fusion.44
  11.2 1.3 fusion.42
  12.6 0.2 multiply_reduce_fusion.3
  12.8 2.9 %collective-permute-done = f32[16,3072]{1,0:T(8,128)S(1)} collective-permute-done((f32[16,3072]{1,0:T(8,128)}, f32[16,3072]{1,0:T(8,128)S(1)}, u32[]{:S(2)}, u32[]{:S(2)}) %collective-permute-start) | collective-permute-done | bytes 196640 | tf_op jit(solution)/shard_map/ppermute | solution.py:118
  15.8 0.2 multiply_reduce_fusion.2
  16.1 1.2 select_bitcast_fusion.1
  17.3 0.4 broadcast_in_dim.53
  17.7 45.1 %all_to_all.82 = bf16[16,2,16,3072]{3,2,1,0:T(8,128)(2,1)S(1)} all-to-all(bf16[16,2,16,3072]{3,2,1,0:T(8,128)(2,1)S(1)} %broadcast_in_dim.53), channel_id=1, replica_groups=mesh['zl'=4,'core'=2,'y'=4,'zh'=2,'x'=4] {'y','x'}, dimensions={0} | all-to-all | bytes 6291456 | tf_op jit(solution)/shard_map/all_to_all | solution.py:77
  62.8 1.7 copy-done.1
  64.5 1.1 convolution_convert_fusion
  65.6 0.9 copy.90
  66.6 8.2 %all-to-all-start.1 = ((bf16[32,16,288]{2,1,0:T(8,128)(2,1)}), bf16[32,16,288]{2,1,0:T(8,128)(2,1)S(1)}, u32[]{:S(2)}, u32[]{:S(2)}) async-start(bf16[32,16,288]{2,1,0:T(8,128)(2,1)} %bitcast.117), calls=%async_computation.1 | async-start | bytes 786432 | tf_op jit(solution)/shard_map/all_to_all | solution.py:156
  74.8 0.7 mul.250
  75.5 0.7 mul.239
  76.3 1.9 reshape.367
  78.2 0.9 convert_reduce_fusion.2
  79.1 11.0 %all-to-all-done.1 = bf16[32,16,288]{2,1,0:T(8,128)(2,1)S(1)} async-done(((bf16[32,16,288]{2,1,0:T(8,128)(2,1)}), bf16[32,16,288]{2,1,0:T(8,128)(2,1)S(1)}, u32[]{:S(2)}, u32[]{:S(2)}) %all-to-all-start.1) | async-done | bytes 294944 | tf_op jit(solution)/shard_map/all_to_all | solution.py:156
  90.1 0.9 copy.137
  91.0 1.3 all_to_all.63
  92.4 0.7 copy.92
  93.1 5.4 %all-to-all-start.2 = ((bf16[16,8,1152]{2,0,1:T(8,128)(2,1)}), bf16[16,8,1152]{2,0,1:T(8,128)(2,1)S(1)}, u32[]{:S(2)}, u32[]{:S(2)}) async-start(bf16[16,8,1152]{2,0,1:T(8,128)(2,1)} %copy.92), calls=%async_computation.2 | async-start | bytes 589824 | tf_op jit(solution)/shard_map/all_to_all | solution.py:159
  98.6 0.7 fusion.75
  99.4 8.1 %all-to-all-done.2 = bf16[16,8,1152]{2,0,1:T(8,128)(2,1)S(1)} async-done(((bf16[16,8,1152]{2,0,1:T(8,128)(2,1)}), bf16[16,8,1152]{2,0,1:T(8,128)(2,1)S(1)}, u32[]{:S(2)}, u32[]{:S(2)}) %all-to-all-start.2) | async-done | bytes 294944 | tf_op jit(solution)/shard_map/all_to_all | solution.py:159
  107.5 0.7 copy-done.3
  108.2 1.0 reshape.369
  109.3 1.1 fusion.74
  110.3 0.7 copy_convert_fusion
  111.3 1.7 copy.99
  113.1 0.8 copy.94
  113.9 0.8 copy.113
  114.7 1.1 multiply_multiply_fusion.1
  115.7 1.1 multiply_multiply_fusion.2
  116.8 2.0 subtract_convert_fusion.1
  118.8 0.2 pad_maximum_fusion.4
  119.0 0.9 pad_maximum_fusion.2
  120.1 0.4 broadcast_in_dim.54
  120.5 40.3 %all_to_all.83 = bf16[16,128,3,256]{3,1,2,0:T(8,128)(2,1)} all-to-all(bf16[16,128,3,256]{3,1,2,0:T(8,128)(2,1)S(1)} %broadcast_in_dim.54), channel_id=1, replica_groups=mesh['zl'=4,'core'=2,'y'=4,'zh'=2,'x'=4] {'y','x'}, dimensions={0} | all-to-all | bytes 6291456 | tf_op jit(solution)/shard_map/all_to_all | solution.py:194
  161.0 0.2 ge.61
  161.9 0.2 pad_maximum_fusion.3
  162.1 4.7 %collective-permute-done.1 = bf16[16,128,3,256]{3,1,2,0:T(8,128)(2,1)} collective-permute-done((bf16[16,128,3,256]{3,1,2,0:T(8,128)(2,1)}, bf16[16,128,3,256]{3,1,2,0:T(8,128)(2,1)}, u32[]{:S(2)}, u32[]{:S(2)}) %collective-permute-start.1) | collective-permute-done | bytes 3145760 | tf_op jit(solution)/shard_map/ppermute | solution.py:197
  166.8 3.4 %pad_maximum_fusion = bf16[2,16,128,3,256]{4,2,3,1,0:T(8,128)(2,1)S(1)} fusion(bf16[1,16,128,3,256]{4,2,3,1,0:T(8,128)(2,1)} %bitcast.22, bf16[1,16,128,3,256]{4,2,3,1,0:T(8,128)(2,1)} %bitcast.21), kind=kLoop, calls=%fused_computation | loop fusion | flops 3145728 | bytes 12582912 | tf_op jit(solution)/shard_map/stack | solution.py:198
  170.2 0.8 copy.105
  171.0 0.5 convolution_multiply_fusion
  171.5 1.0 select_reduce_fusion.2
  172.5 1.7 fusion.2
  174.3 1.0 fusion.13
  175.3 1.4 fusion.4
  176.7 1.0 fusion.12
  177.7 1.0 fusion.11
  178.9 11.7 %all_to_all.84 = bf16[8,16,384]{2,1,0:T(8,128)(2,1)S(1)} all-to-all(bf16[8,16,384]{2,1,0:T(8,128)(2,1)S(1)} %all_to_all.67), channel_id=1, replica_groups=mesh['zl'=4,'core'=2,'y'=4,'zh'=2,'x'=4] {'zl','zh'}, dimensions={0} | all-to-all | bytes 196608 | tf_op jit(solution)/shard_map/all_to_all | solution.py:214
  190.7 0.7 copy.109
  191.4 4.3 %all-to-all-start.5 = ((bf16[16,32,96]{2,0,1:T(8,128)(2,1)}), bf16[16,32,96]{2,0,1:T(8,128)(2,1)S(1)}, u32[]{:S(2)}, u32[]{:S(2)}) async-start(bf16[16,32,96]{2,0,1:T(8,128)(2,1)} %bitcast.37), calls=%async_computation.5 | async-start | bytes 262144 | tf_op jit(solution)/shard_map/all_to_all | solution.py:216
  195.8 8.8 %fusion.31 = f32[512,3072]{1,0:T(8,128)} fusion(bf16[384,3072]{1,0:T(8,128)(2,1)S(1)} %copy-done, bf16[512,3072]{1,0:T(8,128)(2,1)} %bitcast.114, bf16[3072,384]{1,0:T(8,128)(2,1)} %param.19), kind=kOutput, calls=%fused_computation.52 | convolution fusion | flops 2417688576 | bytes 14155776 | tf_op jit(solution)/shard_map/dot_general | solution.py:218
  204.6 3.6 %all-to-all-done.5 = bf16[16,32,96]{2,0,1:T(8,128)(2,1)S(1)} async-done(((bf16[16,32,96]{2,0,1:T(8,128)(2,1)}), bf16[16,32,96]{2,0,1:T(8,128)(2,1)S(1)}, u32[]{:S(2)}, u32[]{:S(2)}) %all-to-all-start.5) | async-done | bytes 98336 | tf_op jit(solution)/shard_map/all_to_all | solution.py:216
  208.2 4.0 %add_convert_fusion = bf16[512,3072]{1,0:T(8,128)(2,1)S(1)} fusion(f32[512,3072]{1,0:T(8,128)} %fusion.31, bf16[512,96]{1,0:T(8,128)(2,1)S(1)} %bitcast.122, bf16[96,3072]{1,0:T(8,128)(2,1)} %param.22), kind=kOutput, calls=%fused_computation.2 | convolution fusion | flops 305135616 | bytes 10125312 | tf_op jit(solution)/shard_map/dot_general | solution.py:220
  212.1 42.4 %all_to_all.85 = bf16[16,2,16,3072]{3,2,1,0:T(8,128)(2,1)S(1)} all-to-all(bf16[16,2,16,3072]{3,2,1,0:T(8,128)(2,1)S(1)} %bitcast.106), channel_id=1, replica_groups=mesh['zl'=4,'core'=2,'y'=4,'zh'=2,'x'=4] {'y','x'}, dimensions={0} | all-to-all | bytes 6291456 | tf_op jit(solution)/shard_map/all_to_all | solution.py:84
  254.5 0.6 convert_reduce_fusion
  255.1 5.6 %collective-permute-start.2 = (bf16[16,3072]{1,0:T(8,128)(2,1)S(1)}, bf16[16,3072]{1,0:T(8,128)(2,1)S(1)}, u32[]{:S(2)}, u32[]{:S(2)}) collective-permute-start(bf16[16,3072]{1,0:T(8,128)(2,1)S(1)} %fusion.49), channel_id=1, source_target_pairs={{0,4},{4,0},{1,5},{5,1},{2,6},{6,2},{3,7},{7,3},{8,12},{12,8},{9,1... | collective-permute-start | bytes 294920 | tf_op jit(solution)/shard_map/ppermute | solution.py:87
  260.7 3.0 %collective-permute-done.2 = bf16[16,3072]{1,0:T(8,128)(2,1)S(1)} collective-permute-done((bf16[16,3072]{1,0:T(8,128)(2,1)S(1)}, bf16[16,3072]{1,0:T(8,128)(2,1)S(1)}, u32[]{:S(2)}, u32[]{:S(2)}) %collective-permute-start.2) | collective-permute-done | bytes 98336 | tf_op jit(solution)/shard_map/ppermute | solution.py:87
  263.7 0.7 fusion.41
  (62 shorter events, 2.3 us)
Async XLA Ops:
  0.0 195.8 %copy-start = (bf16[384,3072]{1,0:T(8,128)(2,1)S(1)}, bf16[384,3072]{1,0:T(8,128)(2,1)}, u32[]{:S(2)}) copy-start(bf16[384,3072]{1,0:T(8,128)(2,1)} %param.23) | copy-start | bytes 7077892
  0.0 12.5 %copy-start.2 = (f32[16,3072]{1,0:T(8,128)S(1)}, f32[16,3072]{1,0:T(8,128)}, u32[]{:S(2)}) copy-start(f32[16,3072]{1,0:T(8,128)} %param.12) | copy-start | bytes 589828
  0.0 15.7 %collective-permute-start = (f32[16,3072]{1,0:T(8,128)}, f32[16,3072]{1,0:T(8,128)S(1)}, u32[]{:S(2)}, u32[]{:S(2)}) collective-permute-start(f32[16,3072]{1,0:T(8,128)} %param.12), channel_id=1, source_target_pairs={{0,4},{4,0},{1,5},{5,1},{2,6},{6,2},{3,7},{7,3},{8,12},{12,8},{9,1... | collective-permute-start | bytes 589832 | tf_op jit(solution)/shard_map/ppermute | solution.py:118
  7.1 3.6 %copy-start.8 = (s32[4,1]{0,1:T(1,128)}, s32[4,1]{0,1:T(1,128)S(1)}, u32[]{:S(2)}) copy-start(s32[4,1]{0,1:T(1,128)S(1)} %reduce-window.8) | copy-start | bytes 52
  17.7 46.9 %copy-start.12 = (bf16[3072,288]{0,1:T(8,128)(2,1)S(1)}, bf16[3072,288]{0,1:T(8,128)(2,1)}, u32[]{:S(2)}) copy-start(bf16[3072,288]{0,1:T(8,128)(2,1)} %param.18) | copy-start | bytes 5308420
  62.8 1.7 copy-start.1
  64.5 10.2 %copy-start.10 = (f32[128]{0:T(128)S(1)}, f32[128]{0:T(128)}, u32[]{:S(2)}) copy-start(f32[128]{0:T(128)} %param.21) | copy-start | bytes 1540
  64.5 11.0 %copy-start.11 = (f32[128]{0:T(128)S(1)}, f32[128]{0:T(128)}, u32[]{:S(2)}) copy-start(f32[128]{0:T(128)} %param.20) | copy-start | bytes 1540
  66.6 23.5 %all-to-all-start.1 = ((bf16[32,16,288]{2,1,0:T(8,128)(2,1)}), bf16[32,16,288]{2,1,0:T(8,128)(2,1)S(1)}, u32[]{:S(2)}, u32[]{:S(2)}) async-start(bf16[32,16,288]{2,1,0:T(8,128)(2,1)} %bitcast.117), calls=%async_computation.1 | async-start | bytes 786432 | tf_op jit(solution)/shard_map/all_to_all | solution.py:156
  93.1 14.4 %all-to-all-start.2 = ((bf16[16,8,1152]{2,0,1:T(8,128)(2,1)}), bf16[16,8,1152]{2,0,1:T(8,128)(2,1)S(1)}, u32[]{:S(2)}, u32[]{:S(2)}) async-start(bf16[16,8,1152]{2,0,1:T(8,128)(2,1)} %copy.92), calls=%async_computation.2 | async-start | bytes 589824 | tf_op jit(solution)/shard_map/all_to_all | solution.py:159
  107.5 0.7 copy-start.3
  110.3 3.6 %copy-start.4 = (bf16[128,3,1,128]{3,2,1,0:T(2,128)(2,1)S(1)}, bf16[128,3,1,128]{3,2,1,0:T(2,128)(2,1)}, u32[]{:S(2)}) copy-start(bf16[128,3,1,128]{3,2,1,0:T(2,128)(2,1)} %get-tuple-element.16) | copy-start | bytes 294916
  120.5 40.8 %copy-start.7 = (s32[4096]{0:T(1024)S(1)}, s32[4096]{0:T(1024)}, u32[]{:S(2)}) copy-start(s32[4096]{0:T(1024)} %param.13) | copy-start | bytes 49156
  120.5 41.2 %copy-start.9 = (s32[4,1]{0,1:T(1,128)S(1)}, s32[4,1]{0,1:T(1,128)}, u32[]{:S(2)}) copy-start(s32[4,1]{0,1:T(1,128)} %copy-done.8) | copy-start | bytes 52
  120.5 41.4 %copy-start.5 = (bf16[128,3,64,1]{0,3,2,1:T(2,128)(2,1)S(1)}, bf16[128,3,64,1]{0,3,2,1:T(2,128)(2,1)}, u32[]{:S(2)}) copy-start(bf16[128,3,64,1]{0,3,2,1:T(2,128)(2,1)} %get-tuple-element.18) | copy-start | bytes 147460
  120.5 41.4 %copy-start.6 = (bf16[128,3,64,1]{0,3,2,1:T(2,128)(2,1)S(1)}, bf16[128,3,64,1]{0,3,2,1:T(2,128)(2,1)}, u32[]{:S(2)}) copy-start(bf16[128,3,64,1]{0,3,2,1:T(2,128)(2,1)} %get-tuple-element.19) | copy-start | bytes 147460
  160.8 6.0 %collective-permute-start.1 = (bf16[16,128,3,256]{3,1,2,0:T(8,128)(2,1)}, bf16[16,128,3,256]{3,1,2,0:T(8,128)(2,1)}, u32[]{:S(2)}, u32[]{:S(2)}) collective-permute-start(bf16[16,128,3,256]{3,1,2,0:T(8,128)(2,1)} %all_to_all.83), channel_id=1, source_target_pairs={{0,32},{32,0},{1,33},{33,1},{2,34},{34,2},{3,35},{35,3},{4,36},{36... | collective-permute-start | bytes 9437192 | tf_op jit(solution)/shard_map/ppermute | solution.py:197
  191.4 16.7 %all-to-all-start.5 = ((bf16[16,32,96]{2,0,1:T(8,128)(2,1)}), bf16[16,32,96]{2,0,1:T(8,128)(2,1)S(1)}, u32[]{:S(2)}, u32[]{:S(2)}) async-start(bf16[16,32,96]{2,0,1:T(8,128)(2,1)} %bitcast.37), calls=%async_computation.5 | async-start | bytes 262144 | tf_op jit(solution)/shard_map/all_to_all | solution.py:216
  255.1 8.6 %collective-permute-start.2 = (bf16[16,3072]{1,0:T(8,128)(2,1)S(1)}, bf16[16,3072]{1,0:T(8,128)(2,1)S(1)}, u32[]{:S(2)}, u32[]{:S(2)}) collective-permute-start(bf16[16,3072]{1,0:T(8,128)(2,1)S(1)} %fusion.49), channel_id=1, source_target_pairs={{0,4},{4,0},{1,5},{5,1},{2,6},{6,2},{3,7},{7,3},{8,12},{12,8},{9,1... | collective-permute-start | bytes 294920 | tf_op jit(solution)/shard_map/ppermute | solution.py:87

commit v12 on v10

--- a/solution.py
+++ b/solution.py
@@ -212,9 +212,7 @@
     attn_feats = lax.all_to_all(attended, group, split_axis=0, concat_axis=1, tiled=True)
     attn_feats = attn_feats.reshape(block_rows, ys, 2, xs, -1).swapaxes(2, 3).reshape(block_rows, -1)
     attn_local = lax.all_to_all(attn_feats, ("y", "x", "zh"), split_axis=1, concat_axis=0, tiled=True)
-    mlp_out = lax.optimization_barrier(
-        jnp.dot(mlp_act, w_mlp_out, preferred_element_type=jnp.float32)
-    )
+    mlp_out = jnp.dot(mlp_act, w_mlp_out, preferred_element_type=jnp.float32)
     partial = (jnp.dot(attn_local, w_attn_out, preferred_element_type=jnp.float32) + mlp_out).astype(
         jnp.bfloat16
     )

time: 267 us -> 273 us (1.022)
  blocking collectives: 140 us -> 156 us
  starting transfers between devices: 29.8 us -> 19.4 us
    all_to_all x0 -> x1, blocking collectives: none -> 16.6 us  [body(): lax.all_to_all(attn_feats, ('y', 'x', 'zh'), split_axis=1, concat_axis=0,...]
    ppermute x1, waiting for transfers between devices: 3.01 us -> 7.85 us  [reduce_blk(): lax.ppermute(theirs.astype(jnp.bfloat16), 'zh', SWAP).astype(jnp.float32)]
    ppermute x1, starting transfers between devices: 5.6 us -> 0.76 us  [reduce_blk(): lax.ppermute(theirs.astype(jnp.bfloat16), 'zh', SWAP).astype(jnp.float32)]
    all_to_all x1 -> x0, starting transfers between devices: 4.34 us -> none  [body(): lax.all_to_all(attn_feats, ('y', 'x', 'zh'), split_axis=1, concat_axis=0,...]
    all_to_all x1 -> x0, waiting for transfers between devices: 3.59 us -> none  [body(): lax.all_to_all(attn_feats, ('y', 'x', 'zh'), split_axis=1, concat_axis=0,...]
  transfers between devices with their start and end apart: 6 -> 5, of which waited for: 6 -> 5; matrix products, arithmetic and copies ran while one was open for 8% -> 5% of each run, Pallas kernels for 0% -> 0%
where the time goes in v12:
time: 273 us; the launch traced here: 272 us
  blocking collectives  156 us (57%)
  waiting for transfers between devices  32.7 us (12%)
  matrix products  26.2 us (10%)
  starting transfers between devices  19.4 us (7%)
  other arithmetic  18.8 us (7%)
  local copies, waits for them, and re-layouts  17.9 us (7%)
    all_to_all x1, blocking collectives, gather_plane(): lax.all_to_all(jnp.broadcast_to(pair[None], (plane,) + pair.shape), PLANE...  46.4 us
    all_to_all x1, blocking collectives, reduce_blk(): got = lax.all_to_all(pieces, PLANE, 0, 0, tiled=True)  41.4 us
    all_to_all x1, blocking collectives, body(): lax.all_to_all(jnp.broadcast_to(kv_rows[None], (ys * xs,) + kv_rows.shape...  40.3 us
    all_to_all x1, blocking collectives, body(): lax.all_to_all(attn_feats, ('y', 'x', 'zh'), split_axis=1, concat_axis=0,...  16.6 us
    all_to_all x1, blocking collectives, body(): lax.all_to_all(attended, group, split_axis=0, concat_axis=1, tiled=True)  11.4 us
    all_to_all x1, waiting for transfers between devices, body(): lax.all_to_all(qkv_cols, ('y', 'x', 'zh'), split_axis=0, concat_axis=1, t...  10.9 us
    dot_general x1, matrix products, body(): mlp_out = jnp.dot(mlp_act, w_mlp_out, preferred_element_type=jnp.float32)  9.59 us
    all_to_all x1, waiting for transfers between devices, body(): lax.all_to_all(by_token, group, split_axis=1, concat_axis=0, tiled=True)  8.12 us
  transfers between devices with their start and end apart: 5, of which 5 were waited for; matrix products, arithmetic and copies ran while one was open for 5% of the time, Pallas kernels for 0%

profile of v12, /device:TPU:32, one launch (start us, length us, event | category | flops | bytes accessed | tf_op | source)
XLA Modules:
  0.0 271.5 jit_solution(2793816699019898759)
XLA Ops:
  0.0 6.3 %collective-permute-start = (f32[16,3072]{1,0:T(8,128)}, f32[16,3072]{1,0:T(8,128)S(1)}, u32[]{:S(2)}, u32[]{:S(2)}) collective-permute-start(f32[16,3072]{1,0:T(8,128)} %param.12), channel_id=1, source_target_pairs={{0,4},{4,0},{1,5},{5,1},{2,6},{6,2},{3,7},{7,3},{8,12},{12,8},{9,1... | collective-permute-start | bytes 589832 | tf_op jit(solution)/shard_map/ppermute | solution.py:118
  6.3 0.8 reduce-window.8
  7.1 0.7 fusion.55
  7.8 1.1 reduce_sum.139
  8.9 1.1 multiply_reduce_fusion.3
  10.1 2.9 %fusion = f32[4,1,9216]{2,1,0:T(1,128)S(1)} fusion(bf16[4,28,9216]{2,0,1:T(4,128)(2,1)} %bitcast.117, pred[4,28,1]{1,0,2:T(4,128)(4,1)S(1)} %fusion.55), kind=kOutput, calls=%fused_computation.8 | convolution fusion | flops 2064384 | bytes 2211952 | tf_op jit(solution)/shard_map/rs,rsk->rk/dot_general | solution.py:122
  13.0 0.4 fusion.43
  13.5 1.3 fusion.41
  14.7 0.9 collective-permute-done
  15.8 0.2 multiply_reduce_fusion.2
  16.0 1.2 select_bitcast_fusion.3
  17.3 0.4 broadcast_in_dim.53
  17.7 46.4 %all_to_all.82 = bf16[16,2,16,3072]{3,2,1,0:T(8,128)(2,1)S(1)} all-to-all(bf16[16,2,16,3072]{3,2,1,0:T(8,128)(2,1)S(1)} %broadcast_in_dim.53), channel_id=1, replica_groups=mesh['zl'=4,'core'=2,'y'=4,'zh'=2,'x'=4] {'y','x'}, dimensions={0} | all-to-all | bytes 6291456 | tf_op jit(solution)/shard_map/all_to_all | solution.py:77
  64.1 1.7 copy-done.1
  65.8 1.1 convolution_convert_fusion
  66.9 0.9 copy.85
  67.8 6.9 %all-to-all-start.1 = ((bf16[32,16,288]{2,1,0:T(8,128)(2,1)}), bf16[32,16,288]{2,1,0:T(8,128)(2,1)S(1)}, u32[]{:S(2)}, u32[]{:S(2)}) async-start(bf16[32,16,288]{2,1,0:T(8,128)(2,1)} %bitcast.119), calls=%async_computation.1 | async-start | bytes 786432 | tf_op jit(solution)/shard_map/all_to_all | solution.py:156
  74.8 0.7 mul.239
  75.5 0.7 mul.250
  76.3 1.9 reshape.484
  78.2 0.9 convert_reduce_fusion.2
  79.2 10.9 %all-to-all-done.1 = bf16[32,16,288]{2,1,0:T(8,128)(2,1)S(1)} async-done(((bf16[32,16,288]{2,1,0:T(8,128)(2,1)}), bf16[32,16,288]{2,1,0:T(8,128)(2,1)S(1)}, u32[]{:S(2)}, u32[]{:S(2)}) %all-to-all-start.1) | async-done | bytes 294944 | tf_op jit(solution)/shard_map/all_to_all | solution.py:156
  90.1 0.9 copy.132
  91.0 1.3 all_to_all.63
  92.4 0.7 copy.87
  93.1 5.4 %all-to-all-start.2 = ((bf16[16,8,1152]{2,0,1:T(8,128)(2,1)}), bf16[16,8,1152]{2,0,1:T(8,128)(2,1)S(1)}, u32[]{:S(2)}, u32[]{:S(2)}) async-start(bf16[16,8,1152]{2,0,1:T(8,128)(2,1)} %copy.87), calls=%async_computation.2 | async-start | bytes 589824 | tf_op jit(solution)/shard_map/all_to_all | solution.py:159
  98.6 0.8 fusion.73
  99.4 8.1 %all-to-all-done.2 = bf16[16,8,1152]{2,0,1:T(8,128)(2,1)S(1)} async-done(((bf16[16,8,1152]{2,0,1:T(8,128)(2,1)}), bf16[16,8,1152]{2,0,1:T(8,128)(2,1)S(1)}, u32[]{:S(2)}, u32[]{:S(2)}) %all-to-all-start.2) | async-done | bytes 294944 | tf_op jit(solution)/shard_map/all_to_all | solution.py:159
  107.5 0.7 copy-done.3
  108.2 1.0 reshape.486
  109.2 1.1 fusion.72
  110.5 0.1 multiply_reduce_fusion
  110.7 1.7 copy.108
  112.4 0.8 copy.89
  113.3 1.1 multiply_multiply_fusion.2
  114.4 0.9 multiply_multiply_fusion.1
  115.3 1.9 subtract_convert_fusion.1
  117.2 0.2 pad_maximum_fusion.4
  117.5 0.9 pad_maximum_fusion.2
  118.4 0.1 copy.99
  118.5 0.4 broadcast_in_dim.54
  118.9 40.3 %all_to_all.83 = bf16[16,128,3,256]{3,1,2,0:T(8,128)(2,1)} all-to-all(bf16[16,128,3,256]{3,1,2,0:T(8,128)(2,1)S(1)} %broadcast_in_dim.54), channel_id=1, replica_groups=mesh['zl'=4,'core'=2,'y'=4,'zh'=2,'x'=4] {'y','x'}, dimensions={0} | all-to-all | bytes 6291456 | tf_op jit(solution)/shard_map/all_to_all | solution.py:192
  159.7 0.2 reshape.495
  160.1 0.2 pad_maximum_fusion.3
  160.3 4.9 %collective-permute-done.1 = bf16[16,128,3,256]{3,1,2,0:T(8,128)(2,1)} collective-permute-done((bf16[16,128,3,256]{3,1,2,0:T(8,128)(2,1)}, bf16[16,128,3,256]{3,1,2,0:T(8,128)(2,1)}, u32[]{:S(2)}, u32[]{:S(2)}) %collective-permute-start.1) | collective-permute-done | bytes 3145760 | tf_op jit(solution)/shard_map/ppermute | solution.py:195
  165.2 3.3 %select_bitcast_fusion.1 = (bf16[1,16,128,3,256]{4,2,3,1,0:T(8,128)(2,1)S(1)}, bf16[1,16,128,3,256]{4,2,3,1,0:T(8,128)(2,1)S(1)}) fusion(bf16[16,128,3,256]{3,1,2,0:T(8,128)(2,1)} %all_to_all.83, bf16[16,128,3,256]{3,1,2,0:T(8,128)(2,1)} %collective-permute-done.1, pred[]{:T(512)S(6)} %eq.141), kind=kLoop, calls=%fused_computation.7 | loop fusion | flops 3145728 | bytes 12582913 | tf_op jit(solution)/shard_map/stack | solution.py:196
  168.5 0.6 pad_maximum_fusion
  169.0 0.8 copy.100
  169.8 0.5 convolution_multiply_fusion
  170.3 1.0 select_reduce_fusion.2
  171.4 1.7 fusion.2
  173.1 1.0 fusion.13
  174.1 1.4 fusion.4
  175.5 1.0 fusion.11
  176.5 1.0 fusion.12
  177.7 11.4 %all_to_all.84 = bf16[8,16,384]{2,1,0:T(8,128)(2,1)S(1)} all-to-all(bf16[8,16,384]{2,1,0:T(8,128)(2,1)S(1)} %all_to_all.67), channel_id=1, replica_groups=mesh['zl'=4,'core'=2,'y'=4,'zh'=2,'x'=4] {'zl','zh'}, dimensions={0} | all-to-all | bytes 196608 | tf_op jit(solution)/shard_map/all_to_all | solution.py:212
  189.3 16.6 %all_to_all.85 = bf16[16,32,96]{2,0,1:T(8,128)(2,1)S(1)} all-to-all(bf16[16,32,96]{2,0,1:T(8,128)(2,1)S(1)} %bitcast.125), channel_id=1, replica_groups=mesh['zl'=4,'core'=2,'y'=4,'zh'=2,'x'=4] {'y','x','zh'}, dimensions={1} | all-to-all | bytes 196608 | tf_op jit(solution)/shard_map/all_to_all | solution.py:214
  205.9 4.7 %fusion.76 = f32[512,3072]{1,0:T(8,128)} fusion(bf16[512,96]{1,0:T(8,128)(2,1)S(1)} %bitcast.122, bf16[96,3072]{1,0:T(8,128)(2,1)} %param.22), kind=kOutput, calls=%fused_computation.158 | convolution fusion | flops 301989888 | bytes 6979584 | tf_op jit(solution)/shard_map/dot_general | solution.py:216
  210.6 9.6 %add_convert_fusion = bf16[512,3072]{1,0:T(8,128)(2,1)} fusion(f32[512,3072]{1,0:T(8,128)} %fusion.76, bf16[384,3072]{1,0:T(8,128)(2,1)S(1)} %copy-done, bf16[512,3072]{1,0:T(8,128)(2,1)} %bitcast.115, bf16[3072,384]{1,0:T(8,128)(2,1)} %param.19), kind=kOutput, calls=%fused_computation.2 | convolution fusion | flops 2420834304 | bytes 17301504 | tf_op jit(solution)/shard_map/dot_general | solution.py:215
  220.2 41.4 %all_to_all.86 = bf16[16,2,16,3072]{3,2,1,0:T(8,128)(2,1)S(1)} all-to-all(bf16[16,2,16,3072]{3,2,1,0:T(8,128)(2,1)} %bitcast.116), channel_id=1, replica_groups=mesh['zl'=4,'core'=2,'y'=4,'zh'=2,'x'=4] {'y','x'}, dimensions={0} | all-to-all | bytes 6291456 | tf_op jit(solution)/shard_map/all_to_all | solution.py:84
  261.6 0.6 convert_reduce_fusion
  262.2 0.8 collective-permute-start.2
  263.0 7.9 %collective-permute-done.2 = bf16[16,3072]{1,0:T(8,128)(2,1)S(1)} collective-permute-done((bf16[16,3072]{1,0:T(8,128)(2,1)S(1)}, bf16[16,3072]{1,0:T(8,128)(2,1)S(1)}, u32[]{:S(2)}, u32[]{:S(2)}) %collective-permute-start.2) | collective-permute-done | bytes 98336 | tf_op jit(solution)/shard_map/ppermute | solution.py:87
  270.8 0.7 fusion.40
  (58 shorter events, 1.9 us)
Async XLA Ops:
  0.0 210.6 %copy-start = (bf16[384,3072]{1,0:T(8,128)(2,1)S(1)}, bf16[384,3072]{1,0:T(8,128)(2,1)}, u32[]{:S(2)}) copy-start(bf16[384,3072]{1,0:T(8,128)(2,1)} %param.23) | copy-start | bytes 7077892
  0.0 15.7 %collective-permute-start = (f32[16,3072]{1,0:T(8,128)}, f32[16,3072]{1,0:T(8,128)S(1)}, u32[]{:S(2)}, u32[]{:S(2)}) collective-permute-start(f32[16,3072]{1,0:T(8,128)} %param.12), channel_id=1, source_target_pairs={{0,4},{4,0},{1,5},{5,1},{2,6},{6,2},{3,7},{7,3},{8,12},{12,8},{9,1... | collective-permute-start | bytes 589832 | tf_op jit(solution)/shard_map/ppermute | solution.py:118
  7.1 7.6 %copy-start.7 = (s32[4,1]{0,1:T(1,128)}, s32[4,1]{0,1:T(1,128)S(1)}, u32[]{:S(2)}) copy-start(s32[4,1]{0,1:T(1,128)S(1)} %reduce-window.8) | copy-start | bytes 52
  10.1 6.0 %copy-start.2 = (f32[16,3072]{1,0:T(8,128)S(1)}, f32[16,3072]{1,0:T(8,128)}, u32[]{:S(2)}) copy-start(f32[16,3072]{1,0:T(8,128)} %param.12) | copy-start | bytes 589828
  17.6 48.1 %copy-start.11 = (bf16[3072,288]{0,1:T(8,128)(2,1)S(1)}, bf16[3072,288]{0,1:T(8,128)(2,1)}, u32[]{:S(2)}) copy-start(bf16[3072,288]{0,1:T(8,128)(2,1)} %param.18) | copy-start | bytes 5308420
  64.1 1.7 copy-start.1
  65.8 9.0 %copy-start.9 = (f32[128]{0:T(128)S(1)}, f32[128]{0:T(128)}, u32[]{:S(2)}) copy-start(f32[128]{0:T(128)} %param.20) | copy-start | bytes 1540
  65.8 9.8 %copy-start.10 = (f32[128]{0:T(128)S(1)}, f32[128]{0:T(128)}, u32[]{:S(2)}) copy-start(f32[128]{0:T(128)} %param.21) | copy-start | bytes 1540
  67.8 22.3 %all-to-all-start.1 = ((bf16[32,16,288]{2,1,0:T(8,128)(2,1)}), bf16[32,16,288]{2,1,0:T(8,128)(2,1)S(1)}, u32[]{:S(2)}, u32[]{:S(2)}) async-start(bf16[32,16,288]{2,1,0:T(8,128)(2,1)} %bitcast.119), calls=%async_computation.1 | async-start | bytes 786432 | tf_op jit(solution)/shard_map/all_to_all | solution.py:156
  93.1 14.4 %all-to-all-start.2 = ((bf16[16,8,1152]{2,0,1:T(8,128)(2,1)}), bf16[16,8,1152]{2,0,1:T(8,128)(2,1)S(1)}, u32[]{:S(2)}, u32[]{:S(2)}) async-start(bf16[16,8,1152]{2,0,1:T(8,128)(2,1)} %copy.87), calls=%async_computation.2 | async-start | bytes 589824 | tf_op jit(solution)/shard_map/all_to_all | solution.py:159
  107.5 0.7 copy-start.3
  118.9 40.4 %copy-start.6 = (s32[4096]{0:T(1024)S(1)}, s32[4096]{0:T(1024)}, u32[]{:S(2)}) copy-start(s32[4096]{0:T(1024)} %param.13) | copy-start | bytes 49156
  118.9 41.0 %copy-start.8 = (s32[4,1]{0,1:T(1,128)S(1)}, s32[4,1]{0,1:T(1,128)}, u32[]{:S(2)}) copy-start(s32[4,1]{0,1:T(1,128)} %copy-done.7) | copy-start | bytes 52
  118.9 41.2 %copy-start.4 = (bf16[128,3,64,1]{0,3,2,1:T(2,128)(2,1)S(1)}, bf16[128,3,64,1]{0,3,2,1:T(2,128)(2,1)}, u32[]{:S(2)}) copy-start(bf16[128,3,64,1]{0,3,2,1:T(2,128)(2,1)} %get-tuple-element.20) | copy-start | bytes 147460
  118.9 41.2 %copy-start.5 = (bf16[128,3,64,1]{0,3,2,1:T(2,128)(2,1)S(1)}, bf16[128,3,64,1]{0,3,2,1:T(2,128)(2,1)}, u32[]{:S(2)}) copy-start(bf16[128,3,64,1]{0,3,2,1:T(2,128)(2,1)} %get-tuple-element.21) | copy-start | bytes 147460
  159.2 6.0 %collective-permute-start.1 = (bf16[16,128,3,256]{3,1,2,0:T(8,128)(2,1)}, bf16[16,128,3,256]{3,1,2,0:T(8,128)(2,1)}, u32[]{:S(2)}, u32[]{:S(2)}) collective-permute-start(bf16[16,128,3,256]{3,1,2,0:T(8,128)(2,1)} %all_to_all.83), channel_id=1, source_target_pairs={{0,32},{32,0},{1,33},{33,1},{2,34},{34,2},{3,35},{35,3},{4,36},{36... | collective-permute-start | bytes 9437192 | tf_op jit(solution)/shard_map/ppermute | solution.py:195
  262.2 8.6 %collective-permute-start.2 = (bf16[16,3072]{1,0:T(8,128)(2,1)S(1)}, bf16[16,3072]{1,0:T(8,128)(2,1)S(1)}, u32[]{:S(2)}, u32[]{:S(2)}) collective-permute-start(bf16[16,3072]{1,0:T(8,128)(2,1)S(1)} %fusion.47), channel_id=1, source_target_pairs={{0,4},{4,0},{1,5},{5,1},{2,6},{6,2},{3,7},{7,3},{8,12},{12,8},{9,1... | collective-permute-start | bytes 294920 | tf_op jit(solution)/shard_map/ppermute | solution.py:87
